TPU v7x, 512 devices: a whole 4x8x8 slice. The times are simulated.
512 devices in a mesh: gx: 128 (over z_lo, x, y), gy: 2 (over core), gz: 2 (over z_hi).
Axes of the slice: x: 4, y: 8, z: 8 (z_hi: 2, z_lo: 4; z = z_hi * 4 + z_lo), core: 2. Of those that a mesh axis runs over, the one named last changes fastest.
Arguments:
- velocity: bfloat16 [3, 256, 16, 256], P(None, 'gx', 'gy', 'gz'), may hold values from -6 to 6
- eddy_viscosity: float32 [256, 16, 256], P('gx', 'gy', 'gz'), may hold values from 0.02 to 0.3
- cell_owner: int32 [2, 2, 262144, 1], P('gy', 'gz', 'gx'), may hold values from 0 to 127; in each aligned block of 2048 rows (0 to 2047, 2048 to 4095, ..., all dimensions but the last counted through in order) at most 24 rows name the same one
- cell_element: int32 [2, 2, 262144], P('gy', 'gz', 'gx'), may hold values from 0 to 3
- cell_position: int32 [2, 2, 262144], P('gy', 'gz', 'gx'), may hold values from 0 to 4095
- acoustic_state: float32 [4, 128, 2, 8, 512], P(None, 'gx', 'gy', 'gz'), may hold values from -6 to 6
Outputs:
- source_moments: float32 [128, 2, 8, 3, 512], P('gx', 'gy', 'gz')
- next_state: float32 [4, 128, 2, 8, 512], P(None, 'gx', 'gy', 'gz')
Inputs may be any that keep to these rules, and one draw needn't show every extreme that they name: `cell_owner`: in the rows of one device (aligned blocks of 2048 rows along the last two dimensions), no owner is named more than 24 times, a bound that some block reaches.
All inputs are finite; a program needn't handle non-finite values.
Results may differ from a plain program's by a relative error of at most 0.0039.
Values may be sent and summed in bfloat16 or wider, within the bound.
No kernel may reach another device: no remote copies, remote signals or barrier semaphores. Data moves between devices by JAX's collectives and lax.ppermute only.
A program may use at most 64 MiB of HBM per device.

v0:
```python
import jax
import jax.numpy as jnp
import numpy as np
from jax import lax
from jax.sharding import PartitionSpec as P

SUB = 16
NODES = 512


GLL_POINTS = np.array(
    [
        -1.0,
        -0.8717401485096066,
        -0.5917001814331423,
        -0.2092992179024789,
        0.2092992179024789,
        0.5917001814331423,
        0.8717401485096066,
        1.0,
    ]
)
LIFT_FACTOR = 28.0
TIME_STEP = 0.01
COUPLING = 4.0
MOMENT_WEIGHT = 0.0625


def derivative_matrix():
    points = GLL_POINTS
    barycentric = np.ones(8)
    for j in range(8):
        for m in range(8):
            if m != j:
                barycentric[j] = barycentric[j] / (points[j] - points[m])
    matrix = np.zeros((8, 8))
    for i in range(8):
        for j in range(8):
            if i != j:
                matrix[i, j] = barycentric[j] / barycentric[i] / (points[i] - points[j])
        matrix[i, i] = -np.sum(matrix[i])
    return matrix


def kron_tables():
    matrix = derivative_matrix().T
    node = np.arange(NODES)
    spreads = [matrix[:, node // 64], matrix[:, node // 8 % 8], matrix[:, node % 8]]
    spreads = lax.optimization_barrier([jnp.asarray(t, jnp.float32) for t in spreads])
    row = lax.broadcasted_iota(jnp.int32, (NODES, NODES), 0)
    col = lax.broadcasted_iota(jnp.int32, (NODES, NODES), 1)
    same_a = row // 64 == col // 64
    same_b = row // 8 % 8 == col // 8 % 8
    same_c = row % 8 == col % 8
    shape = (8, 8, 8, NODES)
    along_x = jnp.broadcast_to(spreads[0][:, None, None, :], shape).reshape(NODES, NODES)
    along_y = jnp.broadcast_to(spreads[1][None, :, None, :], shape).reshape(NODES, NODES)
    along_z = jnp.broadcast_to(spreads[2][None, None, :, :], shape).reshape(NODES, NODES)
    zero = jnp.zeros((), jnp.float32)
    return [
        jnp.where(same_b & same_c, along_x, zero),
        jnp.where(same_a & same_c, along_y, zero),
        jnp.where(same_a & same_b, along_z, zero),
    ]


def basis_table():
    points = GLL_POINTS
    centres = -1.0 + (2.0 * np.arange(SUB) + 1.0) / SUB
    values = np.ones((SUB, 8))
    for j in range(8):
        for m in range(8):
            if m != j:
                values[:, j] = values[:, j] * (centres - points[m]) / (points[j] - points[m])
    return np.asarray(values, dtype=np.float32)


def neighbours(lower, upper, axis):
    count = lax.axis_size(axis)
    if count == 1:
        return jnp.zeros_like(upper), jnp.zeros_like(lower)
    if count == 2:
        index = lax.axis_index(axis)
        sent = jnp.where(index == 0, upper, lower)
        got = lax.ppermute(sent, axis, [(0, 1), (1, 0)])
        zero = jnp.zeros_like(got)
        return jnp.where(index == 1, got, zero), jnp.where(index == 0, got, zero)
    from_below = lax.ppermute(upper, axis, [(i, i + 1) for i in range(count - 1)])
    from_above = lax.ppermute(lower, axis, [(i + 1, i) for i in range(count - 1)])
    return from_below, from_above


def source_cells(velocity, viscosity):
    below_x, above_x = neighbours(velocity[:, :1], velocity[:, -1:], "gx")
    below_y, above_y = neighbours(velocity[:, :, :1], velocity[:, :, -1:], "gy")
    below_z, above_z = neighbours(velocity[..., :1], velocity[..., -1:], "gz")
    centre = velocity.astype(jnp.float32)
    f32 = lambda t: t.astype(jnp.float32)
    plus_x = jnp.concatenate([centre[:, 1:], f32(above_x)], axis=1)
    minus_x = jnp.concatenate([f32(below_x), centre[:, :-1]], axis=1)
    plus_y = jnp.concatenate([centre[:, :, 1:], f32(above_y)], axis=2)
    minus_y = jnp.concatenate([f32(below_y), centre[:, :, :-1]], axis=2)
    plus_z = jnp.concatenate([centre[..., 1:], f32(above_z)], axis=3)
    minus_z = jnp.concatenate([f32(below_z), centre[..., :-1]], axis=3)
    grad_x = 0.5 * (plus_x - minus_x)
    grad_y = 0.5 * (plus_y - minus_y)
    grad_z = 0.5 * (plus_z - minus_z)
    laplace = plus_x + minus_x + plus_y + minus_y + plus_z + minus_z - 6.0 * centre
    curl_x = grad_y[2] - grad_z[1]
    curl_y = grad_z[0] - grad_x[2]
    curl_z = grad_x[1] - grad_y[0]
    lamb_x = curl_y * centre[2] - curl_z * centre[1]
    lamb_y = curl_z * centre[0] - curl_x * centre[2]
    lamb_z = curl_x * centre[1] - curl_y * centre[0]
    lamb = jnp.stack([lamb_x, lamb_y, lamb_z])
    return (viscosity[None] * laplace - lamb).astype(jnp.bfloat16)


def face_correction(inside, outside, normal, component):
    difference = inside - outside
    result = -0.5 * difference
    first = result[0] + 0.5 * normal * difference[component]
    chosen = result[component] + 0.5 * normal * difference[0]
    parts = [result[i] for i in range(4)]
    parts[0] = first
    parts[component] = chosen
    return LIFT_FACTOR * jnp.stack(parts)


def tendency(fields, forcing, tables):
    highest = lax.Precision.HIGHEST
    count = fields.shape[1]
    grads = [jnp.dot(fields[0], table, precision=highest) for table in tables]
    divergence = (
        jnp.dot(fields[1], tables[0], precision=highest)
        + jnp.dot(fields[2], tables[1], precision=highest)
        + jnp.dot(fields[3], tables[2], precision=highest)
    )
    result = jnp.stack(
        [
            -divergence,
            COUPLING * forcing[0] - grads[0],
            COUPLING * forcing[1] - grads[1],
            COUPLING * forcing[2] - grads[2],
        ]
    )

    face = 64
    below_x, above_x = neighbours(fields[..., :face], fields[..., NODES - face :], "gx")
    outer_lower_x = jnp.pad(below_x, ((0, 0), (0, 0), (0, NODES - face)))
    outer_upper_x = jnp.pad(above_x, ((0, 0), (0, 0), (NODES - face, 0)))
    below_y, above_y = neighbours(fields, fields, "gy")
    outer_lower_y = jnp.roll(below_y, -56, axis=2)
    outer_upper_y = jnp.roll(above_y, 56, axis=2)
    below_z, above_z = neighbours(fields[:, :1], fields[:, count - 1 :], "gz")
    outer_lower_z = jnp.roll(jnp.concatenate([below_z, fields[:, :-1]], axis=1), -7, axis=2)
    outer_upper_z = jnp.roll(jnp.concatenate([fields[:, 1:], above_z], axis=1), 7, axis=2)

    node = jnp.arange(NODES, dtype=jnp.int32)
    places = (node // 64, node // 8 % 8, node % 8)
    faces = (
        (outer_lower_x, outer_upper_x),
        (outer_lower_y, outer_upper_y),
        (outer_lower_z, outer_upper_z),
    )
    for direction, (low_out, high_out) in enumerate(faces):
        place = places[direction]
        low_corr = face_correction(fields, low_out, -1.0, direction + 1)
        high_corr = face_correction(fields, high_out, 1.0, direction + 1)
        added = jnp.where(place == 0, low_corr, jnp.where(place == 7, high_corr, 0.0))
        result = result + added
    return result


def runge_kutta(fields, forcing):
    tables = kron_tables()
    step = lambda f: tendency(f, forcing, tables)
    section_one = fields + TIME_STEP * step(fields)
    section_two = 0.75 * fields + 0.25 * (section_one + TIME_STEP * step(section_one))
    return 1.0 / 3.0 * fields + 2.0 / 3.0 * (section_two + TIME_STEP * step(section_two))


def pick_columns(index, table):
    levels = jnp.arange(table.shape[1], dtype=jnp.int32)
    chosen = jnp.where(index[None, None, :] == levels[None, :, None], table[:, :, None], 0.0)
    return jnp.sum(chosen, axis=1)


def on_device(velocity, eddy_viscosity, cell_owner, cell_element, cell_position, acoustic_state):
    sources = source_cells(velocity, eddy_viscosity)
    cell_count = sources.shape[1] * sources.shape[2] * sources.shape[3]
    flat_source = sources.reshape(3, cell_count).astype(jnp.float32)
    owners = cell_owner.reshape(cell_count)
    elements = cell_element.reshape(cell_count)
    positions = cell_position.reshape(cell_count)
    owner_count = lax.axis_size("gx")
    capacity = 3 * cell_count // (2 * owner_count)
    owner_hot = (owners[:, None] == jnp.arange(owner_count, dtype=jnp.int32)[None, :]).astype(
        jnp.int32
    )
    earlier = jnp.cumsum(owner_hot, axis=0) - owner_hot
    order_within = jnp.sum(earlier * owner_hot, axis=1)
    slot_index = owners * capacity + order_within
    subcells = SUB * SUB * SUB
    ident = (elements * subcells + positions).astype(jnp.float32)
    payload = jnp.concatenate([flat_source, ident[None]], axis=0)
    send = (
        jnp.zeros((4, owner_count * capacity), jnp.float32)
        .at[:, slot_index]
        .set(payload)
        .reshape(4, owner_count, capacity)
    )
    send = jnp.transpose(send, (1, 0, 2)).reshape(owner_count, 4 * capacity)
    got = lax.all_to_all(send, "gx", split_axis=0, concat_axis=0, tiled=True)
    got = jnp.transpose(got.reshape(owner_count, 4, capacity), (1, 0, 2)).reshape(
        4, owner_count * capacity
    )
    got_source = got[:3].astype(jnp.bfloat16)
    got_ident = got[3].astype(jnp.int32)
    got_element = got_ident // subcells
    got_position = got_ident % subcells

    values = jnp.asarray(basis_table().T)
    along_a = pick_columns(got_position // (SUB * SUB), values)
    along_b = pick_columns(got_position // SUB % SUB, values)
    along_c = pick_columns(got_position % SUB, values)
    rows = got_position.shape[0]
    node_columns = (
        along_a[:, None, None, :] * along_b[None, :, None, :] * along_c[None, None, :, :]
    ).reshape(NODES, rows).astype(jnp.bfloat16)

    local_elems = acoustic_state.shape[1] * acoustic_state.shape[2] * acoustic_state.shape[3]
    element_hot = got_element[None, :] == jnp.arange(local_elems, dtype=jnp.int32)[:, None]
    weighted = jnp.where(element_hot[None], got_source[:, None, :], jnp.zeros((), jnp.bfloat16))
    weighted = weighted.reshape(3 * local_elems, rows)
    totals = lax.dot_general(
        weighted, node_columns, (((1,), (1,)), ((), ())), preferred_element_type=jnp.float32
    )
    forcing = (totals * MOMENT_WEIGHT).reshape(3, local_elems, NODES)
    moments = jnp.moveaxis(forcing, 0, 1).reshape(
        acoustic_state.shape[1:4] + (3, NODES)
    )

    fields = acoustic_state.reshape(4, local_elems, NODES)
    next_state = runge_kutta(fields, forcing).reshape(acoustic_state.shape)
    return (moments, next_state)


def solution(mesh):
    in_specs = (
        P(None, "gx", "gy", "gz"),
        P("gx", "gy", "gz"),
        P("gy", "gz", "gx", None),
        P("gy", "gz", "gx"),
        P("gy", "gz", "gx"),
        P(None, "gx", "gy", "gz", None),
    )
    out_specs = (P("gx", "gy", "gz", None, None), P(None, "gx", "gy", "gz", None))
    return jax.shard_map(
        on_device, mesh=mesh, in_specs=in_specs, out_specs=out_specs, check_vma=False
    )
```

profile of v0, /device:TPU:64, one launch (start us, length us, event | category | flops | bytes accessed | tf_op | source)
XLA Modules:
  0.0 146.3 jit_solution(7517484868772382151)
XLA Ops:
  0.6 1.3 fusion.211
  1.9 3.5 %collective-permute-start.1 = (bf16[3,1,8,128]{3,2,1,0:T(8,128)(2,1)}, bf16[3,1,8,128]{3,2,1,0:T(8,128)(2,1)}, u32[]{:S(2)}, u32[]{:S(2)}) collective-permute-start(bf16[3,1,8,128]{3,2,1,0:T(8,128)(2,1)} %get-tuple-element.191), channel_id=1, source_target_pairs={{0,4},{4,8},{8,12},{12,16},{16,20},{20,24},{24,28},{28,32},{32,36}... | collective-permute-start | bytes 18440 | tf_op jit(solution)/shard_map/ppermute | solution.py:88
  5.4 6.6 %collective-permute-start = (bf16[3,1,8,128]{3,2,1,0:T(8,128)(2,1)}, bf16[3,1,8,128]{3,2,1,0:T(8,128)(2,1)}, u32[]{:S(2)}, u32[]{:S(2)}) collective-permute-start(bf16[3,1,8,128]{3,2,1,0:T(8,128)(2,1)} %get-tuple-element.190), channel_id=1, source_target_pairs={{4,0},{8,4},{12,8},{16,12},{20,16},{24,20},{28,24},{32,28},{36,32}... | collective-permute-start | bytes 18440 | tf_op jit(solution)/shard_map/ppermute | solution.py:89
  12.0 1.4 broadcast_select_fusion.18
  13.4 1.9 %collective-permute-start.2 = (bf16[3,2,1,128]{3,2,1,0:T(2,128)(2,1)}, bf16[3,2,1,128]{3,2,1,0:T(2,128)(2,1)}, u32[]{:S(2)}, u32[]{:S(2)}) collective-permute-start(bf16[3,2,1,128]{3,2,1,0:T(2,128)(2,1)} %broadcast_select_fusion.18), channel_id=1, source_target_pairs={{0,2},{2,0},{1,3},{3,1},{4,6},{6,4},{5,7},{7,5},{8,10},{10,8},{9,1... | collective-permute-start | bytes 4616 | tf_op jit(solution)/shard_map/ppermute | solution.py:85
  15.3 1.5 slice_select_fusion
  16.8 10.0 %collective-permute-start.3 = (bf16[3,2,8,1]{3,2,1,0:T(8,128)(2,1)}, bf16[3,2,8,1]{3,2,1,0:T(8,128)(2,1)}, u32[]{:S(2)}, u32[]{:S(2)}) collective-permute-start(bf16[3,2,8,1]{3,2,1,0:T(8,128)(2,1)} %slice_select_fusion), channel_id=1, source_target_pairs={{0,1},{1,0},{2,3},{3,2},{4,5},{5,4},{6,7},{7,6},{8,9},{9,8},{10,11... | collective-permute-start | bytes 296 | tf_op jit(solution)/shard_map/ppermute | solution.py:85
  26.8 2.1 %collective-permute-start.6 = (f32[4,4,512]{2,1,0:T(4,128)}, f32[4,4,512]{2,1,0:T(4,128)}, u32[]{:S(2)}, u32[]{:S(2)}) collective-permute-start(f32[4,4,512]{2,1,0:T(4,128)} %bitcast.531), channel_id=1, source_target_pairs={{0,2},{2,0},{1,3},{3,1},{4,6},{6,4},{5,7},{7,5},{8,10},{10,8},{9,1... | collective-permute-start | bytes 98312 | tf_op jit(solution)/shard_map/ppermute | solution.py:85
  28.9 0.7 convert_element_type.100
  29.6 0.7 fusion.210
  30.4 0.8 fusion.208
  31.1 0.9 fusion.209
  32.2 1.4 broadcast_select_fusion.12
  33.6 0.8 fusion.206
  34.5 1.4 fusion.207
  37.5 0.8 copy.218
  39.5 0.6 fusion.14
  40.2 0.6 compare_select_fusion
  41.8 1.2 and_select_fusion.2
  43.0 0.6 fusion.155
  43.7 0.6 convolution_add_fusion.5
  44.4 0.7 fusion.9
  45.1 2.2 %collective-permute-start.7 = (f32[4,1,512]{2,1,0:T(1,128)S(1)}, f32[4,1,512]{2,1,0:T(1,128)S(1)}, u32[]{:S(2)}, u32[]{:S(2)}) collective-permute-start(f32[4,1,512]{2,1,0:T(1,128)S(1)} %copy-done.22), channel_id=1, source_target_pairs={{0,1},{1,0},{2,3},{3,2},{4,5},{5,4},{6,7},{7,6},{8,9},{9,8},{10,11... | collective-permute-start | bytes 24584 | tf_op jit(solution)/shard_map/ppermute | solution.py:85
  47.3 0.7 select_convert_fusion.1
  48.0 1.9 %collective-permute-start.4 = (f32[4,4,64]{2,1,0:T(4,128)S(1)}, f32[4,4,64]{2,1,0:T(4,128)S(1)}, u32[]{:S(2)}, u32[]{:S(2)}) collective-permute-start(f32[4,4,64]{2,1,0:T(4,128)S(1)} %copy-done.24), channel_id=1, source_target_pairs={{0,4},{4,8},{8,12},{12,16},{16,20},{20,24},{24,28},{28,32},{32,36}... | collective-permute-start | bytes 12296 | tf_op jit(solution)/shard_map/ppermute | solution.py:88
  49.9 0.7 fusion.169
  50.7 8.1 %collective-permute-start.5 = (f32[4,4,64]{2,1,0:T(4,128)S(1)}, f32[4,4,64]{2,1,0:T(4,128)S(1)}, u32[]{:S(2)}, u32[]{:S(2)}) collective-permute-start(f32[4,4,64]{2,1,0:T(4,128)S(1)} %copy-done.23), channel_id=1, source_target_pairs={{4,0},{8,4},{12,8},{16,12},{20,16},{24,20},{28,24},{32,28},{36,32}... | collective-permute-start | bytes 12296 | tf_op jit(solution)/shard_map/ppermute | solution.py:89
  58.9 0.7 convert_element_type.102
  59.6 0.7 convert_element_type.101
  60.5 1.4 copy.220
  61.8 7.1 %scatter_custom_fusion = f32[4,3072]{0,1:T(8,128)} fusion(s32[2048]{0:T(1024)} %bitcast.586, f32[2048,4]{1,0:T(8,128)} %copy.220, f32[]{:T(128)} %constant.243.clone.1), kind=kCustom, calls=%fused_computation.56 | custom fusion | bytes 49664 | tf_op jit(solution)/shard_map/scatter | solution.py:210
  69.0 1.9 %copy.221 = f32[4,128,24]{1,2,0:T(8,128)S(1)} copy(f32[4,128,24]{0,2,1:T(8,128)} %bitcast.530) | data formatting | bytes 98304 | tf_op jit(solution)/shard_map/reshape | solution.py:211
  70.9 0.7 copy.222
  71.6 8.3 %all-to-all-start = ((f32[128,1,96]{2,1,0:T(1,128)}), f32[128,1,96]{2,1,0:T(1,128)S(1)}, u32[]{:S(2)}, u32[]{:S(2)}) async-start(f32[128,1,96]{2,1,0:T(1,128)} %copy.222), calls=%async_computation | async-start | bytes 131072 | tf_op jit(solution)/shard_map/all_to_all | solution.py:214
  80.0 0.8 broadcast_select_fusion.5
  81.1 0.6 fusion.204
  81.8 0.6 fusion.200
  82.4 0.6 fusion.202
  83.1 8.0 %all-to-all-done = f32[128,1,96]{2,1,0:T(1,128)S(1)} async-done(((f32[128,1,96]{2,1,0:T(1,128)}), f32[128,1,96]{2,1,0:T(1,128)S(1)}, u32[]{:S(2)}, u32[]{:S(2)}) %all-to-all-start) | async-done | bytes 49184 | tf_op jit(solution)/shard_map/all_to_all | solution.py:214
  91.9 0.9 select_reduce_fusion.2
  93.4 0.9 convolution_multiply_fusion
  94.4 0.6 reshape.5660
  95.1 0.7 fusion.6
  95.8 0.7 fusion.7
  96.4 0.7 fusion.8
  97.9 0.6 convolution_subtract_fusion.4
  98.5 0.6 convolution_subtract_fusion.5
  99.1 0.6 fusion.137
  99.8 1.9 %collective-permute-start.10 = (f32[4,4,512]{2,1,0:T(4,128)S(1)}, f32[4,4,512]{2,1,0:T(4,128)S(1)}, u32[]{:S(2)}, u32[]{:S(2)}) collective-permute-start(f32[4,4,512]{2,1,0:T(4,128)S(1)} %fusion.66), channel_id=1, source_target_pairs={{0,2},{2,0},{1,3},{3,1},{4,6},{6,4},{5,7},{7,5},{8,10},{10,8},{9,1... | collective-permute-start | bytes 98312 | tf_op jit(solution)/shard_map/ppermute | solution.py:85
  102.3 0.6 fusion.5
  102.9 7.5 %collective-permute-start.11 = (f32[4,1,512]{2,1,0:T(1,128)S(1)}, f32[4,1,512]{2,1,0:T(1,128)S(1)}, u32[]{:S(2)}, u32[]{:S(2)}) collective-permute-start(f32[4,1,512]{2,1,0:T(1,128)S(1)} %broadcast_select_fusion.10), channel_id=1, source_target_pairs={{0,1},{1,0},{2,3},{3,2},{4,5},{5,4},{6,7},{7,6},{8,9},{9,8},{10,11... | collective-permute-start | bytes 24584 | tf_op jit(solution)/shard_map/ppermute | solution.py:85
  110.6 4.4 %collective-permute-start.9 = (f32[4,4,64]{2,1,0:T(4,128)S(1)}, f32[4,4,64]{2,1,0:T(4,128)S(1)}, u32[]{:S(2)}, u32[]{:S(2)}) collective-permute-start(f32[4,4,64]{2,1,0:T(4,128)S(1)} %get-tuple-element.140), channel_id=1, source_target_pairs={{4,0},{8,4},{12,8},{16,12},{20,16},{24,20},{28,24},{32,28},{36,32}... | collective-permute-start | bytes 12296 | tf_op jit(solution)/shard_map/ppermute | solution.py:89
  115.0 1.9 %collective-permute-start.8 = (f32[4,4,64]{2,1,0:T(4,128)S(1)}, f32[4,4,64]{2,1,0:T(4,128)S(1)}, u32[]{:S(2)}, u32[]{:S(2)}) collective-permute-start(f32[4,4,64]{2,1,0:T(4,128)S(1)} %get-tuple-element.141), channel_id=1, source_target_pairs={{0,4},{4,8},{8,12},{12,16},{16,20},{20,24},{24,28},{28,32},{32,36}... | collective-permute-start | bytes 12296 | tf_op jit(solution)/shard_map/ppermute | solution.py:88
  117.3 7.5 %collective-permute-done.8 = f32[4,4,64]{2,1,0:T(4,128)S(1)} collective-permute-done((f32[4,4,64]{2,1,0:T(4,128)S(1)}, f32[4,4,64]{2,1,0:T(4,128)S(1)}, u32[]{:S(2)}, u32[]{:S(2)}) %collective-permute-start.8) | collective-permute-done | bytes 4128 | tf_op jit(solution)/shard_map/ppermute | solution.py:88
  125.8 0.6 fusion.1
  126.4 0.6 fusion.2
  127.0 0.6 fusion.124
  127.7 1.9 %collective-permute-start.14 = (f32[4,4,512]{2,1,0:T(4,128)S(1)}, f32[4,4,512]{2,1,0:T(4,128)S(1)}, u32[]{:S(2)}, u32[]{:S(2)}) collective-permute-start(f32[4,4,512]{2,1,0:T(4,128)S(1)} %fusion.78), channel_id=1, source_target_pairs={{0,2},{2,0},{1,3},{3,1},{4,6},{6,4},{5,7},{7,5},{8,10},{10,8},{9,1... | collective-permute-start | bytes 98312 | tf_op jit(solution)/shard_map/ppermute | solution.py:85
  130.3 2.3 %collective-permute-start.15 = (f32[4,1,512]{2,1,0:T(1,128)S(1)}, f32[4,1,512]{2,1,0:T(1,128)S(1)}, u32[]{:S(2)}, u32[]{:S(2)}) collective-permute-start(f32[4,1,512]{2,1,0:T(1,128)S(1)} %broadcast_select_fusion.8), channel_id=1, source_target_pairs={{0,1},{1,0},{2,3},{3,2},{4,5},{5,4},{6,7},{7,6},{8,9},{9,8},{10,11... | collective-permute-start | bytes 24584 | tf_op jit(solution)/shard_map/ppermute | solution.py:85
  133.3 1.9 %collective-permute-start.13 = (f32[4,4,64]{2,1,0:T(4,128)S(1)}, f32[4,4,64]{2,1,0:T(4,128)S(1)}, u32[]{:S(2)}, u32[]{:S(2)}) collective-permute-start(f32[4,4,64]{2,1,0:T(4,128)S(1)} %get-tuple-element.104), channel_id=1, source_target_pairs={{4,0},{8,4},{12,8},{16,12},{20,16},{24,20},{28,24},{32,28},{36,32}... | collective-permute-start | bytes 12296 | tf_op jit(solution)/shard_map/ppermute | solution.py:89
  135.2 3.9 %collective-permute-start.12 = (f32[4,4,64]{2,1,0:T(4,128)S(1)}, f32[4,4,64]{2,1,0:T(4,128)S(1)}, u32[]{:S(2)}, u32[]{:S(2)}) collective-permute-start(f32[4,4,64]{2,1,0:T(4,128)S(1)} %get-tuple-element.105), channel_id=1, source_target_pairs={{0,4},{4,8},{8,12},{12,16},{16,20},{20,24},{24,28},{28,32},{32,36}... | collective-permute-start | bytes 12296 | tf_op jit(solution)/shard_map/ppermute | solution.py:88
  139.1 0.9 collective-permute-done.15
  140.3 4.6 %collective-permute-done.12 = f32[4,4,64]{2,1,0:T(4,128)S(1)} collective-permute-done((f32[4,4,64]{2,1,0:T(4,128)S(1)}, f32[4,4,64]{2,1,0:T(4,128)S(1)}, u32[]{:S(2)}, u32[]{:S(2)}) %collective-permute-start.12) | collective-permute-done | bytes 4128 | tf_op jit(solution)/shard_map/ppermute | solution.py:88
  145.3 1.0 fusion.28
  (180 shorter events, 10.6 us)
Async XLA Ops:
  1.9 48.8 %collective-permute-start.1 = (bf16[3,1,8,128]{3,2,1,0:T(8,128)(2,1)}, bf16[3,1,8,128]{3,2,1,0:T(8,128)(2,1)}, u32[]{:S(2)}, u32[]{:S(2)}) collective-permute-start(bf16[3,1,8,128]{3,2,1,0:T(8,128)(2,1)} %get-tuple-element.191), channel_id=1, source_target_pairs={{0,4},{4,8},{8,12},{12,16},{16,20},{20,24},{24,28},{28,32},{32,36}... | collective-permute-start | bytes 18440 | tf_op jit(solution)/shard_map/ppermute | solution.py:88
  5.4 54.2 %collective-permute-start = (bf16[3,1,8,128]{3,2,1,0:T(8,128)(2,1)}, bf16[3,1,8,128]{3,2,1,0:T(8,128)(2,1)}, u32[]{:S(2)}, u32[]{:S(2)}) collective-permute-start(bf16[3,1,8,128]{3,2,1,0:T(8,128)(2,1)} %get-tuple-element.190), channel_id=1, source_target_pairs={{4,0},{8,4},{12,8},{16,12},{20,16},{24,20},{28,24},{32,28},{36,32}... | collective-permute-start | bytes 18440 | tf_op jit(solution)/shard_map/ppermute | solution.py:89
  13.4 34.6 %collective-permute-start.2 = (bf16[3,2,1,128]{3,2,1,0:T(2,128)(2,1)}, bf16[3,2,1,128]{3,2,1,0:T(2,128)(2,1)}, u32[]{:S(2)}, u32[]{:S(2)}) collective-permute-start(bf16[3,2,1,128]{3,2,1,0:T(2,128)(2,1)} %broadcast_select_fusion.18), channel_id=1, source_target_pairs={{0,2},{2,0},{1,3},{3,1},{4,6},{6,4},{5,7},{7,5},{8,10},{10,8},{9,1... | collective-permute-start | bytes 4616 | tf_op jit(solution)/shard_map/ppermute | solution.py:85
  16.8 28.3 %collective-permute-start.3 = (bf16[3,2,8,1]{3,2,1,0:T(8,128)(2,1)}, bf16[3,2,8,1]{3,2,1,0:T(8,128)(2,1)}, u32[]{:S(2)}, u32[]{:S(2)}) collective-permute-start(bf16[3,2,8,1]{3,2,1,0:T(8,128)(2,1)} %slice_select_fusion), channel_id=1, source_target_pairs={{0,1},{1,0},{2,3},{3,2},{4,5},{5,4},{6,7},{7,6},{8,9},{9,8},{10,11... | collective-permute-start | bytes 296 | tf_op jit(solution)/shard_map/ppermute | solution.py:85
  26.8 53.2 %collective-permute-start.6 = (f32[4,4,512]{2,1,0:T(4,128)}, f32[4,4,512]{2,1,0:T(4,128)}, u32[]{:S(2)}, u32[]{:S(2)}) collective-permute-start(f32[4,4,512]{2,1,0:T(4,128)} %bitcast.531), channel_id=1, source_target_pairs={{0,2},{2,0},{1,3},{3,1},{4,6},{6,4},{5,7},{7,5},{8,10},{10,8},{9,1... | collective-permute-start | bytes 98312 | tf_op jit(solution)/shard_map/ppermute | solution.py:85
  32.1 8.7 %copy-start.32 = (pred[512]{0:T(512)(128)(4,1)}, pred[512]{0:T(512)(128)(4,1)S(1)}, u32[]{:S(2)}) copy-start(pred[512]{0:T(512)(128)(4,1)S(1)} %get-tuple-element.211) | copy-start | bytes 1540
  32.1 9.1 %copy-start.33 = (pred[512]{0:T(512)(128)(4,1)}, pred[512]{0:T(512)(128)(4,1)S(1)}, u32[]{:S(2)}) copy-start(pred[512]{0:T(512)(128)(4,1)S(1)} %fusion.175) | copy-start | bytes 1540
  38.8 0.7 copy-start.2
  38.8 2.0 %copy-start.18 = (f32[8,512]{1,0:T(8,128)S(1)}, f32[8,512]{1,0:T(8,128)}, u32[]{:S(2)}) copy-start(f32[8,512]{1,0:T(8,128)} %constant.278.clone) | copy-start | bytes 49156
  39.2 2.1 %copy-start.17 = (f32[8,512]{1,0:T(8,128)S(1)}, f32[8,512]{1,0:T(8,128)}, u32[]{:S(2)}) copy-start(f32[8,512]{1,0:T(8,128)} %constant.277.clone) | copy-start | bytes 49156
  40.8 2.2 %copy-start.1 = (f32[4,1,1,4,512]{4,3,2,1,0:T(4,128)S(1)}, f32[4,1,1,4,512]{4,3,2,1,0:T(4,128)}, u32[]{:S(2)}) copy-start(f32[4,1,1,4,512]{4,3,2,1,0:T(4,128)} %param.15) | copy-start | bytes 98308
  41.3 2.4 %copy-start.19 = (s32[1,1,2048]{2,1,0:T(1,128)S(1)}, s32[1,1,2048]{2,1,0:T(1,128)}, u32[]{:S(2)}) copy-start(s32[1,1,2048]{2,1,0:T(1,128)} %param.14) | copy-start | bytes 24580
  41.3 2.4 %copy-start.20 = (s32[1,1,2048]{2,1,0:T(1,128)S(1)}, s32[1,1,2048]{2,1,0:T(1,128)}, u32[]{:S(2)}) copy-start(s32[1,1,2048]{2,1,0:T(1,128)} %param.13) | copy-start | bytes 24580
  43.0 2.1 %copy-start.22 = (f32[4,1,512]{2,1,0:T(1,128)S(1)}, f32[4,1,512]{2,1,0:T(1,128)}, u32[]{:S(2)}) copy-start(f32[4,1,512]{2,1,0:T(1,128)} %broadcast_select_fusion.12) | copy-start | bytes 24580
  43.0 5.0 %copy-start.24 = (f32[4,4,64]{2,1,0:T(4,128)S(1)}, f32[4,4,64]{2,1,0:T(4,128)}, u32[]{:S(2)}) copy-start(f32[4,4,64]{2,1,0:T(4,128)} %get-tuple-element.177) | copy-start | bytes 12292
  43.0 7.7 %copy-start.23 = (f32[4,4,64]{2,1,0:T(4,128)S(1)}, f32[4,4,64]{2,1,0:T(4,128)}, u32[]{:S(2)}) copy-start(f32[4,4,64]{2,1,0:T(4,128)} %get-tuple-element.176) | copy-start | bytes 12292
  43.7 16.6 %copy-start = (bf16[3,2,8,128]{3,2,1,0:T(8,128)(2,1)S(1)}, bf16[3,2,8,128]{3,2,1,0:T(8,128)(2,1)}, u32[]{:S(2)}) copy-start(bf16[3,2,8,128]{3,2,1,0:T(8,128)(2,1)} %param.10) | copy-start | bytes 36868
  43.7 16.6 %copy-start.21 = (f32[2,8,128]{2,1,0:T(8,128)S(1)}, f32[2,8,128]{2,1,0:T(8,128)}, u32[]{:S(2)}) copy-start(f32[2,8,128]{2,1,0:T(8,128)} %param.11) | copy-start | bytes 24580
  45.1 34.8 %collective-permute-start.7 = (f32[4,1,512]{2,1,0:T(1,128)S(1)}, f32[4,1,512]{2,1,0:T(1,128)S(1)}, u32[]{:S(2)}, u32[]{:S(2)}) collective-permute-start(f32[4,1,512]{2,1,0:T(1,128)S(1)} %copy-done.22), channel_id=1, source_target_pairs={{0,1},{1,0},{2,3},{3,2},{4,5},{5,4},{6,7},{7,6},{8,9},{9,8},{10,11... | collective-permute-start | bytes 24584 | tf_op jit(solution)/shard_map/ppermute | solution.py:85
  48.0 32.9 %collective-permute-start.4 = (f32[4,4,64]{2,1,0:T(4,128)S(1)}, f32[4,4,64]{2,1,0:T(4,128)S(1)}, u32[]{:S(2)}, u32[]{:S(2)}) collective-permute-start(f32[4,4,64]{2,1,0:T(4,128)S(1)} %copy-done.24), channel_id=1, source_target_pairs={{0,4},{4,8},{8,12},{12,16},{16,20},{20,24},{24,28},{28,32},{32,36}... | collective-permute-start | bytes 12296 | tf_op jit(solution)/shard_map/ppermute | solution.py:88
  50.7 30.2 %collective-permute-start.5 = (f32[4,4,64]{2,1,0:T(4,128)S(1)}, f32[4,4,64]{2,1,0:T(4,128)S(1)}, u32[]{:S(2)}, u32[]{:S(2)}) collective-permute-start(f32[4,4,64]{2,1,0:T(4,128)S(1)} %copy-done.23), channel_id=1, source_target_pairs={{4,0},{8,4},{12,8},{16,12},{20,16},{24,20},{28,24},{32,28},{36,32}... | collective-permute-start | bytes 12296 | tf_op jit(solution)/shard_map/ppermute | solution.py:89
  70.9 21.0 %copy-start.31 = (f32[8,16]{1,0:T(8,128)S(1)}, f32[8,16]{1,0:T(8,128)}, u32[]{:S(2)}) copy-start(f32[8,16]{1,0:T(8,128)} %constant.275.clone) | copy-start | bytes 1540
  71.6 19.4 %all-to-all-start = ((f32[128,1,96]{2,1,0:T(1,128)}), f32[128,1,96]{2,1,0:T(1,128)S(1)}, u32[]{:S(2)}, u32[]{:S(2)}) async-start(f32[128,1,96]{2,1,0:T(1,128)} %copy.222), calls=%async_computation | async-start | bytes 131072 | tf_op jit(solution)/shard_map/all_to_all | solution.py:214
  95.0 2.1 %copy-start.6 = (f32[2,4,512]{2,1,0:T(4,128)S(1)}, f32[2,4,512]{2,1,0:T(4,128)}, u32[]{:S(2)}) copy-start(f32[2,4,512]{2,1,0:T(4,128)} %get-tuple-element.158) | copy-start | bytes 49156
  95.0 2.1 %copy-start.7 = (f32[2,4,512]{2,1,0:T(4,128)S(1)}, f32[2,4,512]{2,1,0:T(4,128)}, u32[]{:S(2)}) copy-start(f32[2,4,512]{2,1,0:T(4,128)} %get-tuple-element.231) | copy-start | bytes 49156
  95.0 2.1 %copy-start.8 = (f32[2,4,512]{2,1,0:T(4,128)S(1)}, f32[2,4,512]{2,1,0:T(4,128)}, u32[]{:S(2)}) copy-start(f32[2,4,512]{2,1,0:T(4,128)} %get-tuple-element.142) | copy-start | bytes 49156
  95.0 2.1 %copy-start.9 = (f32[2,4,512]{2,1,0:T(4,128)S(1)}, f32[2,4,512]{2,1,0:T(4,128)}, u32[]{:S(2)}) copy-start(f32[2,4,512]{2,1,0:T(4,128)} %get-tuple-element.223) | copy-start | bytes 49156
  95.0 2.1 %copy-start.13 = (f32[1,4,512]{2,1,0:T(4,128)S(1)}, f32[1,4,512]{2,1,0:T(4,128)}, u32[]{:S(2)}) copy-start(f32[1,4,512]{2,1,0:T(4,128)} %get-tuple-element.146) | copy-start | bytes 24580
  95.0 2.1 %copy-start.14 = (f32[1,4,512]{2,1,0:T(4,128)S(1)}, f32[1,4,512]{2,1,0:T(4,128)}, u32[]{:S(2)}) copy-start(f32[1,4,512]{2,1,0:T(4,128)} %get-tuple-element.149) | copy-start | bytes 24580
  95.0 2.1 %copy-start.15 = (f32[1,4,512]{2,1,0:T(4,128)S(1)}, f32[1,4,512]{2,1,0:T(4,128)}, u32[]{:S(2)}) copy-start(f32[1,4,512]{2,1,0:T(4,128)} %get-tuple-element.226) | copy-start | bytes 24580
  95.0 2.1 %copy-start.16 = (f32[1,4,512]{2,1,0:T(4,128)S(1)}, f32[1,4,512]{2,1,0:T(4,128)}, u32[]{:S(2)}) copy-start(f32[1,4,512]{2,1,0:T(4,128)} %get-tuple-element.229) | copy-start | bytes 24580
  95.1 2.1 %copy-start.25 = (pred[512]{0:T(512)(128)(4,1)S(1)}, pred[512]{0:T(512)(128)(4,1)}, u32[]{:S(2)}) copy-start(pred[512]{0:T(512)(128)(4,1)} %get-tuple-element.234) | copy-start | bytes 1540
  95.1 2.1 %copy-start.26 = (pred[512]{0:T(512)(128)(4,1)S(1)}, pred[512]{0:T(512)(128)(4,1)}, u32[]{:S(2)}) copy-start(pred[512]{0:T(512)(128)(4,1)} %get-tuple-element.235) | copy-start | bytes 1540
  95.1 2.1 %copy-start.27 = (pred[512]{0:T(512)(128)(4,1)S(1)}, pred[512]{0:T(512)(128)(4,1)}, u32[]{:S(2)}) copy-start(pred[512]{0:T(512)(128)(4,1)} %get-tuple-element.236) | copy-start | bytes 1540
  95.1 2.1 %copy-start.28 = (pred[512]{0:T(512)(128)(4,1)S(1)}, pred[512]{0:T(512)(128)(4,1)}, u32[]{:S(2)}) copy-start(pred[512]{0:T(512)(128)(4,1)} %get-tuple-element.237) | copy-start | bytes 1540
  95.1 2.1 %copy-start.29 = (pred[512]{0:T(512)(128)(4,1)S(1)}, pred[512]{0:T(512)(128)(4,1)}, u32[]{:S(2)}) copy-start(pred[512]{0:T(512)(128)(4,1)} %get-tuple-element.232) | copy-start | bytes 1540
  95.1 2.1 %copy-start.30 = (pred[512]{0:T(512)(128)(4,1)S(1)}, pred[512]{0:T(512)(128)(4,1)}, u32[]{:S(2)}) copy-start(pred[512]{0:T(512)(128)(4,1)} %get-tuple-element.233) | copy-start | bytes 1540
  99.8 17.3 %collective-permute-start.10 = (f32[4,4,512]{2,1,0:T(4,128)S(1)}, f32[4,4,512]{2,1,0:T(4,128)S(1)}, u32[]{:S(2)}, u32[]{:S(2)}) collective-permute-start(f32[4,4,512]{2,1,0:T(4,128)S(1)} %fusion.66), channel_id=1, source_target_pairs={{0,2},{2,0},{1,3},{3,1},{4,6},{6,4},{5,7},{7,5},{8,10},{10,8},{9,1... | collective-permute-start | bytes 98312 | tf_op jit(solution)/shard_map/ppermute | solution.py:85
  102.9 14.0 %collective-permute-start.11 = (f32[4,1,512]{2,1,0:T(1,128)S(1)}, f32[4,1,512]{2,1,0:T(1,128)S(1)}, u32[]{:S(2)}, u32[]{:S(2)}) collective-permute-start(f32[4,1,512]{2,1,0:T(1,128)S(1)} %broadcast_select_fusion.10), channel_id=1, source_target_pairs={{0,1},{1,0},{2,3},{3,2},{4,5},{5,4},{6,7},{7,6},{8,9},{9,8},{10,11... | collective-permute-start | bytes 24584 | tf_op jit(solution)/shard_map/ppermute | solution.py:85
  110.6 6.7 %collective-permute-start.9 = (f32[4,4,64]{2,1,0:T(4,128)S(1)}, f32[4,4,64]{2,1,0:T(4,128)S(1)}, u32[]{:S(2)}, u32[]{:S(2)}) collective-permute-start(f32[4,4,64]{2,1,0:T(4,128)S(1)} %get-tuple-element.140), channel_id=1, source_target_pairs={{4,0},{8,4},{12,8},{16,12},{20,16},{24,20},{28,24},{32,28},{36,32}... | collective-permute-start | bytes 12296 | tf_op jit(solution)/shard_map/ppermute | solution.py:89
  115.0 9.8 %collective-permute-start.8 = (f32[4,4,64]{2,1,0:T(4,128)S(1)}, f32[4,4,64]{2,1,0:T(4,128)S(1)}, u32[]{:S(2)}, u32[]{:S(2)}) collective-permute-start(f32[4,4,64]{2,1,0:T(4,128)S(1)} %get-tuple-element.141), channel_id=1, source_target_pairs={{0,4},{4,8},{8,12},{12,16},{16,20},{20,24},{24,28},{28,32},{32,36}... | collective-permute-start | bytes 12296 | tf_op jit(solution)/shard_map/ppermute | solution.py:88
  127.7 12.5 %collective-permute-start.14 = (f32[4,4,512]{2,1,0:T(4,128)S(1)}, f32[4,4,512]{2,1,0:T(4,128)S(1)}, u32[]{:S(2)}, u32[]{:S(2)}) collective-permute-start(f32[4,4,512]{2,1,0:T(4,128)S(1)} %fusion.78), channel_id=1, source_target_pairs={{0,2},{2,0},{1,3},{3,1},{4,6},{6,4},{5,7},{7,5},{8,10},{10,8},{9,1... | collective-permute-start | bytes 98312 | tf_op jit(solution)/shard_map/ppermute | solution.py:85
  130.3 15.0 %copy-start.3 = (f32[2,1,1,4,512]{4,3,0,2,1:T(4,128)S(1)}, f32[2,1,1,4,512]{4,3,0,2,1:T(4,128)}, u32[]{:S(2)}) copy-start(f32[2,1,1,4,512]{4,3,0,2,1:T(4,128)} %get-tuple-element.230) | copy-start | bytes 49156
  130.3 15.0 %copy-start.4 = (f32[2,1,1,4,512]{4,3,0,2,1:T(4,128)S(1)}, f32[2,1,1,4,512]{4,3,0,2,1:T(4,128)}, u32[]{:S(2)}) copy-start(f32[2,1,1,4,512]{4,3,0,2,1:T(4,128)} %get-tuple-element.143) | copy-start | bytes 49156
  130.3 15.0 %copy-start.5 = (f32[2,1,1,4,512]{4,3,0,2,1:T(4,128)S(1)}, f32[2,1,1,4,512]{4,3,0,2,1:T(4,128)}, u32[]{:S(2)}) copy-start(f32[2,1,1,4,512]{4,3,0,2,1:T(4,128)} %get-tuple-element.222) | copy-start | bytes 49156
  130.3 15.0 %copy-start.10 = (f32[1,1,1,4,512]{4,3,0,2,1:T(4,128)S(1)}, f32[1,1,1,4,512]{4,3,0,2,1:T(4,128)}, u32[]{:S(2)}) copy-start(f32[1,1,1,4,512]{4,3,0,2,1:T(4,128)} %get-tuple-element.148) | copy-start | bytes 24580
  130.3 15.0 %copy-start.11 = (f32[1,1,1,4,512]{4,3,2,1,0:T(4,128)S(1)}, f32[1,1,1,4,512]{4,3,2,1,0:T(4,128)}, u32[]{:S(2)}) copy-start(f32[1,1,1,4,512]{4,3,2,1,0:T(4,128)} %get-tuple-element.227) | copy-start | bytes 24580
  130.3 15.0 %copy-start.12 = (f32[1,1,1,4,512]{4,3,2,1,0:T(4,128)S(1)}, f32[1,1,1,4,512]{4,3,2,1,0:T(4,128)}, u32[]{:S(2)}) copy-start(f32[1,1,1,4,512]{4,3,2,1,0:T(4,128)} %get-tuple-element.228) | copy-start | bytes 24580
  130.3 9.7 %collective-permute-start.15 = (f32[4,1,512]{2,1,0:T(1,128)S(1)}, f32[4,1,512]{2,1,0:T(1,128)S(1)}, u32[]{:S(2)}, u32[]{:S(2)}) collective-permute-start(f32[4,1,512]{2,1,0:T(1,128)S(1)} %broadcast_select_fusion.8), channel_id=1, source_target_pairs={{0,1},{1,0},{2,3},{3,2},{4,5},{5,4},{6,7},{7,6},{8,9},{9,8},{10,11... | collective-permute-start | bytes 24584 | tf_op jit(solution)/shard_map/ppermute | solution.py:85
  133.3 7.1 %collective-permute-start.13 = (f32[4,4,64]{2,1,0:T(4,128)S(1)}, f32[4,4,64]{2,1,0:T(4,128)S(1)}, u32[]{:S(2)}, u32[]{:S(2)}) collective-permute-start(f32[4,4,64]{2,1,0:T(4,128)S(1)} %get-tuple-element.104), channel_id=1, source_target_pairs={{4,0},{8,4},{12,8},{16,12},{20,16},{24,20},{28,24},{32,28},{36,32}... | collective-permute-start | bytes 12296 | tf_op jit(solution)/shard_map/ppermute | solution.py:89
  135.2 9.8 %collective-permute-start.12 = (f32[4,4,64]{2,1,0:T(4,128)S(1)}, f32[4,4,64]{2,1,0:T(4,128)S(1)}, u32[]{:S(2)}, u32[]{:S(2)}) collective-permute-start(f32[4,4,64]{2,1,0:T(4,128)S(1)} %get-tuple-element.105), channel_id=1, source_target_pairs={{0,4},{4,8},{8,12},{12,16},{16,20},{20,24},{24,28},{28,32},{32,36}... | collective-permute-start | bytes 12296 | tf_op jit(solution)/shard_map/ppermute | solution.py:88
where the time goes:
time: 148 us; the launch traced here: 146 us
  starting transfers between devices  70.5 us (48%)
  local copies, waits for them, and re-layouts  21.8 us (15%)
  waiting for transfers between devices  21 us (14%)
  other arithmetic  19 us (13%)
  matrix products  12.1 us (8%)
  between operations  1.85 us (1%)
    ppermute x8, starting transfers between devices, neighbours(): got = lax.ppermute(sent, axis, [(0, 1), (1, 0)])  30 us
    ppermute x4, starting transfers between devices, neighbours(): lax.ppermute(lower, axis, [(i + 1, i) for i in range(count - 1)])  21 us
    ppermute x4, waiting for transfers between devices, neighbours(): lax.ppermute(upper, axis, [(i, i + 1) for i in range(count - 1)])  12.1 us
    ppermute x4, starting transfers between devices, neighbours(): lax.ppermute(upper, axis, [(i, i + 1) for i in range(count - 1)])  11.2 us
    all_to_all x1, starting transfers between devices, on_device(): got = lax.all_to_all(send, 'gx', split_axis=0, concat_axis=0, tiled=True)  8.27 us
    all_to_all x1, waiting for transfers between devices, on_device(): got = lax.all_to_all(send, 'gx', split_axis=0, concat_axis=0, tiled=True)  7.96 us
    scatter x1, local copies, waits for them, and re-layouts, on_device(): send = jnp.zeros((4, owner_count * capacity), jnp.float32).at[:, slot_ind...  7.15 us
    dot_general x9, matrix products, tendency(): grads = [jnp.dot(fields[0], table, precision=highest) for table in tables]  5.61 us
  transfers between devices with their start and end apart: 17, of which 4 were waited for; matrix products, arithmetic and copies ran while one was open for 26% of the time, Pallas kernels for 0%

commit v1 on v0

--- a/solution.py
+++ b/solution.py
@@ -90,10 +90,52 @@
     return from_below, from_above
 
 
-def source_cells(velocity, viscosity):
-    below_x, above_x = neighbours(velocity[:, :1], velocity[:, -1:], "gx")
-    below_y, above_y = neighbours(velocity[:, :, :1], velocity[:, :, -1:], "gy")
-    below_z, above_z = neighbours(velocity[..., :1], velocity[..., -1:], "gz")
+def neighbours_joined(pairs, axis):
+    flat = lambda t: t.astype(jnp.float32).reshape(-1)
+    lower = jnp.concatenate([flat(low) for low, _ in pairs])
+    upper = jnp.concatenate([flat(high) for _, high in pairs])
+    from_below, from_above = neighbours(lower, upper, axis)
+    results = []
+    start = 0
+    for low, high in pairs:
+        size = low.size
+        results.append(
+            (
+                from_below[start : start + size].reshape(high.shape).astype(high.dtype),
+                from_above[start : start + size].reshape(low.shape).astype(low.dtype),
+            )
+        )
+        start += size
+    return results
+
+
+def velocity_faces(velocity):
+    return (
+        (velocity[:, :1], velocity[:, -1:]),
+        (velocity[:, :, :1], velocity[:, :, -1:]),
+        (velocity[..., :1], velocity[..., -1:]),
+    )
+
+
+def state_faces(fields):
+    count = fields.shape[1]
+    face = 64
+    return (
+        (fields[..., :face], fields[..., NODES - face :]),
+        (fields, fields),
+        (fields[:, :1], fields[:, count - 1 :]),
+    )
+
+
+def exchange(face_sets):
+    per_axis = []
+    for direction, axis in enumerate(("gx", "gy", "gz")):
+        per_axis.append(neighbours_joined([faces[direction] for faces in face_sets], axis))
+    return [tuple(per_axis[d][k] for d in range(3)) for k in range(len(face_sets))]
+
+
+def source_cells(velocity, viscosity, halo):
+    (below_x, above_x), (below_y, above_y), (below_z, above_z) = halo
     centre = velocity.astype(jnp.float32)
     f32 = lambda t: t.astype(jnp.float32)
     plus_x = jnp.concatenate([centre[:, 1:], f32(above_x)], axis=1)
@@ -127,7 +169,7 @@
     return LIFT_FACTOR * jnp.stack(parts)
 
 
-def tendency(fields, forcing, tables):
+def tendency(fields, forcing, tables, halo=None):
     highest = lax.Precision.HIGHEST
     count = fields.shape[1]
     grads = [jnp.dot(fields[0], table, precision=highest) for table in tables]
@@ -146,13 +188,13 @@
     )
 
     face = 64
-    below_x, above_x = neighbours(fields[..., :face], fields[..., NODES - face :], "gx")
+    if halo is None:
+        halo = exchange([state_faces(fields)])[0]
+    (below_x, above_x), (below_y, above_y), (below_z, above_z) = halo
     outer_lower_x = jnp.pad(below_x, ((0, 0), (0, 0), (0, NODES - face)))
     outer_upper_x = jnp.pad(above_x, ((0, 0), (0, 0), (NODES - face, 0)))
-    below_y, above_y = neighbours(fields, fields, "gy")
     outer_lower_y = jnp.roll(below_y, -56, axis=2)
     outer_upper_y = jnp.roll(above_y, 56, axis=2)
-    below_z, above_z = neighbours(fields[:, :1], fields[:, count - 1 :], "gz")
     outer_lower_z = jnp.roll(jnp.concatenate([below_z, fields[:, :-1]], axis=1), -7, axis=2)
     outer_upper_z = jnp.roll(jnp.concatenate([fields[:, 1:], above_z], axis=1), 7, axis=2)
 
@@ -172,10 +214,10 @@
     return result
 
 
-def runge_kutta(fields, forcing):
+def runge_kutta(fields, forcing, halo):
     tables = kron_tables()
     step = lambda f: tendency(f, forcing, tables)
-    section_one = fields + TIME_STEP * step(fields)
+    section_one = fields + TIME_STEP * tendency(fields, forcing, tables, halo)
     section_two = 0.75 * fields + 0.25 * (section_one + TIME_STEP * step(section_one))
     return 1.0 / 3.0 * fields + 2.0 / 3.0 * (section_two + TIME_STEP * step(section_two))
 
@@ -187,7 +229,10 @@
 
 
 def on_device(velocity, eddy_viscosity, cell_owner, cell_element, cell_position, acoustic_state):
-    sources = source_cells(velocity, eddy_viscosity)
+    local_elems = acoustic_state.shape[1] * acoustic_state.shape[2] * acoustic_state.shape[3]
+    fields = acoustic_state.reshape(4, local_elems, NODES)
+    velocity_halo, state_halo = exchange([velocity_faces(velocity), state_faces(fields)])
+    sources = source_cells(velocity, eddy_viscosity, velocity_halo)
     cell_count = sources.shape[1] * sources.shape[2] * sources.shape[3]
     flat_source = sources.reshape(3, cell_count).astype(jnp.float32)
     owners = cell_owner.reshape(cell_count)
@@ -210,11 +255,8 @@
         .set(payload)
         .reshape(4, owner_count, capacity)
     )
-    send = jnp.transpose(send, (1, 0, 2)).reshape(owner_count, 4 * capacity)
-    got = lax.all_to_all(send, "gx", split_axis=0, concat_axis=0, tiled=True)
-    got = jnp.transpose(got.reshape(owner_count, 4, capacity), (1, 0, 2)).reshape(
-        4, owner_count * capacity
-    )
+    got = lax.all_to_all(send, "gx", split_axis=1, concat_axis=1, tiled=True)
+    got = got.reshape(4, owner_count * capacity)
     got_source = got[:3].astype(jnp.bfloat16)
     got_ident = got[3].astype(jnp.int32)
     got_element = got_ident // subcells
@@ -229,7 +271,6 @@
         along_a[:, None, None, :] * along_b[None, :, None, :] * along_c[None, None, :, :]
     ).reshape(NODES, rows).astype(jnp.bfloat16)
 
-    local_elems = acoustic_state.shape[1] * acoustic_state.shape[2] * acoustic_state.shape[3]
     element_hot = got_element[None, :] == jnp.arange(local_elems, dtype=jnp.int32)[:, None]
     weighted = jnp.where(element_hot[None], got_source[:, None, :], jnp.zeros((), jnp.bfloat16))
     weighted = weighted.reshape(3 * local_elems, rows)
@@ -241,8 +282,7 @@
         acoustic_state.shape[1:4] + (3, NODES)
     )
 
-    fields = acoustic_state.reshape(4, local_elems, NODES)
-    next_state = runge_kutta(fields, forcing).reshape(acoustic_state.shape)
+    next_state = runge_kutta(fields, forcing, state_halo).reshape(acoustic_state.shape)
     return (moments, next_state)
 
 

time: 148 us -> 175 us (1.18)
  other arithmetic: 19 us -> 35.9 us
  local copies, waits for them, and re-layouts: 21.8 us -> 37.6 us
  starting transfers between devices: 70.5 us -> 59.9 us
  matrix products: 12.1 us -> 14.5 us
    reshape x0 -> x22, local copies, waits for them, and re-layouts: none -> 7.67 us  [the longest x10 3.22 us: neighbours_joined(): flat = lambda t: t.astype(jnp.float32).reshape(-1)]
    ppermute x4 -> x3, starting transfers between devices: 21 us -> 13.6 us  [neighbours(): lax.ppermute(lower, axis, [(i + 1, i) for i in range(count - 1)])]
    ppermute x8 -> x6, starting transfers between devices: 30 us -> 25.7 us  [neighbours(): got = lax.ppermute(sent, axis, [(0, 1), (1, 0)])]
    all_to_all x1, starting transfers between devices: 8.27 us -> 11.3 us  [on_device(): got = lax.all_to_all(send, 'gx', split_axis=1, concat_axis=1, tiled=True)]
    mul x3 -> x5, other arithmetic: 0.46 us -> 3.39 us  [face_correction(): result = -0.5 * difference]
    reshape x0 -> x3, other arithmetic: none -> 2.46 us  [neighbours_joined(): flat = lambda t: t.astype(jnp.float32).reshape(-1)]
    slice x6, local copies, waits for them, and re-layouts: 1.28 us -> 3.7 us  [face_correction(): parts = [result[i] for i in range(4)]]
    select_n x5 -> x4, other arithmetic: 4.31 us -> 1.93 us  [neighbours(): sent = jnp.where(index == 0, upper, lower)]
  transfers between devices with their start and end apart: 17 -> 13, of which waited for: 4 -> 5; matrix products, arithmetic and copies ran while one was open for 26% -> 23% of each run, Pallas kernels for 0% -> 0%
where the time goes in v1:
time: 175 us; the launch traced here: 172 us
  starting transfers between devices  59.9 us (34%)
  local copies, waits for them, and re-layouts  37.6 us (21%)
  other arithmetic  35.9 us (21%)
  waiting for transfers between devices  22.2 us (13%)
  matrix products  14.5 us (8%)
  between operations  2.42 us (1%)
    ppermute x6, starting transfers between devices, neighbours(): got = lax.ppermute(sent, axis, [(0, 1), (1, 0)])  25.7 us
    ppermute x3, starting transfers between devices, neighbours(): lax.ppermute(lower, axis, [(i + 1, i) for i in range(count - 1)])  13.6 us
    ppermute x3, waiting for transfers between devices, neighbours(): lax.ppermute(upper, axis, [(i, i + 1) for i in range(count - 1)])  11.6 us
    all_to_all x1, starting transfers between devices, on_device(): got = lax.all_to_all(send, 'gx', split_axis=1, concat_axis=1, tiled=True)  11.3 us
    ppermute x3, starting transfers between devices, neighbours(): lax.ppermute(upper, axis, [(i, i + 1) for i in range(count - 1)])  9.29 us
    all_to_all x1, waiting for transfers between devices, on_device(): got = lax.all_to_all(send, 'gx', split_axis=1, concat_axis=1, tiled=True)  9.11 us
    dot_general x9, matrix products, tendency(): grads = [jnp.dot(fields[0], table, precision=highest) for table in tables]  7.41 us
    scatter x1, local copies, waits for them, and re-layouts, on_device(): send = jnp.zeros((4, owner_count * capacity), jnp.float32).at[:, slot_ind...  7.16 us
  transfers between devices with their start and end apart: 13, of which 5 were waited for; matrix products, arithmetic and copies ran while one was open for 23% of the time, Pallas kernels for 0%

profile of v1, /device:TPU:64, one launch (start us, length us, event | category | flops | bytes accessed | tf_op | source)
XLA Modules:
  0.0 172.5 jit_solution(816024279318609193)
XLA Ops:
  0.6 0.8 fusion.213
  1.5 0.7 bitcast_convert_fusion.1
  2.8 3.5 %collective-permute-start.1 = (f32[4096]{0:T(1024)}, f32[4096]{0:T(1024)}, u32[]{:S(2)}, u32[]{:S(2)}) collective-permute-start(f32[4096]{0:T(1024)} %pad_maximum_fusion.16), channel_id=1, source_target_pairs={{0,4},{4,8},{8,12},{12,16},{16,20},{20,24},{24,28},{28,32},{32,36}... | collective-permute-start | bytes 49160 | tf_op jit(solution)/shard_map/ppermute | solution.py:88
  7.0 6.6 %collective-permute-start = (f32[4096]{0:T(1024)}, f32[4096]{0:T(1024)}, u32[]{:S(2)}, u32[]{:S(2)}) collective-permute-start(f32[4096]{0:T(1024)} %pad_maximum_fusion.15), channel_id=1, source_target_pairs={{4,0},{8,4},{12,8},{16,12},{20,16},{24,20},{28,24},{32,28},{36,32}... | collective-permute-start | bytes 49160 | tf_op jit(solution)/shard_map/ppermute | solution.py:89
  13.6 0.9 fusion.212
  14.4 0.9 convert_reduce_fusion
  16.2 10.0 %collective-permute-start.3 = (f32[2096]{0:T(1024)}, f32[2096]{0:T(1024)}, u32[]{:S(2)}, u32[]{:S(2)}) collective-permute-start(f32[2096]{0:T(1024)} %maximum_select_fusion.1), channel_id=1, source_target_pairs={{0,1},{1,0},{2,3},{3,2},{4,5},{5,4},{6,7},{7,6},{8,9},{9,8},{10,11... | collective-permute-start | bytes 25160 | tf_op jit(solution)/shard_map/ppermute | solution.py:85
  26.2 0.8 convert_reduce_fusion.2
  27.0 0.8 copy.394
  28.5 1.9 %collective-permute-start.2 = (f32[8960]{0:T(1024)}, f32[8960]{0:T(1024)}, u32[]{:S(2)}, u32[]{:S(2)}) collective-permute-start(f32[8960]{0:T(1024)} %maximum_select_fusion), channel_id=1, source_target_pairs={{0,2},{2,0},{1,3},{3,1},{4,6},{6,4},{5,7},{7,5},{8,10},{10,8},{9,1... | collective-permute-start | bytes 107528 | tf_op jit(solution)/shard_map/ppermute | solution.py:85
  30.4 0.7 fusion.216
  31.1 0.9 fusion.215
  32.0 0.8 fusion.214
  32.9 1.5 fusion.211
  35.5 0.8 copy.316
  39.8 1.2 and_select_fusion.2
  42.9 1.3 fusion.9
  45.3 0.7 broadcast_select_fusion.10
  46.4 0.7 slice_maximum_fusion.2
  48.4 0.7 fusion.167
  49.2 0.7 fusion.165
  53.2 0.8 broadcast_select_fusion.2
  55.4 0.8 multiply_subtract_fusion.2
  56.2 0.8 convert_bitcast_fusion
  57.1 0.7 maximum_bitcast_fusion
  57.8 1.3 copy.322
  59.1 7.2 %scatter_custom_fusion = f32[4,3072]{0,1:T(8,128)} fusion(s32[2048]{0:T(1024)} %bitcast.661, f32[2048,4]{1,0:T(8,128)} %copy.322, f32[]{:T(128)} %constant.243.clone.1), kind=kCustom, calls=%fused_computation.56 | custom fusion | bytes 49664 | tf_op jit(solution)/shard_map/scatter | solution.py:255
  66.3 3.0 %copy.323 = f32[4,128,24]{2,0,1:T(4,128)} copy(f32[4,128,24]{0,2,1:T(8,128)} %bitcast.586) | data formatting | bytes 98304 | tf_op jit(solution)/shard_map/reshape | solution.py:256
  69.2 11.3 %all-to-all-start = ((f32[4,128,24]{2,0,1:T(4,128)}), f32[4,128,24]{2,0,1:T(4,128)S(1)}, u32[]{:S(2)}, u32[]{:S(2)}) async-start(f32[4,128,24]{2,0,1:T(4,128)} %copy.323), calls=%async_computation | async-start | bytes 524288 | tf_op jit(solution)/shard_map/all_to_all | solution.py:258
  80.5 0.8 reshape.5996
  81.4 1.0 broadcast_multiply_fusion.13
  85.0 9.1 %all-to-all-done = f32[4,128,24]{2,0,1:T(4,128)S(1)} async-done(((f32[4,128,24]{2,0,1:T(4,128)}), f32[4,128,24]{2,0,1:T(4,128)S(1)}, u32[]{:S(2)}, u32[]{:S(2)}) %all-to-all-start) | async-done | bytes 49184 | tf_op jit(solution)/shard_map/all_to_all | solution.py:258
  94.1 0.9 fusion.20
  95.0 0.9 convert_element_type.167
  97.4 0.8 broadcast_select_fusion
  98.2 0.7 iota_compare_fusion.5
  98.9 0.7 iota_compare_fusion.4
  99.7 0.7 iota_compare_fusion.3
  100.4 0.9 select_reduce_fusion.2
  101.9 0.9 convolution_multiply_fusion
  105.4 1.9 %collective-permute-start.6 = (f32[8192]{0:T(1024)S(1)}, f32[8192]{0:T(1024)S(1)}, u32[]{:S(2)}, u32[]{:S(2)}) collective-permute-start(f32[8192]{0:T(1024)S(1)} %add.707), channel_id=1, source_target_pairs={{0,2},{2,0},{1,3},{3,1},{4,6},{6,4},{5,7},{7,5},{8,10},{10,8},{9,1... | collective-permute-start | bytes 98312 | tf_op jit(solution)/shard_map/ppermute | solution.py:85
  107.3 1.2 collective-permute-done.6
  108.6 0.7 broadcast_multiply_fusion.9
  114.3 1.9 %collective-permute-start.7 = (f32[2048]{0:T(1024)}, f32[2048]{0:T(1024)}, u32[]{:S(2)}, u32[]{:S(2)}) collective-permute-start(f32[2048]{0:T(1024)} %bitcast.123), channel_id=1, source_target_pairs={{0,1},{1,0},{2,3},{3,2},{4,5},{5,4},{6,7},{7,6},{8,9},{9,8},{10,11... | collective-permute-start | bytes 24584 | tf_op jit(solution)/shard_map/ppermute | solution.py:85
  116.2 1.4 reshape.6001
  117.6 5.1 %collective-permute-start.5 = (f32[1024]{0:T(1024)}, f32[1024]{0:T(1024)}, u32[]{:S(2)}, u32[]{:S(2)}) collective-permute-start(f32[1024]{0:T(1024)} %reshape.6001), channel_id=1, source_target_pairs={{4,0},{8,4},{12,8},{16,12},{20,16},{24,20},{28,24},{32,28},{36,32}... | collective-permute-start | bytes 12296 | tf_op jit(solution)/shard_map/ppermute | solution.py:89
  122.7 1.4 reshape.5999
  124.1 1.9 %collective-permute-start.4 = (f32[1024]{0:T(1024)}, f32[1024]{0:T(1024)}, u32[]{:S(2)}, u32[]{:S(2)}) collective-permute-start(f32[1024]{0:T(1024)} %reshape.5999), channel_id=1, source_target_pairs={{0,4},{4,8},{8,12},{12,16},{16,20},{20,24},{24,28},{28,32},{32,36}... | collective-permute-start | bytes 12296 | tf_op jit(solution)/shard_map/ppermute | solution.py:88
  126.7 0.8 reshape.6002
  127.5 6.6 %collective-permute-done.4 = f32[1024]{0:T(1024)} collective-permute-done((f32[1024]{0:T(1024)}, f32[1024]{0:T(1024)}, u32[]{:S(2)}, u32[]{:S(2)}) %collective-permute-start.4) | collective-permute-done | bytes 4128 | tf_op jit(solution)/shard_map/ppermute | solution.py:88
  134.1 1.3 reshape.6000
  135.4 0.7 broadcast_select_fusion.13
  136.2 0.8 broadcast_multiply_fusion.7
  140.2 0.8 fusion.79
  141.1 2.1 %collective-permute-start.10 = (f32[8192]{0:T(1024)S(1)}, f32[8192]{0:T(1024)S(1)}, u32[]{:S(2)}, u32[]{:S(2)}) collective-permute-start(f32[8192]{0:T(1024)S(1)} %multiply_add_fusion), channel_id=1, source_target_pairs={{0,2},{2,0},{1,3},{3,1},{4,6},{6,4},{5,7},{7,5},{8,10},{10,8},{9,1... | collective-permute-start | bytes 98312 | tf_op jit(solution)/shard_map/ppermute | solution.py:85
  144.3 0.7 broadcast_multiply_fusion.3
  145.0 1.2 fusion
  146.2 1.2 fusion.1
  147.4 1.2 fusion.2
  150.3 7.8 %collective-permute-start.11 = (f32[2048]{0:T(1024)S(1)}, f32[2048]{0:T(1024)S(1)}, u32[]{:S(2)}, u32[]{:S(2)}) collective-permute-start(f32[2048]{0:T(1024)S(1)} %bitcast.662), channel_id=1, source_target_pairs={{0,1},{1,0},{2,3},{3,2},{4,5},{5,4},{6,7},{7,6},{8,9},{9,8},{10,11... | collective-permute-start | bytes 24584 | tf_op jit(solution)/shard_map/ppermute | solution.py:85
  158.2 1.9 %collective-permute-start.9 = (f32[1024]{0:T(1024)S(1)}, f32[1024]{0:T(1024)S(1)}, u32[]{:S(2)}, u32[]{:S(2)}) collective-permute-start(f32[1024]{0:T(1024)S(1)} %reshape.6009), channel_id=1, source_target_pairs={{4,0},{8,4},{12,8},{16,12},{20,16},{24,20},{28,24},{32,28},{36,32}... | collective-permute-start | bytes 12296 | tf_op jit(solution)/shard_map/ppermute | solution.py:89
  160.2 3.9 %collective-permute-start.8 = (f32[1024]{0:T(1024)S(1)}, f32[1024]{0:T(1024)S(1)}, u32[]{:S(2)}, u32[]{:S(2)}) collective-permute-start(f32[1024]{0:T(1024)S(1)} %reshape.6007), channel_id=1, source_target_pairs={{0,4},{4,8},{8,12},{12,16},{16,20},{20,24},{24,28},{28,32},{32,36}... | collective-permute-start | bytes 12296 | tf_op jit(solution)/shard_map/ppermute | solution.py:88
  165.0 5.0 %collective-permute-done.8 = f32[1024]{0:T(1024)S(1)} collective-permute-done((f32[1024]{0:T(1024)S(1)}, f32[1024]{0:T(1024)S(1)}, u32[]{:S(2)}, u32[]{:S(2)}) %collective-permute-start.8) | collective-permute-done | bytes 4128 | tf_op jit(solution)/shard_map/ppermute | solution.py:88
  170.8 1.7 fusion.29
  (326 shorter events, 36.7 us)
Async XLA Ops:
  2.8 45.6 %collective-permute-start.1 = (f32[4096]{0:T(1024)}, f32[4096]{0:T(1024)}, u32[]{:S(2)}, u32[]{:S(2)}) collective-permute-start(f32[4096]{0:T(1024)} %pad_maximum_fusion.16), channel_id=1, source_target_pairs={{0,4},{4,8},{8,12},{12,16},{16,20},{20,24},{24,28},{28,32},{32,36}... | collective-permute-start | bytes 49160 | tf_op jit(solution)/shard_map/ppermute | solution.py:88
  7.0 42.2 %collective-permute-start = (f32[4096]{0:T(1024)}, f32[4096]{0:T(1024)}, u32[]{:S(2)}, u32[]{:S(2)}) collective-permute-start(f32[4096]{0:T(1024)} %pad_maximum_fusion.15), channel_id=1, source_target_pairs={{4,0},{8,4},{12,8},{16,12},{20,16},{24,20},{28,24},{32,28},{36,32}... | collective-permute-start | bytes 49160 | tf_op jit(solution)/shard_map/ppermute | solution.py:89
  16.2 29.1 %collective-permute-start.3 = (f32[2096]{0:T(1024)}, f32[2096]{0:T(1024)}, u32[]{:S(2)}, u32[]{:S(2)}) collective-permute-start(f32[2096]{0:T(1024)} %maximum_select_fusion.1), channel_id=1, source_target_pairs={{0,1},{1,0},{2,3},{3,2},{4,5},{5,4},{6,7},{7,6},{8,9},{9,8},{10,11... | collective-permute-start | bytes 25160 | tf_op jit(solution)/shard_map/ppermute | solution.py:85
  28.5 24.7 %collective-permute-start.2 = (f32[8960]{0:T(1024)}, f32[8960]{0:T(1024)}, u32[]{:S(2)}, u32[]{:S(2)}) collective-permute-start(f32[8960]{0:T(1024)} %maximum_select_fusion), channel_id=1, source_target_pairs={{0,2},{2,0},{1,3},{3,1},{4,6},{6,4},{5,7},{7,5},{8,10},{10,8},{9,1... | collective-permute-start | bytes 107528 | tf_op jit(solution)/shard_map/ppermute | solution.py:85
  31.1 18.8 %copy-start.3 = (f32[3,1,8,128]{3,2,1,0:T(8,128)}, f32[3,1,8,128]{3,2,1,0:T(8,128)S(1)}, u32[]{:S(2)}) copy-start(f32[3,1,8,128]{3,2,1,0:T(8,128)S(1)} %get-tuple-element.193) | copy-start | bytes 36868
  54.0 12.3 %copy-start.2 = (f32[4,4,512]{2,1,0:T(4,128)}, f32[4,4,512]{2,1,0:T(4,128)S(1)}, u32[]{:S(2)}) copy-start(f32[4,4,512]{2,1,0:T(4,128)S(1)} %reshape.5995) | copy-start | bytes 98308
  66.3 15.1 %copy-start.31 = (f32[2048]{0:T(1024)S(1)}, f32[2048]{0:T(1024)}, u32[]{:S(2)}) copy-start(f32[2048]{0:T(1024)} %copy-done.30) | copy-start | bytes 24580
  66.3 15.1 %slice-start = ((f32[4,4,512]{2,1,0:T(4,128)}), f32[4,4,56]{2,1,0:T(4,128)S(1)}, s32[]{:S(2)}) async-start(f32[4,4,512]{2,1,0:T(4,128)} %copy-done.2), calls=%async_computation.1 | async-start | bytes 16384 | tf_op jit(solution)/shard_map/jit(_roll_static)/slice | solution.py:196
  69.2 24.9 %all-to-all-start = ((f32[4,128,24]{2,0,1:T(4,128)}), f32[4,128,24]{2,0,1:T(4,128)S(1)}, u32[]{:S(2)}, u32[]{:S(2)}) async-start(f32[4,128,24]{2,0,1:T(4,128)} %copy.323), calls=%async_computation | async-start | bytes 524288 | tf_op jit(solution)/shard_map/all_to_all | solution.py:258
  82.4 18.0 %copy-start.87 = (f32[8,16]{1,0:T(8,128)S(1)}, f32[8,16]{1,0:T(8,128)}, u32[]{:S(2)}) copy-start(f32[8,16]{1,0:T(8,128)} %constant.275.clone) | copy-start | bytes 1540
  83.0 22.0 %copy-start.8 = (f32[1,4,512]{2,1,0:T(4,128)}, f32[1,4,512]{2,1,0:T(4,128)S(1)}, u32[]{:S(2)}) copy-start(f32[1,4,512]{2,1,0:T(4,128)S(1)} %get-tuple-element.222) | copy-start | bytes 24580
  83.1 22.0 %copy-start.10 = (f32[1,4,512]{2,1,0:T(4,128)}, f32[1,4,512]{2,1,0:T(4,128)S(1)}, u32[]{:S(2)}) copy-start(f32[1,4,512]{2,1,0:T(4,128)S(1)} %get-tuple-element.223) | copy-start | bytes 24580
  84.4 20.7 %copy-start.12 = (f32[1,4,512]{2,1,0:T(4,128)}, f32[1,4,512]{2,1,0:T(4,128)S(1)}, u32[]{:S(2)}) copy-start(f32[1,4,512]{2,1,0:T(4,128)S(1)} %get-tuple-element.154) | copy-start | bytes 24580
  84.4 20.7 %copy-start.14 = (f32[1,4,512]{2,1,0:T(4,128)}, f32[1,4,512]{2,1,0:T(4,128)S(1)}, u32[]{:S(2)}) copy-start(f32[1,4,512]{2,1,0:T(4,128)S(1)} %get-tuple-element.155) | copy-start | bytes 24580
  105.4 3.1 %collective-permute-start.6 = (f32[8192]{0:T(1024)S(1)}, f32[8192]{0:T(1024)S(1)}, u32[]{:S(2)}, u32[]{:S(2)}) collective-permute-start(f32[8192]{0:T(1024)S(1)} %add.707), channel_id=1, source_target_pairs={{0,2},{2,0},{1,3},{3,1},{4,6},{6,4},{5,7},{7,5},{8,10},{10,8},{9,1... | collective-permute-start | bytes 98312 | tf_op jit(solution)/shard_map/ppermute | solution.py:85
  111.1 14.8 %copy-start.46 = (f32[4,4,512]{2,1,0:T(4,128)S(1)}, f32[4,4,512]{2,1,0:T(4,128)}, u32[]{:S(2)}) copy-start(f32[4,4,512]{2,1,0:T(4,128)} %get-tuple-element.33) | copy-start | bytes 98308
  114.3 21.2 %collective-permute-start.7 = (f32[2048]{0:T(1024)}, f32[2048]{0:T(1024)}, u32[]{:S(2)}, u32[]{:S(2)}) collective-permute-start(f32[2048]{0:T(1024)} %bitcast.123), channel_id=1, source_target_pairs={{0,1},{1,0},{2,3},{3,2},{4,5},{5,4},{6,7},{7,6},{8,9},{9,8},{10,11... | collective-permute-start | bytes 24584 | tf_op jit(solution)/shard_map/ppermute | solution.py:85
  117.6 9.2 %collective-permute-start.5 = (f32[1024]{0:T(1024)}, f32[1024]{0:T(1024)}, u32[]{:S(2)}, u32[]{:S(2)}) collective-permute-start(f32[1024]{0:T(1024)} %reshape.6001), channel_id=1, source_target_pairs={{4,0},{8,4},{12,8},{16,12},{20,16},{24,20},{28,24},{32,28},{36,32}... | collective-permute-start | bytes 12296 | tf_op jit(solution)/shard_map/ppermute | solution.py:89
  124.1 10.0 %collective-permute-start.4 = (f32[1024]{0:T(1024)}, f32[1024]{0:T(1024)}, u32[]{:S(2)}, u32[]{:S(2)}) collective-permute-start(f32[1024]{0:T(1024)} %reshape.5999), channel_id=1, source_target_pairs={{0,4},{4,8},{8,12},{12,16},{16,20},{20,24},{24,28},{28,32},{32,36}... | collective-permute-start | bytes 12296 | tf_op jit(solution)/shard_map/ppermute | solution.py:88
  137.7 9.7 %copy-start.32 = (f32[1,4,512]{2,1,0:T(4,128)}, f32[1,4,512]{2,1,0:T(4,128)S(1)}, u32[]{:S(2)}) copy-start(f32[1,4,512]{2,1,0:T(4,128)S(1)} %get-tuple-element.79) | copy-start | bytes 24580
  141.1 3.1 %collective-permute-start.10 = (f32[8192]{0:T(1024)S(1)}, f32[8192]{0:T(1024)S(1)}, u32[]{:S(2)}, u32[]{:S(2)}) collective-permute-start(f32[8192]{0:T(1024)S(1)} %multiply_add_fusion), channel_id=1, source_target_pairs={{0,2},{2,0},{1,3},{3,1},{4,6},{6,4},{5,7},{7,5},{8,10},{10,8},{9,1... | collective-permute-start | bytes 98312 | tf_op jit(solution)/shard_map/ppermute | solution.py:85
  148.6 15.5 %copy-start.47 = (f32[4,4,512]{2,1,0:T(4,128)S(1)}, f32[4,4,512]{2,1,0:T(4,128)}, u32[]{:S(2)}) copy-start(f32[4,4,512]{2,1,0:T(4,128)} %get-tuple-element.20) | copy-start | bytes 98308
  149.4 21.0 %copy-start.9 = (f32[1,4,512]{2,1,0:T(4,128)S(1)}, f32[1,4,512]{2,1,0:T(4,128)}, u32[]{:S(2)}) copy-start(f32[1,4,512]{2,1,0:T(4,128)} %copy-done.8) | copy-start | bytes 24580
  149.4 21.1 %copy-start.11 = (f32[1,4,512]{2,1,0:T(4,128)S(1)}, f32[1,4,512]{2,1,0:T(4,128)}, u32[]{:S(2)}) copy-start(f32[1,4,512]{2,1,0:T(4,128)} %copy-done.10) | copy-start | bytes 24580
  149.4 21.1 %copy-start.13 = (f32[1,4,512]{2,1,0:T(4,128)S(1)}, f32[1,4,512]{2,1,0:T(4,128)}, u32[]{:S(2)}) copy-start(f32[1,4,512]{2,1,0:T(4,128)} %copy-done.12) | copy-start | bytes 24580
  149.4 21.1 %copy-start.15 = (f32[1,4,512]{2,1,0:T(4,128)S(1)}, f32[1,4,512]{2,1,0:T(4,128)}, u32[]{:S(2)}) copy-start(f32[1,4,512]{2,1,0:T(4,128)} %copy-done.14) | copy-start | bytes 24580
  149.4 21.1 %copy-start.17 = (f32[1,4,512]{2,1,0:T(4,128)S(1)}, f32[1,4,512]{2,1,0:T(4,128)}, u32[]{:S(2)}) copy-start(f32[1,4,512]{2,1,0:T(4,128)} %get-tuple-element.226) | copy-start | bytes 24580
  149.4 21.1 %copy-start.19 = (f32[1,4,512]{2,1,0:T(4,128)S(1)}, f32[1,4,512]{2,1,0:T(4,128)}, u32[]{:S(2)}) copy-start(f32[1,4,512]{2,1,0:T(4,128)} %get-tuple-element.227) | copy-start | bytes 24580
  149.4 21.1 %copy-start.21 = (f32[1,4,512]{2,1,0:T(4,128)S(1)}, f32[1,4,512]{2,1,0:T(4,128)}, u32[]{:S(2)}) copy-start(f32[1,4,512]{2,1,0:T(4,128)} %get-tuple-element.80) | copy-start | bytes 24580
  149.4 21.1 %copy-start.23 = (f32[1,4,512]{2,1,0:T(4,128)S(1)}, f32[1,4,512]{2,1,0:T(4,128)}, u32[]{:S(2)}) copy-start(f32[1,4,512]{2,1,0:T(4,128)} %get-tuple-element.81) | copy-start | bytes 24580
  149.4 21.1 %copy-start.25 = (f32[1,4,512]{2,1,0:T(4,128)S(1)}, f32[1,4,512]{2,1,0:T(4,128)}, u32[]{:S(2)}) copy-start(f32[1,4,512]{2,1,0:T(4,128)} %get-tuple-element.220) | copy-start | bytes 24580
  149.4 21.1 %copy-start.27 = (f32[1,4,512]{2,1,0:T(4,128)S(1)}, f32[1,4,512]{2,1,0:T(4,128)}, u32[]{:S(2)}) copy-start(f32[1,4,512]{2,1,0:T(4,128)} %get-tuple-element.221) | copy-start | bytes 24580
  149.4 21.1 %copy-start.28 = (f32[1,4,512]{2,1,0:T(4,128)S(1)}, f32[1,4,512]{2,1,0:T(4,128)}, u32[]{:S(2)}) copy-start(f32[1,4,512]{2,1,0:T(4,128)} %get-tuple-element.120) | copy-start | bytes 24580
  149.4 21.1 %copy-start.29 = (f32[1,4,512]{2,1,0:T(4,128)S(1)}, f32[1,4,512]{2,1,0:T(4,128)}, u32[]{:S(2)}) copy-start(f32[1,4,512]{2,1,0:T(4,128)} %get-tuple-element.121) | copy-start | bytes 24580
  149.4 21.1 %copy-start.33 = (f32[1,4,512]{2,1,0:T(4,128)S(1)}, f32[1,4,512]{2,1,0:T(4,128)}, u32[]{:S(2)}) copy-start(f32[1,4,512]{2,1,0:T(4,128)} %copy-done.32) | copy-start | bytes 24580
  149.5 21.1 %copy-start.35 = (f32[1,4,512]{2,1,0:T(4,128)S(1)}, f32[1,4,512]{2,1,0:T(4,128)}, u32[]{:S(2)}) copy-start(f32[1,4,512]{2,1,0:T(4,128)} %copy-done.34) | copy-start | bytes 24580
  149.5 21.1 %copy-start.37 = (f32[1,4,512]{2,1,0:T(4,128)S(1)}, f32[1,4,512]{2,1,0:T(4,128)}, u32[]{:S(2)}) copy-start(f32[1,4,512]{2,1,0:T(4,128)} %copy-done.36) | copy-start | bytes 24580
  149.5 21.1 %copy-start.39 = (f32[1,4,512]{2,1,0:T(4,128)S(1)}, f32[1,4,512]{2,1,0:T(4,128)}, u32[]{:S(2)}) copy-start(f32[1,4,512]{2,1,0:T(4,128)} %copy-done.38) | copy-start | bytes 24580
  149.5 21.1 %copy-start.41 = (f32[1,4,512]{2,1,0:T(4,128)S(1)}, f32[1,4,512]{2,1,0:T(4,128)}, u32[]{:S(2)}) copy-start(f32[1,4,512]{2,1,0:T(4,128)} %copy-done.40) | copy-start | bytes 24580
  149.5 21.1 %copy-start.43 = (f32[1,4,512]{2,1,0:T(4,128)S(1)}, f32[1,4,512]{2,1,0:T(4,128)}, u32[]{:S(2)}) copy-start(f32[1,4,512]{2,1,0:T(4,128)} %copy-done.42) | copy-start | bytes 24580
  149.5 21.1 %copy-start.45 = (f32[1,4,512]{2,1,0:T(4,128)S(1)}, f32[1,4,512]{2,1,0:T(4,128)}, u32[]{:S(2)}) copy-start(f32[1,4,512]{2,1,0:T(4,128)} %copy-done.44) | copy-start | bytes 24580
  149.5 21.1 %copy-start.48 = (f32[2,1,1,4,512]{4,3,0,2,1:T(4,128)S(1)}, f32[2,1,1,4,512]{4,3,0,2,1:T(4,128)}, u32[]{:S(2)}) copy-start(f32[2,1,1,4,512]{4,3,0,2,1:T(4,128)} %get-tuple-element.131) | copy-start | bytes 49156
  149.5 21.1 %copy-start.49 = (f32[2,1,1,4,512]{4,3,0,2,1:T(4,128)S(1)}, f32[2,1,1,4,512]{4,3,0,2,1:T(4,128)}, u32[]{:S(2)}) copy-start(f32[2,1,1,4,512]{4,3,0,2,1:T(4,128)} %get-tuple-element.129) | copy-start | bytes 49156
  149.5 21.1 %copy-start.50 = (f32[2,1,1,4,512]{4,3,0,2,1:T(4,128)S(1)}, f32[2,1,1,4,512]{4,3,0,2,1:T(4,128)}, u32[]{:S(2)}) copy-start(f32[2,1,1,4,512]{4,3,0,2,1:T(4,128)} %get-tuple-element.115) | copy-start | bytes 49156
  149.5 21.1 %copy-start.51 = (f32[2,1,1,4,512]{4,3,0,2,1:T(4,128)S(1)}, f32[2,1,1,4,512]{4,3,0,2,1:T(4,128)}, u32[]{:S(2)}) copy-start(f32[2,1,1,4,512]{4,3,0,2,1:T(4,128)} %get-tuple-element.113) | copy-start | bytes 49156
  149.6 21.1 %copy-start.52 = (f32[2,1,1,4,512]{4,3,0,2,1:T(4,128)S(1)}, f32[2,1,1,4,512]{4,3,0,2,1:T(4,128)}, u32[]{:S(2)}) copy-start(f32[2,1,1,4,512]{4,3,0,2,1:T(4,128)} %get-tuple-element.163) | copy-start | bytes 49156
  149.6 21.1 %copy-start.53 = (f32[2,1,1,4,512]{4,3,0,2,1:T(4,128)S(1)}, f32[2,1,1,4,512]{4,3,0,2,1:T(4,128)}, u32[]{:S(2)}) copy-start(f32[2,1,1,4,512]{4,3,0,2,1:T(4,128)} %get-tuple-element.232) | copy-start | bytes 49156
  149.6 21.1 %copy-start.54 = (f32[2,1,1,4,512]{4,3,0,2,1:T(4,128)S(1)}, f32[2,1,1,4,512]{4,3,0,2,1:T(4,128)}, u32[]{:S(2)}) copy-start(f32[2,1,1,4,512]{4,3,0,2,1:T(4,128)} %get-tuple-element.147) | copy-start | bytes 49156
  149.6 21.1 %copy-start.55 = (f32[2,1,1,4,512]{4,3,0,2,1:T(4,128)S(1)}, f32[2,1,1,4,512]{4,3,0,2,1:T(4,128)}, u32[]{:S(2)}) copy-start(f32[2,1,1,4,512]{4,3,0,2,1:T(4,128)} %get-tuple-element.224) | copy-start | bytes 49156
  149.6 21.1 %copy-start.60 = (f32[1,1,1,4,512]{4,3,2,1,0:T(4,128)S(1)}, f32[1,1,1,4,512]{4,3,2,1,0:T(4,128)}, u32[]{:S(2)}) copy-start(f32[1,1,1,4,512]{4,3,2,1,0:T(4,128)} %fusion) | copy-start | bytes 24580
  149.6 21.1 %copy-start.61 = (f32[1,1,1,4,512]{4,3,2,1,0:T(4,128)S(1)}, f32[1,1,1,4,512]{4,3,2,1,0:T(4,128)}, u32[]{:S(2)}) copy-start(f32[1,1,1,4,512]{4,3,2,1,0:T(4,128)} %fusion.1) | copy-start | bytes 24580
  149.6 21.1 %copy-start.62 = (f32[1,1,1,4,512]{4,3,2,1,0:T(4,128)S(1)}, f32[1,1,1,4,512]{4,3,2,1,0:T(4,128)}, u32[]{:S(2)}) copy-start(f32[1,1,1,4,512]{4,3,2,1,0:T(4,128)} %fusion.2) | copy-start | bytes 24580
  149.6 21.1 %copy-start.63 = (f32[1,1,1,4,512]{4,3,2,1,0:T(4,128)S(1)}, f32[1,1,1,4,512]{4,3,2,1,0:T(4,128)}, u32[]{:S(2)}) copy-start(f32[1,1,1,4,512]{4,3,2,1,0:T(4,128)} %get-tuple-element.151) | copy-start | bytes 24580
  149.6 21.1 %copy-start.64 = (f32[1,1,1,4,512]{4,3,2,1,0:T(4,128)S(1)}, f32[1,1,1,4,512]{4,3,2,1,0:T(4,128)}, u32[]{:S(2)}) copy-start(f32[1,1,1,4,512]{4,3,2,1,0:T(4,128)} %get-tuple-element.152) | copy-start | bytes 24580
  149.6 21.1 %copy-start.65 = (f32[1,1,1,4,512]{4,3,2,1,0:T(4,128)S(1)}, f32[1,1,1,4,512]{4,3,2,1,0:T(4,128)}, u32[]{:S(2)}) copy-start(f32[1,1,1,4,512]{4,3,2,1,0:T(4,128)} %get-tuple-element.229) | copy-start | bytes 24580
  149.7 21.1 %copy-start.66 = (f32[1,1,1,4,512]{4,3,2,1,0:T(4,128)S(1)}, f32[1,1,1,4,512]{4,3,2,1,0:T(4,128)}, u32[]{:S(2)}) copy-start(f32[1,1,1,4,512]{4,3,2,1,0:T(4,128)} %get-tuple-element.230) | copy-start | bytes 24580
  149.7 21.1 %copy-start.67 = (f32[1,1,1,4,512]{4,3,0,2,1:T(4,128)S(1)}, f32[1,1,1,4,512]{4,3,0,2,1:T(4,128)}, u32[]{:S(2)}) copy-start(f32[1,1,1,4,512]{4,3,0,2,1:T(4,128)} %get-tuple-element.117) | copy-start | bytes 24580
  149.7 21.1 %copy-start.68 = (f32[1,1,1,4,512]{4,3,0,2,1:T(4,128)S(1)}, f32[1,1,1,4,512]{4,3,0,2,1:T(4,128)}, u32[]{:S(2)}) copy-start(f32[1,1,1,4,512]{4,3,0,2,1:T(4,128)} %get-tuple-element.118) | copy-start | bytes 24580
  149.7 21.1 %copy-start.69 = (f32[1,1,1,4,512]{4,3,0,2,1:T(4,128)S(1)}, f32[1,1,1,4,512]{4,3,0,2,1:T(4,128)}, u32[]{:S(2)}) copy-start(f32[1,1,1,4,512]{4,3,0,2,1:T(4,128)} %get-tuple-element.123) | copy-start | bytes 24580
  149.7 21.1 %copy-start.70 = (f32[1,1,1,4,512]{4,3,0,2,1:T(4,128)S(1)}, f32[1,1,1,4,512]{4,3,0,2,1:T(4,128)}, u32[]{:S(2)}) copy-start(f32[1,1,1,4,512]{4,3,0,2,1:T(4,128)} %get-tuple-element.124) | copy-start | bytes 24580
  149.7 21.1 %copy-start.81 = (pred[512]{0:T(512)(128)(4,1)S(1)}, pred[512]{0:T(512)(128)(4,1)}, u32[]{:S(2)}) copy-start(pred[512]{0:T(512)(128)(4,1)} %get-tuple-element.236) | copy-start | bytes 1540
  150.3 19.7 %collective-permute-start.11 = (f32[2048]{0:T(1024)S(1)}, f32[2048]{0:T(1024)S(1)}, u32[]{:S(2)}, u32[]{:S(2)}) collective-permute-start(f32[2048]{0:T(1024)S(1)} %bitcast.662), channel_id=1, source_target_pairs={{0,1},{1,0},{2,3},{3,2},{4,5},{5,4},{6,7},{7,6},{8,9},{9,8},{10,11... | collective-permute-start | bytes 24584 | tf_op jit(solution)/shard_map/ppermute | solution.py:85
  158.2 6.7 %collective-permute-start.9 = (f32[1024]{0:T(1024)S(1)}, f32[1024]{0:T(1024)S(1)}, u32[]{:S(2)}, u32[]{:S(2)}) collective-permute-start(f32[1024]{0:T(1024)S(1)} %reshape.6009), channel_id=1, source_target_pairs={{4,0},{8,4},{12,8},{16,12},{20,16},{24,20},{28,24},{32,28},{36,32}... | collective-permute-start | bytes 12296 | tf_op jit(solution)/shard_map/ppermute | solution.py:89
  160.2 9.7 %collective-permute-start.8 = (f32[1024]{0:T(1024)S(1)}, f32[1024]{0:T(1024)S(1)}, u32[]{:S(2)}, u32[]{:S(2)}) collective-permute-start(f32[1024]{0:T(1024)S(1)} %reshape.6007), channel_id=1, source_target_pairs={{0,4},{4,8},{8,12},{12,16},{16,20},{20,24},{24,28},{28,32},{32,36}... | collective-permute-start | bytes 12296 | tf_op jit(solution)/shard_map/ppermute | solution.py:88
  (40 other events, 104.4 us)

commit v2 on v0

--- a/solution.py
+++ b/solution.py
@@ -3,6 +3,7 @@
 import numpy as np
 from jax import lax
 from jax.sharding import PartitionSpec as P
+
 
 SUB = 16
 NODES = 512
@@ -147,12 +148,12 @@
 
     face = 64
     below_x, above_x = neighbours(fields[..., :face], fields[..., NODES - face :], "gx")
+    below_y, above_y = neighbours(fields, fields, "gy")
+    below_z, above_z = neighbours(fields[:, :1], fields[:, count - 1 :], "gz")
     outer_lower_x = jnp.pad(below_x, ((0, 0), (0, 0), (0, NODES - face)))
     outer_upper_x = jnp.pad(above_x, ((0, 0), (0, 0), (NODES - face, 0)))
-    below_y, above_y = neighbours(fields, fields, "gy")
     outer_lower_y = jnp.roll(below_y, -56, axis=2)
     outer_upper_y = jnp.roll(above_y, 56, axis=2)
-    below_z, above_z = neighbours(fields[:, :1], fields[:, count - 1 :], "gz")
     outer_lower_z = jnp.roll(jnp.concatenate([below_z, fields[:, :-1]], axis=1), -7, axis=2)
     outer_upper_z = jnp.roll(jnp.concatenate([fields[:, 1:], above_z], axis=1), 7, axis=2)
 
@@ -175,7 +176,7 @@
 def runge_kutta(fields, forcing):
     tables = kron_tables()
     step = lambda f: tendency(f, forcing, tables)
-    section_one = fields + TIME_STEP * step(fields)
+    section_one = fields + TIME_STEP * tendency(fields, forcing, tables)
     section_two = 0.75 * fields + 0.25 * (section_one + TIME_STEP * step(section_one))
     return 1.0 / 3.0 * fields + 2.0 / 3.0 * (section_two + TIME_STEP * step(section_two))
 
@@ -186,7 +187,7 @@
     return jnp.sum(chosen, axis=1)
 
 
-def on_device(velocity, eddy_viscosity, cell_owner, cell_element, cell_position, acoustic_state):
+def on_device_body(velocity, eddy_viscosity, cell_owner, cell_element, cell_position, acoustic_state):
     sources = source_cells(velocity, eddy_viscosity)
     cell_count = sources.shape[1] * sources.shape[2] * sources.shape[3]
     flat_source = sources.reshape(3, cell_count).astype(jnp.float32)
@@ -257,5 +258,5 @@
     )
     out_specs = (P("gx", "gy", "gz", None, None), P(None, "gx", "gy", "gz", None))
     return jax.shard_map(
-        on_device, mesh=mesh, in_specs=in_specs, out_specs=out_specs, check_vma=False
-    )
+        on_device_body, mesh=mesh, in_specs=in_specs, out_specs=out_specs, check_vma=False
+    )

time: 148 us -> 148 us (level)
  no operation moved by 1% of the time
where the time goes in v2:
time: 148 us; the launch traced here: 146 us
  starting transfers between devices  70.5 us (48%)
  local copies, waits for them, and re-layouts  21.8 us (15%)
  waiting for transfers between devices  21 us (14%)
  other arithmetic  19 us (13%)
  matrix products  12.1 us (8%)
  between operations  1.85 us (1%)
    ppermute x8, starting transfers between devices, neighbours(): got = lax.ppermute(sent, axis, [(0, 1), (1, 0)])  30 us
    ppermute x4, starting transfers between devices, neighbours(): lax.ppermute(lower, axis, [(i + 1, i) for i in range(count - 1)])  21 us
    ppermute x4, waiting for transfers between devices, neighbours(): lax.ppermute(upper, axis, [(i, i + 1) for i in range(count - 1)])  12.1 us
    ppermute x4, starting transfers between devices, neighbours(): lax.ppermute(upper, axis, [(i, i + 1) for i in range(count - 1)])  11.2 us
    all_to_all x1, starting transfers between devices, on_device_body(): got = lax.all_to_all(send, 'gx', split_axis=0, concat_axis=0, tiled=True)  8.27 us
    all_to_all x1, waiting for transfers between devices, on_device_body(): got = lax.all_to_all(send, 'gx', split_axis=0, concat_axis=0, tiled=True)  7.96 us
    scatter x1, local copies, waits for them, and re-layouts, on_device_body(): send = jnp.zeros((4, owner_count * capacity), jnp.float32).at[:, slot_ind...  7.15 us
    dot_general x9, matrix products, tendency(): grads = [jnp.dot(fields[0], table, precision=highest) for table in tables]  5.61 us
  transfers between devices with their start and end apart: 17, of which 4 were waited for; matrix products, arithmetic and copies ran while one was open for 26% of the time, Pallas kernels for 0%

profile of v2, /device:TPU:64, one launch (start us, length us, event | category | flops | bytes accessed | tf_op | source)
XLA Modules:
  0.0 146.3 jit_solution(7517484868772382151)
XLA Ops:
  0.6 1.3 fusion.211
  1.9 3.5 %collective-permute-start.1 = (bf16[3,1,8,128]{3,2,1,0:T(8,128)(2,1)}, bf16[3,1,8,128]{3,2,1,0:T(8,128)(2,1)}, u32[]{:S(2)}, u32[]{:S(2)}) collective-permute-start(bf16[3,1,8,128]{3,2,1,0:T(8,128)(2,1)} %get-tuple-element.191), channel_id=1, source_target_pairs={{0,4},{4,8},{8,12},{12,16},{16,20},{20,24},{24,28},{28,32},{32,36}... | collective-permute-start | bytes 18440 | tf_op jit(solution)/shard_map/ppermute | solution.py:89
  5.4 6.6 %collective-permute-start = (bf16[3,1,8,128]{3,2,1,0:T(8,128)(2,1)}, bf16[3,1,8,128]{3,2,1,0:T(8,128)(2,1)}, u32[]{:S(2)}, u32[]{:S(2)}) collective-permute-start(bf16[3,1,8,128]{3,2,1,0:T(8,128)(2,1)} %get-tuple-element.190), channel_id=1, source_target_pairs={{4,0},{8,4},{12,8},{16,12},{20,16},{24,20},{28,24},{32,28},{36,32}... | collective-permute-start | bytes 18440 | tf_op jit(solution)/shard_map/ppermute | solution.py:90
  12.0 1.4 broadcast_select_fusion.18
  13.4 1.9 %collective-permute-start.2 = (bf16[3,2,1,128]{3,2,1,0:T(2,128)(2,1)}, bf16[3,2,1,128]{3,2,1,0:T(2,128)(2,1)}, u32[]{:S(2)}, u32[]{:S(2)}) collective-permute-start(bf16[3,2,1,128]{3,2,1,0:T(2,128)(2,1)} %broadcast_select_fusion.18), channel_id=1, source_target_pairs={{0,2},{2,0},{1,3},{3,1},{4,6},{6,4},{5,7},{7,5},{8,10},{10,8},{9,1... | collective-permute-start | bytes 4616 | tf_op jit(solution)/shard_map/ppermute | solution.py:86
  15.3 1.5 slice_select_fusion
  16.8 10.0 %collective-permute-start.3 = (bf16[3,2,8,1]{3,2,1,0:T(8,128)(2,1)}, bf16[3,2,8,1]{3,2,1,0:T(8,128)(2,1)}, u32[]{:S(2)}, u32[]{:S(2)}) collective-permute-start(bf16[3,2,8,1]{3,2,1,0:T(8,128)(2,1)} %slice_select_fusion), channel_id=1, source_target_pairs={{0,1},{1,0},{2,3},{3,2},{4,5},{5,4},{6,7},{7,6},{8,9},{9,8},{10,11... | collective-permute-start | bytes 296 | tf_op jit(solution)/shard_map/ppermute | solution.py:86
  26.8 2.1 %collective-permute-start.6 = (f32[4,4,512]{2,1,0:T(4,128)}, f32[4,4,512]{2,1,0:T(4,128)}, u32[]{:S(2)}, u32[]{:S(2)}) collective-permute-start(f32[4,4,512]{2,1,0:T(4,128)} %bitcast.531), channel_id=1, source_target_pairs={{0,2},{2,0},{1,3},{3,1},{4,6},{6,4},{5,7},{7,5},{8,10},{10,8},{9,1... | collective-permute-start | bytes 98312 | tf_op jit(solution)/shard_map/ppermute | solution.py:86
  28.9 0.7 convert_element_type.100
  29.6 0.7 fusion.210
  30.4 0.8 fusion.208
  31.1 0.9 fusion.209
  32.2 1.4 broadcast_select_fusion.12
  33.6 0.8 fusion.206
  34.5 1.4 fusion.207
  37.5 0.8 copy.218
  39.5 0.6 fusion.14
  40.2 0.6 compare_select_fusion
  41.8 1.2 and_select_fusion.2
  43.0 0.6 fusion.155
  43.7 0.6 convolution_add_fusion.5
  44.4 0.7 fusion.9
  45.1 2.2 %collective-permute-start.7 = (f32[4,1,512]{2,1,0:T(1,128)S(1)}, f32[4,1,512]{2,1,0:T(1,128)S(1)}, u32[]{:S(2)}, u32[]{:S(2)}) collective-permute-start(f32[4,1,512]{2,1,0:T(1,128)S(1)} %copy-done.22), channel_id=1, source_target_pairs={{0,1},{1,0},{2,3},{3,2},{4,5},{5,4},{6,7},{7,6},{8,9},{9,8},{10,11... | collective-permute-start | bytes 24584 | tf_op jit(solution)/shard_map/ppermute | solution.py:86
  47.3 0.7 select_convert_fusion.1
  48.0 1.9 %collective-permute-start.4 = (f32[4,4,64]{2,1,0:T(4,128)S(1)}, f32[4,4,64]{2,1,0:T(4,128)S(1)}, u32[]{:S(2)}, u32[]{:S(2)}) collective-permute-start(f32[4,4,64]{2,1,0:T(4,128)S(1)} %copy-done.24), channel_id=1, source_target_pairs={{0,4},{4,8},{8,12},{12,16},{16,20},{20,24},{24,28},{28,32},{32,36}... | collective-permute-start | bytes 12296 | tf_op jit(solution)/shard_map/ppermute | solution.py:89
  49.9 0.7 fusion.169
  50.7 8.1 %collective-permute-start.5 = (f32[4,4,64]{2,1,0:T(4,128)S(1)}, f32[4,4,64]{2,1,0:T(4,128)S(1)}, u32[]{:S(2)}, u32[]{:S(2)}) collective-permute-start(f32[4,4,64]{2,1,0:T(4,128)S(1)} %copy-done.23), channel_id=1, source_target_pairs={{4,0},{8,4},{12,8},{16,12},{20,16},{24,20},{28,24},{32,28},{36,32}... | collective-permute-start | bytes 12296 | tf_op jit(solution)/shard_map/ppermute | solution.py:90
  58.9 0.7 convert_element_type.102
  59.6 0.7 convert_element_type.101
  60.5 1.4 copy.220
  61.8 7.1 %scatter_custom_fusion = f32[4,3072]{0,1:T(8,128)} fusion(s32[2048]{0:T(1024)} %bitcast.586, f32[2048,4]{1,0:T(8,128)} %copy.220, f32[]{:T(128)} %constant.243.clone.1), kind=kCustom, calls=%fused_computation.56 | custom fusion | bytes 49664 | tf_op jit(solution)/shard_map/scatter | solution.py:211
  69.0 1.9 %copy.221 = f32[4,128,24]{1,2,0:T(8,128)S(1)} copy(f32[4,128,24]{0,2,1:T(8,128)} %bitcast.530) | data formatting | bytes 98304 | tf_op jit(solution)/shard_map/reshape | solution.py:212
  70.9 0.7 copy.222
  71.6 8.3 %all-to-all-start = ((f32[128,1,96]{2,1,0:T(1,128)}), f32[128,1,96]{2,1,0:T(1,128)S(1)}, u32[]{:S(2)}, u32[]{:S(2)}) async-start(f32[128,1,96]{2,1,0:T(1,128)} %copy.222), calls=%async_computation | async-start | bytes 131072 | tf_op jit(solution)/shard_map/all_to_all | solution.py:215
  80.0 0.8 broadcast_select_fusion.5
  81.1 0.6 fusion.204
  81.8 0.6 fusion.200
  82.4 0.6 fusion.202
  83.1 8.0 %all-to-all-done = f32[128,1,96]{2,1,0:T(1,128)S(1)} async-done(((f32[128,1,96]{2,1,0:T(1,128)}), f32[128,1,96]{2,1,0:T(1,128)S(1)}, u32[]{:S(2)}, u32[]{:S(2)}) %all-to-all-start) | async-done | bytes 49184 | tf_op jit(solution)/shard_map/all_to_all | solution.py:215
  91.9 0.9 select_reduce_fusion.2
  93.4 0.9 convolution_multiply_fusion
  94.4 0.6 reshape.5660
  95.1 0.7 fusion.6
  95.8 0.7 fusion.7
  96.4 0.7 fusion.8
  97.9 0.6 convolution_subtract_fusion.4
  98.5 0.6 convolution_subtract_fusion.5
  99.1 0.6 fusion.137
  99.8 1.9 %collective-permute-start.10 = (f32[4,4,512]{2,1,0:T(4,128)S(1)}, f32[4,4,512]{2,1,0:T(4,128)S(1)}, u32[]{:S(2)}, u32[]{:S(2)}) collective-permute-start(f32[4,4,512]{2,1,0:T(4,128)S(1)} %fusion.66), channel_id=1, source_target_pairs={{0,2},{2,0},{1,3},{3,1},{4,6},{6,4},{5,7},{7,5},{8,10},{10,8},{9,1... | collective-permute-start | bytes 98312 | tf_op jit(solution)/shard_map/ppermute | solution.py:86
  102.3 0.6 fusion.5
  102.9 7.5 %collective-permute-start.11 = (f32[4,1,512]{2,1,0:T(1,128)S(1)}, f32[4,1,512]{2,1,0:T(1,128)S(1)}, u32[]{:S(2)}, u32[]{:S(2)}) collective-permute-start(f32[4,1,512]{2,1,0:T(1,128)S(1)} %broadcast_select_fusion.10), channel_id=1, source_target_pairs={{0,1},{1,0},{2,3},{3,2},{4,5},{5,4},{6,7},{7,6},{8,9},{9,8},{10,11... | collective-permute-start | bytes 24584 | tf_op jit(solution)/shard_map/ppermute | solution.py:86
  110.6 4.4 %collective-permute-start.9 = (f32[4,4,64]{2,1,0:T(4,128)S(1)}, f32[4,4,64]{2,1,0:T(4,128)S(1)}, u32[]{:S(2)}, u32[]{:S(2)}) collective-permute-start(f32[4,4,64]{2,1,0:T(4,128)S(1)} %get-tuple-element.140), channel_id=1, source_target_pairs={{4,0},{8,4},{12,8},{16,12},{20,16},{24,20},{28,24},{32,28},{36,32}... | collective-permute-start | bytes 12296 | tf_op jit(solution)/shard_map/ppermute | solution.py:90
  115.0 1.9 %collective-permute-start.8 = (f32[4,4,64]{2,1,0:T(4,128)S(1)}, f32[4,4,64]{2,1,0:T(4,128)S(1)}, u32[]{:S(2)}, u32[]{:S(2)}) collective-permute-start(f32[4,4,64]{2,1,0:T(4,128)S(1)} %get-tuple-element.141), channel_id=1, source_target_pairs={{0,4},{4,8},{8,12},{12,16},{16,20},{20,24},{24,28},{28,32},{32,36}... | collective-permute-start | bytes 12296 | tf_op jit(solution)/shard_map/ppermute | solution.py:89
  117.3 7.5 %collective-permute-done.8 = f32[4,4,64]{2,1,0:T(4,128)S(1)} collective-permute-done((f32[4,4,64]{2,1,0:T(4,128)S(1)}, f32[4,4,64]{2,1,0:T(4,128)S(1)}, u32[]{:S(2)}, u32[]{:S(2)}) %collective-permute-start.8) | collective-permute-done | bytes 4128 | tf_op jit(solution)/shard_map/ppermute | solution.py:89
  125.8 0.6 fusion.1
  126.4 0.6 fusion.2
  127.0 0.6 fusion.124
  127.7 1.9 %collective-permute-start.14 = (f32[4,4,512]{2,1,0:T(4,128)S(1)}, f32[4,4,512]{2,1,0:T(4,128)S(1)}, u32[]{:S(2)}, u32[]{:S(2)}) collective-permute-start(f32[4,4,512]{2,1,0:T(4,128)S(1)} %fusion.78), channel_id=1, source_target_pairs={{0,2},{2,0},{1,3},{3,1},{4,6},{6,4},{5,7},{7,5},{8,10},{10,8},{9,1... | collective-permute-start | bytes 98312 | tf_op jit(solution)/shard_map/ppermute | solution.py:86
  130.3 2.3 %collective-permute-start.15 = (f32[4,1,512]{2,1,0:T(1,128)S(1)}, f32[4,1,512]{2,1,0:T(1,128)S(1)}, u32[]{:S(2)}, u32[]{:S(2)}) collective-permute-start(f32[4,1,512]{2,1,0:T(1,128)S(1)} %broadcast_select_fusion.8), channel_id=1, source_target_pairs={{0,1},{1,0},{2,3},{3,2},{4,5},{5,4},{6,7},{7,6},{8,9},{9,8},{10,11... | collective-permute-start | bytes 24584 | tf_op jit(solution)/shard_map/ppermute | solution.py:86
  133.3 1.9 %collective-permute-start.13 = (f32[4,4,64]{2,1,0:T(4,128)S(1)}, f32[4,4,64]{2,1,0:T(4,128)S(1)}, u32[]{:S(2)}, u32[]{:S(2)}) collective-permute-start(f32[4,4,64]{2,1,0:T(4,128)S(1)} %get-tuple-element.104), channel_id=1, source_target_pairs={{4,0},{8,4},{12,8},{16,12},{20,16},{24,20},{28,24},{32,28},{36,32}... | collective-permute-start | bytes 12296 | tf_op jit(solution)/shard_map/ppermute | solution.py:90
  135.2 3.9 %collective-permute-start.12 = (f32[4,4,64]{2,1,0:T(4,128)S(1)}, f32[4,4,64]{2,1,0:T(4,128)S(1)}, u32[]{:S(2)}, u32[]{:S(2)}) collective-permute-start(f32[4,4,64]{2,1,0:T(4,128)S(1)} %get-tuple-element.105), channel_id=1, source_target_pairs={{0,4},{4,8},{8,12},{12,16},{16,20},{20,24},{24,28},{28,32},{32,36}... | collective-permute-start | bytes 12296 | tf_op jit(solution)/shard_map/ppermute | solution.py:89
  139.1 0.9 collective-permute-done.15
  140.3 4.6 %collective-permute-done.12 = f32[4,4,64]{2,1,0:T(4,128)S(1)} collective-permute-done((f32[4,4,64]{2,1,0:T(4,128)S(1)}, f32[4,4,64]{2,1,0:T(4,128)S(1)}, u32[]{:S(2)}, u32[]{:S(2)}) %collective-permute-start.12) | collective-permute-done | bytes 4128 | tf_op jit(solution)/shard_map/ppermute | solution.py:89
  145.3 1.0 fusion.28
  (180 shorter events, 10.6 us)
Async XLA Ops:
  1.9 48.8 %collective-permute-start.1 = (bf16[3,1,8,128]{3,2,1,0:T(8,128)(2,1)}, bf16[3,1,8,128]{3,2,1,0:T(8,128)(2,1)}, u32[]{:S(2)}, u32[]{:S(2)}) collective-permute-start(bf16[3,1,8,128]{3,2,1,0:T(8,128)(2,1)} %get-tuple-element.191), channel_id=1, source_target_pairs={{0,4},{4,8},{8,12},{12,16},{16,20},{20,24},{24,28},{28,32},{32,36}... | collective-permute-start | bytes 18440 | tf_op jit(solution)/shard_map/ppermute | solution.py:89
  5.4 54.2 %collective-permute-start = (bf16[3,1,8,128]{3,2,1,0:T(8,128)(2,1)}, bf16[3,1,8,128]{3,2,1,0:T(8,128)(2,1)}, u32[]{:S(2)}, u32[]{:S(2)}) collective-permute-start(bf16[3,1,8,128]{3,2,1,0:T(8,128)(2,1)} %get-tuple-element.190), channel_id=1, source_target_pairs={{4,0},{8,4},{12,8},{16,12},{20,16},{24,20},{28,24},{32,28},{36,32}... | collective-permute-start | bytes 18440 | tf_op jit(solution)/shard_map/ppermute | solution.py:90
  13.4 34.6 %collective-permute-start.2 = (bf16[3,2,1,128]{3,2,1,0:T(2,128)(2,1)}, bf16[3,2,1,128]{3,2,1,0:T(2,128)(2,1)}, u32[]{:S(2)}, u32[]{:S(2)}) collective-permute-start(bf16[3,2,1,128]{3,2,1,0:T(2,128)(2,1)} %broadcast_select_fusion.18), channel_id=1, source_target_pairs={{0,2},{2,0},{1,3},{3,1},{4,6},{6,4},{5,7},{7,5},{8,10},{10,8},{9,1... | collective-permute-start | bytes 4616 | tf_op jit(solution)/shard_map/ppermute | solution.py:86
  16.8 28.3 %collective-permute-start.3 = (bf16[3,2,8,1]{3,2,1,0:T(8,128)(2,1)}, bf16[3,2,8,1]{3,2,1,0:T(8,128)(2,1)}, u32[]{:S(2)}, u32[]{:S(2)}) collective-permute-start(bf16[3,2,8,1]{3,2,1,0:T(8,128)(2,1)} %slice_select_fusion), channel_id=1, source_target_pairs={{0,1},{1,0},{2,3},{3,2},{4,5},{5,4},{6,7},{7,6},{8,9},{9,8},{10,11... | collective-permute-start | bytes 296 | tf_op jit(solution)/shard_map/ppermute | solution.py:86
  26.8 53.2 %collective-permute-start.6 = (f32[4,4,512]{2,1,0:T(4,128)}, f32[4,4,512]{2,1,0:T(4,128)}, u32[]{:S(2)}, u32[]{:S(2)}) collective-permute-start(f32[4,4,512]{2,1,0:T(4,128)} %bitcast.531), channel_id=1, source_target_pairs={{0,2},{2,0},{1,3},{3,1},{4,6},{6,4},{5,7},{7,5},{8,10},{10,8},{9,1... | collective-permute-start | bytes 98312 | tf_op jit(solution)/shard_map/ppermute | solution.py:86
  32.1 8.7 %copy-start.32 = (pred[512]{0:T(512)(128)(4,1)}, pred[512]{0:T(512)(128)(4,1)S(1)}, u32[]{:S(2)}) copy-start(pred[512]{0:T(512)(128)(4,1)S(1)} %get-tuple-element.211) | copy-start | bytes 1540
  32.1 9.1 %copy-start.33 = (pred[512]{0:T(512)(128)(4,1)}, pred[512]{0:T(512)(128)(4,1)S(1)}, u32[]{:S(2)}) copy-start(pred[512]{0:T(512)(128)(4,1)S(1)} %fusion.175) | copy-start | bytes 1540
  38.8 0.7 copy-start.2
  38.8 2.0 %copy-start.18 = (f32[8,512]{1,0:T(8,128)S(1)}, f32[8,512]{1,0:T(8,128)}, u32[]{:S(2)}) copy-start(f32[8,512]{1,0:T(8,128)} %constant.278.clone) | copy-start | bytes 49156
  39.2 2.1 %copy-start.17 = (f32[8,512]{1,0:T(8,128)S(1)}, f32[8,512]{1,0:T(8,128)}, u32[]{:S(2)}) copy-start(f32[8,512]{1,0:T(8,128)} %constant.277.clone) | copy-start | bytes 49156
  40.8 2.2 %copy-start.1 = (f32[4,1,1,4,512]{4,3,2,1,0:T(4,128)S(1)}, f32[4,1,1,4,512]{4,3,2,1,0:T(4,128)}, u32[]{:S(2)}) copy-start(f32[4,1,1,4,512]{4,3,2,1,0:T(4,128)} %param.15) | copy-start | bytes 98308
  41.3 2.4 %copy-start.19 = (s32[1,1,2048]{2,1,0:T(1,128)S(1)}, s32[1,1,2048]{2,1,0:T(1,128)}, u32[]{:S(2)}) copy-start(s32[1,1,2048]{2,1,0:T(1,128)} %param.14) | copy-start | bytes 24580
  41.3 2.4 %copy-start.20 = (s32[1,1,2048]{2,1,0:T(1,128)S(1)}, s32[1,1,2048]{2,1,0:T(1,128)}, u32[]{:S(2)}) copy-start(s32[1,1,2048]{2,1,0:T(1,128)} %param.13) | copy-start | bytes 24580
  43.0 2.1 %copy-start.22 = (f32[4,1,512]{2,1,0:T(1,128)S(1)}, f32[4,1,512]{2,1,0:T(1,128)}, u32[]{:S(2)}) copy-start(f32[4,1,512]{2,1,0:T(1,128)} %broadcast_select_fusion.12) | copy-start | bytes 24580
  43.0 5.0 %copy-start.24 = (f32[4,4,64]{2,1,0:T(4,128)S(1)}, f32[4,4,64]{2,1,0:T(4,128)}, u32[]{:S(2)}) copy-start(f32[4,4,64]{2,1,0:T(4,128)} %get-tuple-element.177) | copy-start | bytes 12292
  43.0 7.7 %copy-start.23 = (f32[4,4,64]{2,1,0:T(4,128)S(1)}, f32[4,4,64]{2,1,0:T(4,128)}, u32[]{:S(2)}) copy-start(f32[4,4,64]{2,1,0:T(4,128)} %get-tuple-element.176) | copy-start | bytes 12292
  43.7 16.6 %copy-start = (bf16[3,2,8,128]{3,2,1,0:T(8,128)(2,1)S(1)}, bf16[3,2,8,128]{3,2,1,0:T(8,128)(2,1)}, u32[]{:S(2)}) copy-start(bf16[3,2,8,128]{3,2,1,0:T(8,128)(2,1)} %param.10) | copy-start | bytes 36868
  43.7 16.6 %copy-start.21 = (f32[2,8,128]{2,1,0:T(8,128)S(1)}, f32[2,8,128]{2,1,0:T(8,128)}, u32[]{:S(2)}) copy-start(f32[2,8,128]{2,1,0:T(8,128)} %param.11) | copy-start | bytes 24580
  45.1 34.8 %collective-permute-start.7 = (f32[4,1,512]{2,1,0:T(1,128)S(1)}, f32[4,1,512]{2,1,0:T(1,128)S(1)}, u32[]{:S(2)}, u32[]{:S(2)}) collective-permute-start(f32[4,1,512]{2,1,0:T(1,128)S(1)} %copy-done.22), channel_id=1, source_target_pairs={{0,1},{1,0},{2,3},{3,2},{4,5},{5,4},{6,7},{7,6},{8,9},{9,8},{10,11... | collective-permute-start | bytes 24584 | tf_op jit(solution)/shard_map/ppermute | solution.py:86
  48.0 32.9 %collective-permute-start.4 = (f32[4,4,64]{2,1,0:T(4,128)S(1)}, f32[4,4,64]{2,1,0:T(4,128)S(1)}, u32[]{:S(2)}, u32[]{:S(2)}) collective-permute-start(f32[4,4,64]{2,1,0:T(4,128)S(1)} %copy-done.24), channel_id=1, source_target_pairs={{0,4},{4,8},{8,12},{12,16},{16,20},{20,24},{24,28},{28,32},{32,36}... | collective-permute-start | bytes 12296 | tf_op jit(solution)/shard_map/ppermute | solution.py:89
  50.7 30.2 %collective-permute-start.5 = (f32[4,4,64]{2,1,0:T(4,128)S(1)}, f32[4,4,64]{2,1,0:T(4,128)S(1)}, u32[]{:S(2)}, u32[]{:S(2)}) collective-permute-start(f32[4,4,64]{2,1,0:T(4,128)S(1)} %copy-done.23), channel_id=1, source_target_pairs={{4,0},{8,4},{12,8},{16,12},{20,16},{24,20},{28,24},{32,28},{36,32}... | collective-permute-start | bytes 12296 | tf_op jit(solution)/shard_map/ppermute | solution.py:90
  70.9 21.0 %copy-start.31 = (f32[8,16]{1,0:T(8,128)S(1)}, f32[8,16]{1,0:T(8,128)}, u32[]{:S(2)}) copy-start(f32[8,16]{1,0:T(8,128)} %constant.275.clone) | copy-start | bytes 1540
  71.6 19.4 %all-to-all-start = ((f32[128,1,96]{2,1,0:T(1,128)}), f32[128,1,96]{2,1,0:T(1,128)S(1)}, u32[]{:S(2)}, u32[]{:S(2)}) async-start(f32[128,1,96]{2,1,0:T(1,128)} %copy.222), calls=%async_computation | async-start | bytes 131072 | tf_op jit(solution)/shard_map/all_to_all | solution.py:215
  95.0 2.1 %copy-start.6 = (f32[2,4,512]{2,1,0:T(4,128)S(1)}, f32[2,4,512]{2,1,0:T(4,128)}, u32[]{:S(2)}) copy-start(f32[2,4,512]{2,1,0:T(4,128)} %get-tuple-element.158) | copy-start | bytes 49156
  95.0 2.1 %copy-start.7 = (f32[2,4,512]{2,1,0:T(4,128)S(1)}, f32[2,4,512]{2,1,0:T(4,128)}, u32[]{:S(2)}) copy-start(f32[2,4,512]{2,1,0:T(4,128)} %get-tuple-element.231) | copy-start | bytes 49156
  95.0 2.1 %copy-start.8 = (f32[2,4,512]{2,1,0:T(4,128)S(1)}, f32[2,4,512]{2,1,0:T(4,128)}, u32[]{:S(2)}) copy-start(f32[2,4,512]{2,1,0:T(4,128)} %get-tuple-element.142) | copy-start | bytes 49156
  95.0 2.1 %copy-start.9 = (f32[2,4,512]{2,1,0:T(4,128)S(1)}, f32[2,4,512]{2,1,0:T(4,128)}, u32[]{:S(2)}) copy-start(f32[2,4,512]{2,1,0:T(4,128)} %get-tuple-element.223) | copy-start | bytes 49156
  95.0 2.1 %copy-start.13 = (f32[1,4,512]{2,1,0:T(4,128)S(1)}, f32[1,4,512]{2,1,0:T(4,128)}, u32[]{:S(2)}) copy-start(f32[1,4,512]{2,1,0:T(4,128)} %get-tuple-element.146) | copy-start | bytes 24580
  95.0 2.1 %copy-start.14 = (f32[1,4,512]{2,1,0:T(4,128)S(1)}, f32[1,4,512]{2,1,0:T(4,128)}, u32[]{:S(2)}) copy-start(f32[1,4,512]{2,1,0:T(4,128)} %get-tuple-element.149) | copy-start | bytes 24580
  95.0 2.1 %copy-start.15 = (f32[1,4,512]{2,1,0:T(4,128)S(1)}, f32[1,4,512]{2,1,0:T(4,128)}, u32[]{:S(2)}) copy-start(f32[1,4,512]{2,1,0:T(4,128)} %get-tuple-element.226) | copy-start | bytes 24580
  95.0 2.1 %copy-start.16 = (f32[1,4,512]{2,1,0:T(4,128)S(1)}, f32[1,4,512]{2,1,0:T(4,128)}, u32[]{:S(2)}) copy-start(f32[1,4,512]{2,1,0:T(4,128)} %get-tuple-element.229) | copy-start | bytes 24580
  95.1 2.1 %copy-start.25 = (pred[512]{0:T(512)(128)(4,1)S(1)}, pred[512]{0:T(512)(128)(4,1)}, u32[]{:S(2)}) copy-start(pred[512]{0:T(512)(128)(4,1)} %get-tuple-element.234) | copy-start | bytes 1540
  95.1 2.1 %copy-start.26 = (pred[512]{0:T(512)(128)(4,1)S(1)}, pred[512]{0:T(512)(128)(4,1)}, u32[]{:S(2)}) copy-start(pred[512]{0:T(512)(128)(4,1)} %get-tuple-element.235) | copy-start | bytes 1540
  95.1 2.1 %copy-start.27 = (pred[512]{0:T(512)(128)(4,1)S(1)}, pred[512]{0:T(512)(128)(4,1)}, u32[]{:S(2)}) copy-start(pred[512]{0:T(512)(128)(4,1)} %get-tuple-element.236) | copy-start | bytes 1540
  95.1 2.1 %copy-start.28 = (pred[512]{0:T(512)(128)(4,1)S(1)}, pred[512]{0:T(512)(128)(4,1)}, u32[]{:S(2)}) copy-start(pred[512]{0:T(512)(128)(4,1)} %get-tuple-element.237) | copy-start | bytes 1540
  95.1 2.1 %copy-start.29 = (pred[512]{0:T(512)(128)(4,1)S(1)}, pred[512]{0:T(512)(128)(4,1)}, u32[]{:S(2)}) copy-start(pred[512]{0:T(512)(128)(4,1)} %get-tuple-element.232) | copy-start | bytes 1540
  95.1 2.1 %copy-start.30 = (pred[512]{0:T(512)(128)(4,1)S(1)}, pred[512]{0:T(512)(128)(4,1)}, u32[]{:S(2)}) copy-start(pred[512]{0:T(512)(128)(4,1)} %get-tuple-element.233) | copy-start | bytes 1540
  99.8 17.3 %collective-permute-start.10 = (f32[4,4,512]{2,1,0:T(4,128)S(1)}, f32[4,4,512]{2,1,0:T(4,128)S(1)}, u32[]{:S(2)}, u32[]{:S(2)}) collective-permute-start(f32[4,4,512]{2,1,0:T(4,128)S(1)} %fusion.66), channel_id=1, source_target_pairs={{0,2},{2,0},{1,3},{3,1},{4,6},{6,4},{5,7},{7,5},{8,10},{10,8},{9,1... | collective-permute-start | bytes 98312 | tf_op jit(solution)/shard_map/ppermute | solution.py:86
  102.9 14.0 %collective-permute-start.11 = (f32[4,1,512]{2,1,0:T(1,128)S(1)}, f32[4,1,512]{2,1,0:T(1,128)S(1)}, u32[]{:S(2)}, u32[]{:S(2)}) collective-permute-start(f32[4,1,512]{2,1,0:T(1,128)S(1)} %broadcast_select_fusion.10), channel_id=1, source_target_pairs={{0,1},{1,0},{2,3},{3,2},{4,5},{5,4},{6,7},{7,6},{8,9},{9,8},{10,11... | collective-permute-start | bytes 24584 | tf_op jit(solution)/shard_map/ppermute | solution.py:86
  110.6 6.7 %collective-permute-start.9 = (f32[4,4,64]{2,1,0:T(4,128)S(1)}, f32[4,4,64]{2,1,0:T(4,128)S(1)}, u32[]{:S(2)}, u32[]{:S(2)}) collective-permute-start(f32[4,4,64]{2,1,0:T(4,128)S(1)} %get-tuple-element.140), channel_id=1, source_target_pairs={{4,0},{8,4},{12,8},{16,12},{20,16},{24,20},{28,24},{32,28},{36,32}... | collective-permute-start | bytes 12296 | tf_op jit(solution)/shard_map/ppermute | solution.py:90
  115.0 9.8 %collective-permute-start.8 = (f32[4,4,64]{2,1,0:T(4,128)S(1)}, f32[4,4,64]{2,1,0:T(4,128)S(1)}, u32[]{:S(2)}, u32[]{:S(2)}) collective-permute-start(f32[4,4,64]{2,1,0:T(4,128)S(1)} %get-tuple-element.141), channel_id=1, source_target_pairs={{0,4},{4,8},{8,12},{12,16},{16,20},{20,24},{24,28},{28,32},{32,36}... | collective-permute-start | bytes 12296 | tf_op jit(solution)/shard_map/ppermute | solution.py:89
  127.7 12.5 %collective-permute-start.14 = (f32[4,4,512]{2,1,0:T(4,128)S(1)}, f32[4,4,512]{2,1,0:T(4,128)S(1)}, u32[]{:S(2)}, u32[]{:S(2)}) collective-permute-start(f32[4,4,512]{2,1,0:T(4,128)S(1)} %fusion.78), channel_id=1, source_target_pairs={{0,2},{2,0},{1,3},{3,1},{4,6},{6,4},{5,7},{7,5},{8,10},{10,8},{9,1... | collective-permute-start | bytes 98312 | tf_op jit(solution)/shard_map/ppermute | solution.py:86
  130.3 15.0 %copy-start.3 = (f32[2,1,1,4,512]{4,3,0,2,1:T(4,128)S(1)}, f32[2,1,1,4,512]{4,3,0,2,1:T(4,128)}, u32[]{:S(2)}) copy-start(f32[2,1,1,4,512]{4,3,0,2,1:T(4,128)} %get-tuple-element.230) | copy-start | bytes 49156
  130.3 15.0 %copy-start.4 = (f32[2,1,1,4,512]{4,3,0,2,1:T(4,128)S(1)}, f32[2,1,1,4,512]{4,3,0,2,1:T(4,128)}, u32[]{:S(2)}) copy-start(f32[2,1,1,4,512]{4,3,0,2,1:T(4,128)} %get-tuple-element.143) | copy-start | bytes 49156
  130.3 15.0 %copy-start.5 = (f32[2,1,1,4,512]{4,3,0,2,1:T(4,128)S(1)}, f32[2,1,1,4,512]{4,3,0,2,1:T(4,128)}, u32[]{:S(2)}) copy-start(f32[2,1,1,4,512]{4,3,0,2,1:T(4,128)} %get-tuple-element.222) | copy-start | bytes 49156
  130.3 15.0 %copy-start.10 = (f32[1,1,1,4,512]{4,3,0,2,1:T(4,128)S(1)}, f32[1,1,1,4,512]{4,3,0,2,1:T(4,128)}, u32[]{:S(2)}) copy-start(f32[1,1,1,4,512]{4,3,0,2,1:T(4,128)} %get-tuple-element.148) | copy-start | bytes 24580
  130.3 15.0 %copy-start.11 = (f32[1,1,1,4,512]{4,3,2,1,0:T(4,128)S(1)}, f32[1,1,1,4,512]{4,3,2,1,0:T(4,128)}, u32[]{:S(2)}) copy-start(f32[1,1,1,4,512]{4,3,2,1,0:T(4,128)} %get-tuple-element.227) | copy-start | bytes 24580
  130.3 15.0 %copy-start.12 = (f32[1,1,1,4,512]{4,3,2,1,0:T(4,128)S(1)}, f32[1,1,1,4,512]{4,3,2,1,0:T(4,128)}, u32[]{:S(2)}) copy-start(f32[1,1,1,4,512]{4,3,2,1,0:T(4,128)} %get-tuple-element.228) | copy-start | bytes 24580
  130.3 9.7 %collective-permute-start.15 = (f32[4,1,512]{2,1,0:T(1,128)S(1)}, f32[4,1,512]{2,1,0:T(1,128)S(1)}, u32[]{:S(2)}, u32[]{:S(2)}) collective-permute-start(f32[4,1,512]{2,1,0:T(1,128)S(1)} %broadcast_select_fusion.8), channel_id=1, source_target_pairs={{0,1},{1,0},{2,3},{3,2},{4,5},{5,4},{6,7},{7,6},{8,9},{9,8},{10,11... | collective-permute-start | bytes 24584 | tf_op jit(solution)/shard_map/ppermute | solution.py:86
  133.3 7.1 %collective-permute-start.13 = (f32[4,4,64]{2,1,0:T(4,128)S(1)}, f32[4,4,64]{2,1,0:T(4,128)S(1)}, u32[]{:S(2)}, u32[]{:S(2)}) collective-permute-start(f32[4,4,64]{2,1,0:T(4,128)S(1)} %get-tuple-element.104), channel_id=1, source_target_pairs={{4,0},{8,4},{12,8},{16,12},{20,16},{24,20},{28,24},{32,28},{36,32}... | collective-permute-start | bytes 12296 | tf_op jit(solution)/shard_map/ppermute | solution.py:90
  135.2 9.8 %collective-permute-start.12 = (f32[4,4,64]{2,1,0:T(4,128)S(1)}, f32[4,4,64]{2,1,0:T(4,128)S(1)}, u32[]{:S(2)}, u32[]{:S(2)}) collective-permute-start(f32[4,4,64]{2,1,0:T(4,128)S(1)} %get-tuple-element.105), channel_id=1, source_target_pairs={{0,4},{4,8},{8,12},{12,16},{16,20},{20,24},{24,28},{28,32},{32,36}... | collective-permute-start | bytes 12296 | tf_op jit(solution)/shard_map/ppermute | solution.py:89

commit v3 on v2

--- a/solution.py
+++ b/solution.py
@@ -80,6 +80,10 @@
     count = lax.axis_size(axis)
     if count == 1:
         return jnp.zeros_like(upper), jnp.zeros_like(lower)
+    return neighbours_on(lower, upper, axis, count)
+
+
+def neighbours_on(lower, upper, axis, count):
     if count == 2:
         index = lax.axis_index(axis)
         sent = jnp.where(index == 0, upper, lower)
@@ -91,7 +95,7 @@
     return from_below, from_above
 
 
-def source_cells(velocity, viscosity):
+def source_from_halo(velocity, viscosity):
     below_x, above_x = neighbours(velocity[:, :1], velocity[:, -1:], "gx")
     below_y, above_y = neighbours(velocity[:, :, :1], velocity[:, :, -1:], "gy")
     below_z, above_z = neighbours(velocity[..., :1], velocity[..., -1:], "gz")
@@ -128,7 +132,7 @@
     return LIFT_FACTOR * jnp.stack(parts)
 
 
-def tendency(fields, forcing, tables):
+def tendency(fields, tables):
     highest = lax.Precision.HIGHEST
     count = fields.shape[1]
     grads = [jnp.dot(fields[0], table, precision=highest) for table in tables]
@@ -137,14 +141,7 @@
         + jnp.dot(fields[2], tables[1], precision=highest)
         + jnp.dot(fields[3], tables[2], precision=highest)
     )
-    result = jnp.stack(
-        [
-            -divergence,
-            COUPLING * forcing[0] - grads[0],
-            COUPLING * forcing[1] - grads[1],
-            COUPLING * forcing[2] - grads[2],
-        ]
-    )
+    result = jnp.stack([-divergence, -grads[0], -grads[1], -grads[2]])
 
     face = 64
     below_x, above_x = neighbours(fields[..., :face], fields[..., NODES - face :], "gx")
@@ -175,8 +172,10 @@
 
 def runge_kutta(fields, forcing):
     tables = kron_tables()
-    step = lambda f: tendency(f, forcing, tables)
-    section_one = fields + TIME_STEP * tendency(fields, forcing, tables)
+    coupled = jnp.concatenate([jnp.zeros_like(forcing[:1]), COUPLING * forcing])
+    step = lambda f: tendency(f, tables) + coupled
+    first = tendency(fields, tables)
+    section_one = fields + TIME_STEP * (first + coupled)
     section_two = 0.75 * fields + 0.25 * (section_one + TIME_STEP * step(section_one))
     return 1.0 / 3.0 * fields + 2.0 / 3.0 * (section_two + TIME_STEP * step(section_two))
 
@@ -188,7 +187,7 @@
 
 
 def on_device_body(velocity, eddy_viscosity, cell_owner, cell_element, cell_position, acoustic_state):
-    sources = source_cells(velocity, eddy_viscosity)
+    sources = source_from_halo(velocity, eddy_viscosity)
     cell_count = sources.shape[1] * sources.shape[2] * sources.shape[3]
     flat_source = sources.reshape(3, cell_count).astype(jnp.float32)
     owners = cell_owner.reshape(cell_count)

time: 148 us -> 148 us (level)
  the two profiles are of different devices: /device:TPU:64 before, /device:TPU:62 now
where the time goes in v3:
time: 148 us; the launch traced here: 146 us
  starting transfers between devices  69.9 us (47%)
  other arithmetic  22.7 us (15%)
  local copies, waits for them, and re-layouts  20.2 us (14%)
  waiting for transfers between devices  16.9 us (11%)
  matrix products  14.5 us (10%)
  between operations  2.04 us (1%)
    ppermute x8, starting transfers between devices, neighbours_on(): got = lax.ppermute(sent, axis, [(0, 1), (1, 0)])  30.2 us
    ppermute x4, starting transfers between devices, neighbours_on(): lax.ppermute(upper, axis, [(i, i + 1) for i in range(count - 1)])  16.5 us
    ppermute x4, waiting for transfers between devices, neighbours_on(): lax.ppermute(lower, axis, [(i + 1, i) for i in range(count - 1)])  13 us
    ppermute x4, starting transfers between devices, neighbours_on(): lax.ppermute(lower, axis, [(i + 1, i) for i in range(count - 1)])  12.8 us
    all_to_all x1, starting transfers between devices, on_device_body(): got = lax.all_to_all(send, 'gx', split_axis=0, concat_axis=0, tiled=True)  10.4 us
    dot_general x9, matrix products, tendency(): grads = [jnp.dot(fields[0], table, precision=highest) for table in tables]  7.43 us
    scatter x1, local copies, waits for them, and re-layouts, on_device_body(): send = jnp.zeros((4, owner_count * capacity), jnp.float32).at[:, slot_ind...  7.16 us
    select_n x5, other arithmetic, neighbours_on(): sent = jnp.where(index == 0, upper, lower)  4.3 us
  transfers between devices with their start and end apart: 17, of which 3 were waited for; matrix products, arithmetic and copies ran while one was open for 33% of the time, Pallas kernels for 0%

profile of v3, /device:TPU:62, one launch (start us, length us, event | category | flops | bytes accessed | tf_op | source)
XLA Modules:
  0.0 146.2 jit_solution(187407596080932320)
XLA Ops:
  0.6 1.5 slice_select_fusion
  2.1 10.9 %collective-permute-start.3 = (bf16[3,2,8,1]{3,2,1,0:T(8,128)(2,1)}, bf16[3,2,8,1]{3,2,1,0:T(8,128)(2,1)}, u32[]{:S(2)}, u32[]{:S(2)}) collective-permute-start(bf16[3,2,8,1]{3,2,1,0:T(8,128)(2,1)} %slice_select_fusion), channel_id=1, source_target_pairs={{0,1},{1,0},{2,3},{3,2},{4,5},{5,4},{6,7},{7,6},{8,9},{9,8},{10,11... | collective-permute-start | bytes 296 | tf_op jit(solution)/shard_map/ppermute | solution.py:90
  13.0 1.4 broadcast_select_fusion.18
  14.4 1.9 %collective-permute-start.2 = (bf16[3,2,1,128]{3,2,1,0:T(2,128)(2,1)}, bf16[3,2,1,128]{3,2,1,0:T(2,128)(2,1)}, u32[]{:S(2)}, u32[]{:S(2)}) collective-permute-start(bf16[3,2,1,128]{3,2,1,0:T(2,128)(2,1)} %broadcast_select_fusion.18), channel_id=1, source_target_pairs={{0,2},{2,0},{1,3},{3,1},{4,6},{6,4},{5,7},{7,5},{8,10},{10,8},{9,1... | collective-permute-start | bytes 4616 | tf_op jit(solution)/shard_map/ppermute | solution.py:90
  16.3 1.3 fusion.171
  17.6 3.2 %collective-permute-start = (bf16[3,1,8,128]{3,2,1,0:T(8,128)(2,1)}, bf16[3,1,8,128]{3,2,1,0:T(8,128)(2,1)}, u32[]{:S(2)}, u32[]{:S(2)}) collective-permute-start(bf16[3,1,8,128]{3,2,1,0:T(8,128)(2,1)} %get-tuple-element.166), channel_id=1, source_target_pairs={{4,0},{8,4},{12,8},{16,12},{20,16},{24,20},{28,24},{32,28},{36,32}... | collective-permute-start | bytes 18440 | tf_op jit(solution)/shard_map/ppermute | solution.py:94
  20.9 6.8 %collective-permute-start.1 = (bf16[3,1,8,128]{3,2,1,0:T(8,128)(2,1)}, bf16[3,1,8,128]{3,2,1,0:T(8,128)(2,1)}, u32[]{:S(2)}, u32[]{:S(2)}) collective-permute-start(bf16[3,1,8,128]{3,2,1,0:T(8,128)(2,1)} %get-tuple-element.167), channel_id=1, source_target_pairs={{0,4},{4,8},{8,12},{12,16},{16,20},{20,24},{24,28},{28,32},{32,36}... | collective-permute-start | bytes 18440 | tf_op jit(solution)/shard_map/ppermute | solution.py:93
  27.7 1.9 %collective-permute-start.6 = (f32[4,4,512]{2,1,0:T(4,128)}, f32[4,4,512]{2,1,0:T(4,128)S(1)}, u32[]{:S(2)}, u32[]{:S(2)}) collective-permute-start(f32[4,4,512]{2,1,0:T(4,128)} %bitcast.181), channel_id=1, source_target_pairs={{0,2},{2,0},{1,3},{3,1},{4,6},{6,4},{5,7},{7,5},{8,10},{10,8},{9,1... | collective-permute-start | bytes 98312 | tf_op jit(solution)/shard_map/ppermute | solution.py:90
  29.6 0.8 fusion.168
  30.4 0.9 fusion.169
  31.3 0.7 fusion.170
  32.0 1.4 broadcast_select_fusion.12
  33.4 0.8 fusion.166
  34.3 1.4 fusion.167
  35.9 1.2 and_select_fusion.2
  37.1 0.6 fusion.127
  37.7 1.3 fusion.12
  41.7 0.6 fusion.19
  42.3 0.6 compare_select_fusion
  43.5 1.3 fusion.11
  44.7 0.6 convolution_add_fusion.5
  45.9 1.2 fusion.10
  47.2 1.3 fusion.14
  48.5 1.9 %collective-permute-start.7 = (f32[4,1,512]{2,1,0:T(1,128)}, f32[4,1,512]{2,1,0:T(1,128)}, u32[]{:S(2)}, u32[]{:S(2)}) collective-permute-start(f32[4,1,512]{2,1,0:T(1,128)} %broadcast_select_fusion.12), channel_id=1, source_target_pairs={{0,1},{1,0},{2,3},{3,2},{4,5},{5,4},{6,7},{7,6},{8,9},{9,8},{10,11... | collective-permute-start | bytes 24584 | tf_op jit(solution)/shard_map/ppermute | solution.py:90
  50.4 0.7 select_convert_fusion.1
  51.2 2.1 %collective-permute-start.4 = (f32[4,4,64]{2,1,0:T(4,128)}, f32[4,4,64]{2,1,0:T(4,128)S(1)}, u32[]{:S(2)}, u32[]{:S(2)}) collective-permute-start(f32[4,4,64]{2,1,0:T(4,128)} %get-tuple-element.153), channel_id=1, source_target_pairs={{0,4},{4,8},{8,12},{12,16},{16,20},{20,24},{24,28},{28,32},{32,36}... | collective-permute-start | bytes 12296 | tf_op jit(solution)/shard_map/ppermute | solution.py:93
  53.3 0.7 fusion.141
  54.1 3.7 %collective-permute-start.5 = (f32[4,4,64]{2,1,0:T(4,128)}, f32[4,4,64]{2,1,0:T(4,128)}, u32[]{:S(2)}, u32[]{:S(2)}) collective-permute-start(f32[4,4,64]{2,1,0:T(4,128)} %get-tuple-element.152), channel_id=1, source_target_pairs={{4,0},{8,4},{12,8},{16,12},{20,16},{24,20},{28,24},{32,28},{36,32}... | collective-permute-start | bytes 12296 | tf_op jit(solution)/shard_map/ppermute | solution.py:94
  57.8 0.7 convert_element_type.101
  58.5 0.7 convert_element_type.102
  59.4 1.3 copy.34
  60.7 7.2 %scatter_custom_fusion = f32[4,3072]{0,1:T(8,128)} fusion(s32[2048]{0:T(1024)} %bitcast.196, f32[2048,4]{1,0:T(8,128)} %copy.34, f32[]{:T(128)} %constant.244.clone.1), kind=kCustom, calls=%fused_computation.61 | custom fusion | bytes 49664 | tf_op jit(solution)/shard_map/scatter | solution.py:210
  67.9 1.9 %copy.35 = f32[4,128,24]{1,2,0:T(8,128)S(1)} copy(f32[4,128,24]{0,2,1:T(8,128)} %bitcast.180) | data formatting | bytes 98304 | tf_op jit(solution)/shard_map/reshape | solution.py:211
  69.8 0.7 copy.36
  70.5 10.4 %all-to-all-start = ((f32[128,1,96]{2,1,0:T(1,128)}), f32[128,1,96]{2,1,0:T(1,128)S(1)}, u32[]{:S(2)}, u32[]{:S(2)}) async-start(f32[128,1,96]{2,1,0:T(1,128)} %copy.36), calls=%async_computation | async-start | bytes 131072 | tf_op jit(solution)/shard_map/all_to_all | solution.py:214
  80.9 0.7 broadcast_select_fusion.11
  82.0 0.9 broadcast_multiply_fusion.13
  82.8 0.7 fusion.115
  83.5 0.6 fusion.111
  84.1 0.6 fusion.119
  85.9 3.9 %all-to-all-done = f32[128,1,96]{2,1,0:T(1,128)S(1)} async-done(((f32[128,1,96]{2,1,0:T(1,128)}), f32[128,1,96]{2,1,0:T(1,128)S(1)}, u32[]{:S(2)}, u32[]{:S(2)}) %all-to-all-start) | async-done | bytes 49184 | tf_op jit(solution)/shard_map/all_to_all | solution.py:214
  90.3 0.6 iota_compare_fusion.6
  91.2 0.8 broadcast_select_fusion
  92.0 1.6 %select_reduce_fusion.2 = (f32[8,3072]{1,0:T(8,128)S(1)}, f32[8,3072]{1,0:T(8,128)S(1)}, f32[8,3072]{1,0:T(8,128)S(1)}) fusion(f32[8,16]{1,0:T(8,128)} %constant.276.clone, pred[16,3072]{1,0:T(8,128)(4,1)S(1)} %iota_compare_fusion.5, pred[16,3072]{1,0:T(8,128)(4,1)S(1)} %iota_compare_fusion.4, pred[16,3072]{1,0:T(8,128)(4,1)S(1)} %iota_compare_fusion.3), kind=kLoop, calls=%fused_computation.14 | loop fusion | flops 2285568 | bytes 442880 | tf_op jit(solution)/shard_map/reduce_sum | solution.py:186
  94.5 0.9 convolution_multiply_fusion
  95.7 0.8 fusion.26
  96.5 1.9 %collective-permute-start.10 = (f32[4,4,512]{2,1,0:T(4,128)S(1)}, f32[4,4,512]{2,1,0:T(4,128)S(1)}, u32[]{:S(2)}, u32[]{:S(2)}) collective-permute-start(f32[4,4,512]{2,1,0:T(4,128)S(1)} %fusion.26), channel_id=1, source_target_pairs={{0,2},{2,0},{1,3},{3,1},{4,6},{6,4},{5,7},{7,5},{8,10},{10,8},{9,1... | collective-permute-start | bytes 98312 | tf_op jit(solution)/shard_map/ppermute | solution.py:90
  99.2 0.6 fusion.7
  99.8 0.6 fusion.6
  100.4 7.8 %collective-permute-start.11 = (f32[4,1,512]{2,1,0:T(1,128)S(1)}, f32[4,1,512]{2,1,0:T(1,128)S(1)}, u32[]{:S(2)}, u32[]{:S(2)}) collective-permute-start(f32[4,1,512]{2,1,0:T(1,128)S(1)} %broadcast_select_fusion.10), channel_id=1, source_target_pairs={{0,1},{1,0},{2,3},{3,2},{4,5},{5,4},{6,7},{7,6},{8,9},{9,8},{10,11... | collective-permute-start | bytes 24584 | tf_op jit(solution)/shard_map/ppermute | solution.py:90
  109.4 0.6 fusion.5
  110.0 5.6 %collective-permute-start.8 = (f32[4,4,64]{2,1,0:T(4,128)S(1)}, f32[4,4,64]{2,1,0:T(4,128)S(1)}, u32[]{:S(2)}, u32[]{:S(2)}) collective-permute-start(f32[4,4,64]{2,1,0:T(4,128)S(1)} %get-tuple-element.133), channel_id=1, source_target_pairs={{0,4},{4,8},{8,12},{12,16},{16,20},{20,24},{24,28},{28,32},{32,36}... | collective-permute-start | bytes 12296 | tf_op jit(solution)/shard_map/ppermute | solution.py:93
  115.7 1.9 %collective-permute-start.9 = (f32[4,4,64]{2,1,0:T(4,128)S(1)}, f32[4,4,64]{2,1,0:T(4,128)S(1)}, u32[]{:S(2)}, u32[]{:S(2)}) collective-permute-start(f32[4,4,64]{2,1,0:T(4,128)S(1)} %get-tuple-element.132), channel_id=1, source_target_pairs={{4,0},{8,4},{12,8},{16,12},{20,16},{24,20},{28,24},{32,28},{36,32}... | collective-permute-start | bytes 12296 | tf_op jit(solution)/shard_map/ppermute | solution.py:94
  118.0 7.5 %collective-permute-done.9 = f32[4,4,64]{2,1,0:T(4,128)S(1)} collective-permute-done((f32[4,4,64]{2,1,0:T(4,128)S(1)}, f32[4,4,64]{2,1,0:T(4,128)S(1)}, u32[]{:S(2)}, u32[]{:S(2)}) %collective-permute-start.9) | collective-permute-done | bytes 4128 | tf_op jit(solution)/shard_map/ppermute | solution.py:94
  125.9 1.9 %collective-permute-start.14 = (f32[4,4,512]{2,1,0:T(4,128)S(1)}, f32[4,4,512]{2,1,0:T(4,128)S(1)}, u32[]{:S(2)}, u32[]{:S(2)}) collective-permute-start(f32[4,4,512]{2,1,0:T(4,128)S(1)} %fusion.30), channel_id=1, source_target_pairs={{0,2},{2,0},{1,3},{3,1},{4,6},{6,4},{5,7},{7,5},{8,10},{10,8},{9,1... | collective-permute-start | bytes 98312 | tf_op jit(solution)/shard_map/ppermute | solution.py:90
  128.5 0.6 fusion.2
  129.1 0.6 fusion.1
  129.8 1.9 %collective-permute-start.15 = (f32[4,1,512]{2,1,0:T(1,128)S(1)}, f32[4,1,512]{2,1,0:T(1,128)S(1)}, u32[]{:S(2)}, u32[]{:S(2)}) collective-permute-start(f32[4,1,512]{2,1,0:T(1,128)S(1)} %broadcast_select_fusion.8), channel_id=1, source_target_pairs={{0,1},{1,0},{2,3},{3,2},{4,5},{5,4},{6,7},{7,6},{8,9},{9,8},{10,11... | collective-permute-start | bytes 24584 | tf_op jit(solution)/shard_map/ppermute | solution.py:90
  132.3 0.6 fusion.4
  132.9 0.6 fusion
  133.5 1.9 %collective-permute-start.12 = (f32[4,4,64]{2,1,0:T(4,128)S(1)}, f32[4,4,64]{2,1,0:T(4,128)S(1)}, u32[]{:S(2)}, u32[]{:S(2)}) collective-permute-start(f32[4,4,64]{2,1,0:T(4,128)S(1)} %get-tuple-element.113), channel_id=1, source_target_pairs={{0,4},{4,8},{8,12},{12,16},{16,20},{20,24},{24,28},{28,32},{32,36}... | collective-permute-start | bytes 12296 | tf_op jit(solution)/shard_map/ppermute | solution.py:93
  135.4 3.9 %collective-permute-start.13 = (f32[4,4,64]{2,1,0:T(4,128)S(1)}, f32[4,4,64]{2,1,0:T(4,128)S(1)}, u32[]{:S(2)}, u32[]{:S(2)}) collective-permute-start(f32[4,4,64]{2,1,0:T(4,128)S(1)} %get-tuple-element.112), channel_id=1, source_target_pairs={{4,0},{8,4},{12,8},{16,12},{20,16},{24,20},{28,24},{32,28},{36,32}... | collective-permute-start | bytes 12296 | tf_op jit(solution)/shard_map/ppermute | solution.py:94
  139.7 5.5 %collective-permute-done.13 = f32[4,4,64]{2,1,0:T(4,128)S(1)} collective-permute-done((f32[4,4,64]{2,1,0:T(4,128)S(1)}, f32[4,4,64]{2,1,0:T(4,128)S(1)}, u32[]{:S(2)}, u32[]{:S(2)}) %collective-permute-start.13) | collective-permute-done | bytes 4128 | tf_op jit(solution)/shard_map/ppermute | solution.py:94
  145.5 0.7 fusion.35
  (205 shorter events, 11.4 us)
Async XLA Ops:
  0.6 36.5 %copy-start.1 = (f32[4,1,1,4,512]{4,3,2,1,0:T(4,128)S(1)}, f32[4,1,1,4,512]{4,3,2,1,0:T(4,128)}, u32[]{:S(2)}) copy-start(f32[4,1,1,4,512]{4,3,2,1,0:T(4,128)} %param.15) | copy-start | bytes 98308
  2.1 46.4 %collective-permute-start.3 = (bf16[3,2,8,1]{3,2,1,0:T(8,128)(2,1)}, bf16[3,2,8,1]{3,2,1,0:T(8,128)(2,1)}, u32[]{:S(2)}, u32[]{:S(2)}) collective-permute-start(bf16[3,2,8,1]{3,2,1,0:T(8,128)(2,1)} %slice_select_fusion), channel_id=1, source_target_pairs={{0,1},{1,0},{2,3},{3,2},{4,5},{5,4},{6,7},{7,6},{8,9},{9,8},{10,11... | collective-permute-start | bytes 296 | tf_op jit(solution)/shard_map/ppermute | solution.py:90
  14.4 36.8 %collective-permute-start.2 = (bf16[3,2,1,128]{3,2,1,0:T(2,128)(2,1)}, bf16[3,2,1,128]{3,2,1,0:T(2,128)(2,1)}, u32[]{:S(2)}, u32[]{:S(2)}) collective-permute-start(bf16[3,2,1,128]{3,2,1,0:T(2,128)(2,1)} %broadcast_select_fusion.18), channel_id=1, source_target_pairs={{0,2},{2,0},{1,3},{3,1},{4,6},{6,4},{5,7},{7,5},{8,10},{10,8},{9,1... | collective-permute-start | bytes 4616 | tf_op jit(solution)/shard_map/ppermute | solution.py:90
  17.6 36.5 %collective-permute-start = (bf16[3,1,8,128]{3,2,1,0:T(8,128)(2,1)}, bf16[3,1,8,128]{3,2,1,0:T(8,128)(2,1)}, u32[]{:S(2)}, u32[]{:S(2)}) collective-permute-start(bf16[3,1,8,128]{3,2,1,0:T(8,128)(2,1)} %get-tuple-element.166), channel_id=1, source_target_pairs={{4,0},{8,4},{12,8},{16,12},{20,16},{24,20},{28,24},{32,28},{36,32}... | collective-permute-start | bytes 18440 | tf_op jit(solution)/shard_map/ppermute | solution.py:94
  20.9 37.6 %collective-permute-start.1 = (bf16[3,1,8,128]{3,2,1,0:T(8,128)(2,1)}, bf16[3,1,8,128]{3,2,1,0:T(8,128)(2,1)}, u32[]{:S(2)}, u32[]{:S(2)}) collective-permute-start(bf16[3,1,8,128]{3,2,1,0:T(8,128)(2,1)} %get-tuple-element.167), channel_id=1, source_target_pairs={{0,4},{4,8},{8,12},{12,16},{16,20},{20,24},{24,28},{28,32},{32,36}... | collective-permute-start | bytes 18440 | tf_op jit(solution)/shard_map/ppermute | solution.py:93
  27.7 54.1 %collective-permute-start.6 = (f32[4,4,512]{2,1,0:T(4,128)}, f32[4,4,512]{2,1,0:T(4,128)S(1)}, u32[]{:S(2)}, u32[]{:S(2)}) collective-permute-start(f32[4,4,512]{2,1,0:T(4,128)} %bitcast.181), channel_id=1, source_target_pairs={{0,2},{2,0},{1,3},{3,1},{4,6},{6,4},{5,7},{7,5},{8,10},{10,8},{9,1... | collective-permute-start | bytes 98312 | tf_op jit(solution)/shard_map/ppermute | solution.py:90
  35.8 1.3 copy-start.28
  35.8 7.2 %copy-start.26 = (s32[512]{0:T(512)}, s32[512]{0:T(512)S(1)}, u32[]{:S(2)}) copy-start(s32[512]{0:T(512)S(1)} %get-tuple-element.188) | copy-start | bytes 6148
  35.8 1.3 copy-start.43
  35.8 7.1 %copy-start.41 = (pred[512]{0:T(512)(128)(4,1)}, pred[512]{0:T(512)(128)(4,1)S(1)}, u32[]{:S(2)}) copy-start(pred[512]{0:T(512)(128)(4,1)S(1)} %get-tuple-element.186) | copy-start | bytes 1540
  35.9 4.9 %copy-start.3 = (s32[1,1,2048,1]{2,3,1,0:T(1,128)S(1)}, s32[1,1,2048,1]{2,3,1,0:T(1,128)}, u32[]{:S(2)}) copy-start(s32[1,1,2048,1]{2,3,1,0:T(1,128)} %param.12) | copy-start | bytes 24580
  41.3 1.6 %copy-start.31 = (f32[8,512]{1,0:T(8,128)S(1)}, f32[8,512]{1,0:T(8,128)}, u32[]{:S(2)}) copy-start(f32[8,512]{1,0:T(8,128)} %constant.278.clone) | copy-start | bytes 49156
  42.9 2.4 %copy-start.29 = (s32[512]{0:T(512)S(1)}, s32[512]{0:T(512)}, u32[]{:S(2)}) copy-start(s32[512]{0:T(512)} %copy-done.28) | copy-start | bytes 6148
  42.9 2.4 %copy-start.30 = (f32[8,512]{1,0:T(8,128)S(1)}, f32[8,512]{1,0:T(8,128)}, u32[]{:S(2)}) copy-start(f32[8,512]{1,0:T(8,128)} %constant.279.clone) | copy-start | bytes 49156
  43.0 2.4 %copy-start.44 = (pred[512]{0:T(512)(128)(4,1)S(1)}, pred[512]{0:T(512)(128)(4,1)}, u32[]{:S(2)}) copy-start(pred[512]{0:T(512)(128)(4,1)} %copy-done.43) | copy-start | bytes 1540
  43.4 1.9 %copy-start.27 = (s32[512]{0:T(512)S(1)}, s32[512]{0:T(512)}, u32[]{:S(2)}) copy-start(s32[512]{0:T(512)} %copy-done.26) | copy-start | bytes 6148
  43.5 1.9 %copy-start.42 = (pred[512]{0:T(512)(128)(4,1)S(1)}, pred[512]{0:T(512)(128)(4,1)}, u32[]{:S(2)}) copy-start(pred[512]{0:T(512)(128)(4,1)} %copy-done.41) | copy-start | bytes 1540
  45.4 3.0 %copy-start.32 = (s32[1,1,2048]{2,1,0:T(1,128)S(1)}, s32[1,1,2048]{2,1,0:T(1,128)}, u32[]{:S(2)}) copy-start(s32[1,1,2048]{2,1,0:T(1,128)} %param.14) | copy-start | bytes 24580
  45.4 3.0 %copy-start.33 = (s32[1,1,2048]{2,1,0:T(1,128)S(1)}, s32[1,1,2048]{2,1,0:T(1,128)}, u32[]{:S(2)}) copy-start(s32[1,1,2048]{2,1,0:T(1,128)} %param.13) | copy-start | bytes 24580
  45.4 3.0 %copy-start = (bf16[3,2,8,128]{3,2,1,0:T(8,128)(2,1)S(1)}, bf16[3,2,8,128]{3,2,1,0:T(8,128)(2,1)}, u32[]{:S(2)}) copy-start(bf16[3,2,8,128]{3,2,1,0:T(8,128)(2,1)} %param.10) | copy-start | bytes 36868
  45.9 13.3 %copy-start.34 = (f32[2,8,128]{2,1,0:T(8,128)S(1)}, f32[2,8,128]{2,1,0:T(8,128)}, u32[]{:S(2)}) copy-start(f32[2,8,128]{2,1,0:T(8,128)} %param.11) | copy-start | bytes 24580
  48.5 32.4 %collective-permute-start.7 = (f32[4,1,512]{2,1,0:T(1,128)}, f32[4,1,512]{2,1,0:T(1,128)}, u32[]{:S(2)}, u32[]{:S(2)}) collective-permute-start(f32[4,1,512]{2,1,0:T(1,128)} %broadcast_select_fusion.12), channel_id=1, source_target_pairs={{0,1},{1,0},{2,3},{3,2},{4,5},{5,4},{6,7},{7,6},{8,9},{9,8},{10,11... | collective-permute-start | bytes 24584 | tf_op jit(solution)/shard_map/ppermute | solution.py:90
  51.2 30.8 %collective-permute-start.4 = (f32[4,4,64]{2,1,0:T(4,128)}, f32[4,4,64]{2,1,0:T(4,128)S(1)}, u32[]{:S(2)}, u32[]{:S(2)}) collective-permute-start(f32[4,4,64]{2,1,0:T(4,128)} %get-tuple-element.153), channel_id=1, source_target_pairs={{0,4},{4,8},{8,12},{12,16},{16,20},{20,24},{24,28},{28,32},{32,36}... | collective-permute-start | bytes 12296 | tf_op jit(solution)/shard_map/ppermute | solution.py:93
  54.1 27.9 %collective-permute-start.5 = (f32[4,4,64]{2,1,0:T(4,128)}, f32[4,4,64]{2,1,0:T(4,128)}, u32[]{:S(2)}, u32[]{:S(2)}) collective-permute-start(f32[4,4,64]{2,1,0:T(4,128)} %get-tuple-element.152), channel_id=1, source_target_pairs={{4,0},{8,4},{12,8},{16,12},{20,16},{24,20},{28,24},{32,28},{36,32}... | collective-permute-start | bytes 12296 | tf_op jit(solution)/shard_map/ppermute | solution.py:94
  70.5 19.3 %all-to-all-start = ((f32[128,1,96]{2,1,0:T(1,128)}), f32[128,1,96]{2,1,0:T(1,128)S(1)}, u32[]{:S(2)}, u32[]{:S(2)}) async-start(f32[128,1,96]{2,1,0:T(1,128)} %copy.36), calls=%async_computation | async-start | bytes 131072 | tf_op jit(solution)/shard_map/all_to_all | solution.py:214
  94.2 1.2 copy-start.4
  94.2 1.2 copy-start.5
  94.3 1.2 copy-start.6
  94.3 1.2 copy-start.7
  94.3 1.2 copy-start.8
  94.3 1.2 copy-start.9
  94.3 1.2 copy-start.10
  94.3 1.2 copy-start.11
  94.3 1.2 copy-start.12
  94.3 1.2 copy-start.13
  94.3 1.2 copy-start.14
  94.3 1.2 copy-start.15
  94.4 1.2 copy-start.16
  94.4 1.2 copy-start.17
  94.4 1.2 copy-start.18
  94.4 1.2 copy-start.19
  94.4 1.2 copy-start.20
  94.4 1.2 copy-start.21
  94.4 1.2 copy-start.22
  94.4 1.2 copy-start.23
  94.4 1.2 copy-start.24
  94.4 1.2 copy-start.25
  94.5 1.2 copy-start.35
  94.5 1.2 copy-start.36
  94.5 1.2 copy-start.37
  94.5 1.2 copy-start.38
  95.4 4.9 %copy-start.2 = (f32[3,4,512]{2,1,0:T(4,128)}, f32[3,4,512]{2,1,0:T(4,128)S(1)}, u32[]{:S(2)}) copy-start(f32[3,4,512]{2,1,0:T(4,128)S(1)} %reshape.4564) | copy-start | bytes 73732
  96.5 21.2 %collective-permute-start.10 = (f32[4,4,512]{2,1,0:T(4,128)S(1)}, f32[4,4,512]{2,1,0:T(4,128)S(1)}, u32[]{:S(2)}, u32[]{:S(2)}) collective-permute-start(f32[4,4,512]{2,1,0:T(4,128)S(1)} %fusion.26), channel_id=1, source_target_pairs={{0,2},{2,0},{1,3},{3,1},{4,6},{6,4},{5,7},{7,5},{8,10},{10,8},{9,1... | collective-permute-start | bytes 98312 | tf_op jit(solution)/shard_map/ppermute | solution.py:90
  100.4 17.2 %collective-permute-start.11 = (f32[4,1,512]{2,1,0:T(1,128)S(1)}, f32[4,1,512]{2,1,0:T(1,128)S(1)}, u32[]{:S(2)}, u32[]{:S(2)}) collective-permute-start(f32[4,1,512]{2,1,0:T(1,128)S(1)} %broadcast_select_fusion.10), channel_id=1, source_target_pairs={{0,1},{1,0},{2,3},{3,2},{4,5},{5,4},{6,7},{7,6},{8,9},{9,8},{10,11... | collective-permute-start | bytes 24584 | tf_op jit(solution)/shard_map/ppermute | solution.py:90
  108.8 16.9 %copy-start.39 = (pred[512]{0:T(512)(128)(4,1)S(1)}, pred[512]{0:T(512)(128)(4,1)}, u32[]{:S(2)}) copy-start(pred[512]{0:T(512)(128)(4,1)} %get-tuple-element.206) | copy-start | bytes 1540
  108.8 16.9 %copy-start.40 = (pred[512]{0:T(512)(128)(4,1)S(1)}, pred[512]{0:T(512)(128)(4,1)}, u32[]{:S(2)}) copy-start(pred[512]{0:T(512)(128)(4,1)} %get-tuple-element.207) | copy-start | bytes 1540
  110.0 7.9 %collective-permute-start.8 = (f32[4,4,64]{2,1,0:T(4,128)S(1)}, f32[4,4,64]{2,1,0:T(4,128)S(1)}, u32[]{:S(2)}, u32[]{:S(2)}) collective-permute-start(f32[4,4,64]{2,1,0:T(4,128)S(1)} %get-tuple-element.133), channel_id=1, source_target_pairs={{0,4},{4,8},{8,12},{12,16},{16,20},{20,24},{24,28},{28,32},{32,36}... | collective-permute-start | bytes 12296 | tf_op jit(solution)/shard_map/ppermute | solution.py:93
  115.7 9.8 %collective-permute-start.9 = (f32[4,4,64]{2,1,0:T(4,128)S(1)}, f32[4,4,64]{2,1,0:T(4,128)S(1)}, u32[]{:S(2)}, u32[]{:S(2)}) collective-permute-start(f32[4,4,64]{2,1,0:T(4,128)S(1)} %get-tuple-element.132), channel_id=1, source_target_pairs={{4,0},{8,4},{12,8},{16,12},{20,16},{24,20},{28,24},{32,28},{36,32}... | collective-permute-start | bytes 12296 | tf_op jit(solution)/shard_map/ppermute | solution.py:94
  125.9 13.6 %collective-permute-start.14 = (f32[4,4,512]{2,1,0:T(4,128)S(1)}, f32[4,4,512]{2,1,0:T(4,128)S(1)}, u32[]{:S(2)}, u32[]{:S(2)}) collective-permute-start(f32[4,4,512]{2,1,0:T(4,128)S(1)} %fusion.30), channel_id=1, source_target_pairs={{0,2},{2,0},{1,3},{3,1},{4,6},{6,4},{5,7},{7,5},{8,10},{10,8},{9,1... | collective-permute-start | bytes 98312 | tf_op jit(solution)/shard_map/ppermute | solution.py:90
  129.8 9.6 %collective-permute-start.15 = (f32[4,1,512]{2,1,0:T(1,128)S(1)}, f32[4,1,512]{2,1,0:T(1,128)S(1)}, u32[]{:S(2)}, u32[]{:S(2)}) collective-permute-start(f32[4,1,512]{2,1,0:T(1,128)S(1)} %broadcast_select_fusion.8), channel_id=1, source_target_pairs={{0,1},{1,0},{2,3},{3,2},{4,5},{5,4},{6,7},{7,6},{8,9},{9,8},{10,11... | collective-permute-start | bytes 24584 | tf_op jit(solution)/shard_map/ppermute | solution.py:90
  133.5 6.2 %collective-permute-start.12 = (f32[4,4,64]{2,1,0:T(4,128)S(1)}, f32[4,4,64]{2,1,0:T(4,128)S(1)}, u32[]{:S(2)}, u32[]{:S(2)}) collective-permute-start(f32[4,4,64]{2,1,0:T(4,128)S(1)} %get-tuple-element.113), channel_id=1, source_target_pairs={{0,4},{4,8},{8,12},{12,16},{16,20},{20,24},{24,28},{28,32},{32,36}... | collective-permute-start | bytes 12296 | tf_op jit(solution)/shard_map/ppermute | solution.py:93
  135.4 9.8 %collective-permute-start.13 = (f32[4,4,64]{2,1,0:T(4,128)S(1)}, f32[4,4,64]{2,1,0:T(4,128)S(1)}, u32[]{:S(2)}, u32[]{:S(2)}) collective-permute-start(f32[4,4,64]{2,1,0:T(4,128)S(1)} %get-tuple-element.112), channel_id=1, source_target_pairs={{4,0},{8,4},{12,8},{16,12},{20,16},{24,20},{28,24},{32,28},{36,32}... | collective-permute-start | bytes 12296 | tf_op jit(solution)/shard_map/ppermute | solution.py:94

commit v4 on v3

--- a/solution.py
+++ b/solution.py
@@ -80,10 +80,6 @@
     count = lax.axis_size(axis)
     if count == 1:
         return jnp.zeros_like(upper), jnp.zeros_like(lower)
-    return neighbours_on(lower, upper, axis, count)
-
-
-def neighbours_on(lower, upper, axis, count):
     if count == 2:
         index = lax.axis_index(axis)
         sent = jnp.where(index == 0, upper, lower)
@@ -95,7 +91,7 @@
     return from_below, from_above
 
 
-def source_from_halo(velocity, viscosity):
+def source_cells(velocity, viscosity):
     below_x, above_x = neighbours(velocity[:, :1], velocity[:, -1:], "gx")
     below_y, above_y = neighbours(velocity[:, :, :1], velocity[:, :, -1:], "gy")
     below_z, above_z = neighbours(velocity[..., :1], velocity[..., -1:], "gz")
@@ -187,7 +183,7 @@
 
 
 def on_device_body(velocity, eddy_viscosity, cell_owner, cell_element, cell_position, acoustic_state):
-    sources = source_from_halo(velocity, eddy_viscosity)
+    sources = source_cells(velocity, eddy_viscosity)
     cell_count = sources.shape[1] * sources.shape[2] * sources.shape[3]
     flat_source = sources.reshape(3, cell_count).astype(jnp.float32)
     owners = cell_owner.reshape(cell_count)

time: 148 us -> 148 us (level)
  no operation moved by 1% of the time
where the time goes in v4:
time: 148 us; the launch traced here: 146 us
  starting transfers between devices  69.9 us (47%)
  other arithmetic  22.7 us (15%)
  local copies, waits for them, and re-layouts  20.2 us (14%)
  waiting for transfers between devices  16.9 us (11%)
  matrix products  14.5 us (10%)
  between operations  2.04 us (1%)
    ppermute x8, starting transfers between devices, neighbours(): got = lax.ppermute(sent, axis, [(0, 1), (1, 0)])  30.2 us
    ppermute x4, starting transfers between devices, neighbours(): lax.ppermute(upper, axis, [(i, i + 1) for i in range(count - 1)])  16.5 us
    ppermute x4, waiting for transfers between devices, neighbours(): lax.ppermute(lower, axis, [(i + 1, i) for i in range(count - 1)])  13 us
    ppermute x4, starting transfers between devices, neighbours(): lax.ppermute(lower, axis, [(i + 1, i) for i in range(count - 1)])  12.8 us
    all_to_all x1, starting transfers between devices, on_device_body(): got = lax.all_to_all(send, 'gx', split_axis=0, concat_axis=0, tiled=True)  10.4 us
    dot_general x9, matrix products, tendency(): grads = [jnp.dot(fields[0], table, precision=highest) for table in tables]  7.43 us
    scatter x1, local copies, waits for them, and re-layouts, on_device_body(): send = jnp.zeros((4, owner_count * capacity), jnp.float32).at[:, slot_ind...  7.16 us
    select_n x5, other arithmetic, neighbours(): sent = jnp.where(index == 0, upper, lower)  4.3 us
  transfers between devices with their start and end apart: 17, of which 3 were waited for; matrix products, arithmetic and copies ran while one was open for 33% of the time, Pallas kernels for 0%

profile of v4, /device:TPU:62, one launch (start us, length us, event | category | flops | bytes accessed | tf_op | source)
XLA Modules:
  0.0 146.2 jit_solution(187407596080932320)
XLA Ops:
  0.6 1.5 slice_select_fusion
  2.1 10.9 %collective-permute-start.3 = (bf16[3,2,8,1]{3,2,1,0:T(8,128)(2,1)}, bf16[3,2,8,1]{3,2,1,0:T(8,128)(2,1)}, u32[]{:S(2)}, u32[]{:S(2)}) collective-permute-start(bf16[3,2,8,1]{3,2,1,0:T(8,128)(2,1)} %slice_select_fusion), channel_id=1, source_target_pairs={{0,1},{1,0},{2,3},{3,2},{4,5},{5,4},{6,7},{7,6},{8,9},{9,8},{10,11... | collective-permute-start | bytes 296 | tf_op jit(solution)/shard_map/ppermute | solution.py:86
  13.0 1.4 broadcast_select_fusion.18
  14.4 1.9 %collective-permute-start.2 = (bf16[3,2,1,128]{3,2,1,0:T(2,128)(2,1)}, bf16[3,2,1,128]{3,2,1,0:T(2,128)(2,1)}, u32[]{:S(2)}, u32[]{:S(2)}) collective-permute-start(bf16[3,2,1,128]{3,2,1,0:T(2,128)(2,1)} %broadcast_select_fusion.18), channel_id=1, source_target_pairs={{0,2},{2,0},{1,3},{3,1},{4,6},{6,4},{5,7},{7,5},{8,10},{10,8},{9,1... | collective-permute-start | bytes 4616 | tf_op jit(solution)/shard_map/ppermute | solution.py:86
  16.3 1.3 fusion.171
  17.6 3.2 %collective-permute-start = (bf16[3,1,8,128]{3,2,1,0:T(8,128)(2,1)}, bf16[3,1,8,128]{3,2,1,0:T(8,128)(2,1)}, u32[]{:S(2)}, u32[]{:S(2)}) collective-permute-start(bf16[3,1,8,128]{3,2,1,0:T(8,128)(2,1)} %get-tuple-element.166), channel_id=1, source_target_pairs={{4,0},{8,4},{12,8},{16,12},{20,16},{24,20},{28,24},{32,28},{36,32}... | collective-permute-start | bytes 18440 | tf_op jit(solution)/shard_map/ppermute | solution.py:90
  20.9 6.8 %collective-permute-start.1 = (bf16[3,1,8,128]{3,2,1,0:T(8,128)(2,1)}, bf16[3,1,8,128]{3,2,1,0:T(8,128)(2,1)}, u32[]{:S(2)}, u32[]{:S(2)}) collective-permute-start(bf16[3,1,8,128]{3,2,1,0:T(8,128)(2,1)} %get-tuple-element.167), channel_id=1, source_target_pairs={{0,4},{4,8},{8,12},{12,16},{16,20},{20,24},{24,28},{28,32},{32,36}... | collective-permute-start | bytes 18440 | tf_op jit(solution)/shard_map/ppermute | solution.py:89
  27.7 1.9 %collective-permute-start.6 = (f32[4,4,512]{2,1,0:T(4,128)}, f32[4,4,512]{2,1,0:T(4,128)S(1)}, u32[]{:S(2)}, u32[]{:S(2)}) collective-permute-start(f32[4,4,512]{2,1,0:T(4,128)} %bitcast.181), channel_id=1, source_target_pairs={{0,2},{2,0},{1,3},{3,1},{4,6},{6,4},{5,7},{7,5},{8,10},{10,8},{9,1... | collective-permute-start | bytes 98312 | tf_op jit(solution)/shard_map/ppermute | solution.py:86
  29.6 0.8 fusion.168
  30.4 0.9 fusion.169
  31.3 0.7 fusion.170
  32.0 1.4 broadcast_select_fusion.12
  33.4 0.8 fusion.166
  34.3 1.4 fusion.167
  35.9 1.2 and_select_fusion.2
  37.1 0.6 fusion.127
  37.7 1.3 fusion.12
  41.7 0.6 fusion.19
  42.3 0.6 compare_select_fusion
  43.5 1.3 fusion.11
  44.7 0.6 convolution_add_fusion.5
  45.9 1.2 fusion.10
  47.2 1.3 fusion.14
  48.5 1.9 %collective-permute-start.7 = (f32[4,1,512]{2,1,0:T(1,128)}, f32[4,1,512]{2,1,0:T(1,128)}, u32[]{:S(2)}, u32[]{:S(2)}) collective-permute-start(f32[4,1,512]{2,1,0:T(1,128)} %broadcast_select_fusion.12), channel_id=1, source_target_pairs={{0,1},{1,0},{2,3},{3,2},{4,5},{5,4},{6,7},{7,6},{8,9},{9,8},{10,11... | collective-permute-start | bytes 24584 | tf_op jit(solution)/shard_map/ppermute | solution.py:86
  50.4 0.7 select_convert_fusion.1
  51.2 2.1 %collective-permute-start.4 = (f32[4,4,64]{2,1,0:T(4,128)}, f32[4,4,64]{2,1,0:T(4,128)S(1)}, u32[]{:S(2)}, u32[]{:S(2)}) collective-permute-start(f32[4,4,64]{2,1,0:T(4,128)} %get-tuple-element.153), channel_id=1, source_target_pairs={{0,4},{4,8},{8,12},{12,16},{16,20},{20,24},{24,28},{28,32},{32,36}... | collective-permute-start | bytes 12296 | tf_op jit(solution)/shard_map/ppermute | solution.py:89
  53.3 0.7 fusion.141
  54.1 3.7 %collective-permute-start.5 = (f32[4,4,64]{2,1,0:T(4,128)}, f32[4,4,64]{2,1,0:T(4,128)}, u32[]{:S(2)}, u32[]{:S(2)}) collective-permute-start(f32[4,4,64]{2,1,0:T(4,128)} %get-tuple-element.152), channel_id=1, source_target_pairs={{4,0},{8,4},{12,8},{16,12},{20,16},{24,20},{28,24},{32,28},{36,32}... | collective-permute-start | bytes 12296 | tf_op jit(solution)/shard_map/ppermute | solution.py:90
  57.8 0.7 convert_element_type.101
  58.5 0.7 convert_element_type.102
  59.4 1.3 copy.34
  60.7 7.2 %scatter_custom_fusion = f32[4,3072]{0,1:T(8,128)} fusion(s32[2048]{0:T(1024)} %bitcast.196, f32[2048,4]{1,0:T(8,128)} %copy.34, f32[]{:T(128)} %constant.244.clone.1), kind=kCustom, calls=%fused_computation.61 | custom fusion | bytes 49664 | tf_op jit(solution)/shard_map/scatter | solution.py:206
  67.9 1.9 %copy.35 = f32[4,128,24]{1,2,0:T(8,128)S(1)} copy(f32[4,128,24]{0,2,1:T(8,128)} %bitcast.180) | data formatting | bytes 98304 | tf_op jit(solution)/shard_map/reshape | solution.py:207
  69.8 0.7 copy.36
  70.5 10.4 %all-to-all-start = ((f32[128,1,96]{2,1,0:T(1,128)}), f32[128,1,96]{2,1,0:T(1,128)S(1)}, u32[]{:S(2)}, u32[]{:S(2)}) async-start(f32[128,1,96]{2,1,0:T(1,128)} %copy.36), calls=%async_computation | async-start | bytes 131072 | tf_op jit(solution)/shard_map/all_to_all | solution.py:210
  80.9 0.7 broadcast_select_fusion.11
  82.0 0.9 broadcast_multiply_fusion.13
  82.8 0.7 fusion.115
  83.5 0.6 fusion.111
  84.1 0.6 fusion.119
  85.9 3.9 %all-to-all-done = f32[128,1,96]{2,1,0:T(1,128)S(1)} async-done(((f32[128,1,96]{2,1,0:T(1,128)}), f32[128,1,96]{2,1,0:T(1,128)S(1)}, u32[]{:S(2)}, u32[]{:S(2)}) %all-to-all-start) | async-done | bytes 49184 | tf_op jit(solution)/shard_map/all_to_all | solution.py:210
  90.3 0.6 iota_compare_fusion.6
  91.2 0.8 broadcast_select_fusion
  92.0 1.6 %select_reduce_fusion.2 = (f32[8,3072]{1,0:T(8,128)S(1)}, f32[8,3072]{1,0:T(8,128)S(1)}, f32[8,3072]{1,0:T(8,128)S(1)}) fusion(f32[8,16]{1,0:T(8,128)} %constant.276.clone, pred[16,3072]{1,0:T(8,128)(4,1)S(1)} %iota_compare_fusion.5, pred[16,3072]{1,0:T(8,128)(4,1)S(1)} %iota_compare_fusion.4, pred[16,3072]{1,0:T(8,128)(4,1)S(1)} %iota_compare_fusion.3), kind=kLoop, calls=%fused_computation.14 | loop fusion | flops 2285568 | bytes 442880 | tf_op jit(solution)/shard_map/reduce_sum | solution.py:182
  94.5 0.9 convolution_multiply_fusion
  95.7 0.8 fusion.26
  96.5 1.9 %collective-permute-start.10 = (f32[4,4,512]{2,1,0:T(4,128)S(1)}, f32[4,4,512]{2,1,0:T(4,128)S(1)}, u32[]{:S(2)}, u32[]{:S(2)}) collective-permute-start(f32[4,4,512]{2,1,0:T(4,128)S(1)} %fusion.26), channel_id=1, source_target_pairs={{0,2},{2,0},{1,3},{3,1},{4,6},{6,4},{5,7},{7,5},{8,10},{10,8},{9,1... | collective-permute-start | bytes 98312 | tf_op jit(solution)/shard_map/ppermute | solution.py:86
  99.2 0.6 fusion.7
  99.8 0.6 fusion.6
  100.4 7.8 %collective-permute-start.11 = (f32[4,1,512]{2,1,0:T(1,128)S(1)}, f32[4,1,512]{2,1,0:T(1,128)S(1)}, u32[]{:S(2)}, u32[]{:S(2)}) collective-permute-start(f32[4,1,512]{2,1,0:T(1,128)S(1)} %broadcast_select_fusion.10), channel_id=1, source_target_pairs={{0,1},{1,0},{2,3},{3,2},{4,5},{5,4},{6,7},{7,6},{8,9},{9,8},{10,11... | collective-permute-start | bytes 24584 | tf_op jit(solution)/shard_map/ppermute | solution.py:86
  109.4 0.6 fusion.5
  110.0 5.6 %collective-permute-start.8 = (f32[4,4,64]{2,1,0:T(4,128)S(1)}, f32[4,4,64]{2,1,0:T(4,128)S(1)}, u32[]{:S(2)}, u32[]{:S(2)}) collective-permute-start(f32[4,4,64]{2,1,0:T(4,128)S(1)} %get-tuple-element.133), channel_id=1, source_target_pairs={{0,4},{4,8},{8,12},{12,16},{16,20},{20,24},{24,28},{28,32},{32,36}... | collective-permute-start | bytes 12296 | tf_op jit(solution)/shard_map/ppermute | solution.py:89
  115.7 1.9 %collective-permute-start.9 = (f32[4,4,64]{2,1,0:T(4,128)S(1)}, f32[4,4,64]{2,1,0:T(4,128)S(1)}, u32[]{:S(2)}, u32[]{:S(2)}) collective-permute-start(f32[4,4,64]{2,1,0:T(4,128)S(1)} %get-tuple-element.132), channel_id=1, source_target_pairs={{4,0},{8,4},{12,8},{16,12},{20,16},{24,20},{28,24},{32,28},{36,32}... | collective-permute-start | bytes 12296 | tf_op jit(solution)/shard_map/ppermute | solution.py:90
  118.0 7.5 %collective-permute-done.9 = f32[4,4,64]{2,1,0:T(4,128)S(1)} collective-permute-done((f32[4,4,64]{2,1,0:T(4,128)S(1)}, f32[4,4,64]{2,1,0:T(4,128)S(1)}, u32[]{:S(2)}, u32[]{:S(2)}) %collective-permute-start.9) | collective-permute-done | bytes 4128 | tf_op jit(solution)/shard_map/ppermute | solution.py:90
  125.9 1.9 %collective-permute-start.14 = (f32[4,4,512]{2,1,0:T(4,128)S(1)}, f32[4,4,512]{2,1,0:T(4,128)S(1)}, u32[]{:S(2)}, u32[]{:S(2)}) collective-permute-start(f32[4,4,512]{2,1,0:T(4,128)S(1)} %fusion.30), channel_id=1, source_target_pairs={{0,2},{2,0},{1,3},{3,1},{4,6},{6,4},{5,7},{7,5},{8,10},{10,8},{9,1... | collective-permute-start | bytes 98312 | tf_op jit(solution)/shard_map/ppermute | solution.py:86
  128.5 0.6 fusion.2
  129.1 0.6 fusion.1
  129.8 1.9 %collective-permute-start.15 = (f32[4,1,512]{2,1,0:T(1,128)S(1)}, f32[4,1,512]{2,1,0:T(1,128)S(1)}, u32[]{:S(2)}, u32[]{:S(2)}) collective-permute-start(f32[4,1,512]{2,1,0:T(1,128)S(1)} %broadcast_select_fusion.8), channel_id=1, source_target_pairs={{0,1},{1,0},{2,3},{3,2},{4,5},{5,4},{6,7},{7,6},{8,9},{9,8},{10,11... | collective-permute-start | bytes 24584 | tf_op jit(solution)/shard_map/ppermute | solution.py:86
  132.3 0.6 fusion.4
  132.9 0.6 fusion
  133.5 1.9 %collective-permute-start.12 = (f32[4,4,64]{2,1,0:T(4,128)S(1)}, f32[4,4,64]{2,1,0:T(4,128)S(1)}, u32[]{:S(2)}, u32[]{:S(2)}) collective-permute-start(f32[4,4,64]{2,1,0:T(4,128)S(1)} %get-tuple-element.113), channel_id=1, source_target_pairs={{0,4},{4,8},{8,12},{12,16},{16,20},{20,24},{24,28},{28,32},{32,36}... | collective-permute-start | bytes 12296 | tf_op jit(solution)/shard_map/ppermute | solution.py:89
  135.4 3.9 %collective-permute-start.13 = (f32[4,4,64]{2,1,0:T(4,128)S(1)}, f32[4,4,64]{2,1,0:T(4,128)S(1)}, u32[]{:S(2)}, u32[]{:S(2)}) collective-permute-start(f32[4,4,64]{2,1,0:T(4,128)S(1)} %get-tuple-element.112), channel_id=1, source_target_pairs={{4,0},{8,4},{12,8},{16,12},{20,16},{24,20},{28,24},{32,28},{36,32}... | collective-permute-start | bytes 12296 | tf_op jit(solution)/shard_map/ppermute | solution.py:90
  139.7 5.5 %collective-permute-done.13 = f32[4,4,64]{2,1,0:T(4,128)S(1)} collective-permute-done((f32[4,4,64]{2,1,0:T(4,128)S(1)}, f32[4,4,64]{2,1,0:T(4,128)S(1)}, u32[]{:S(2)}, u32[]{:S(2)}) %collective-permute-start.13) | collective-permute-done | bytes 4128 | tf_op jit(solution)/shard_map/ppermute | solution.py:90
  145.5 0.7 fusion.35
  (205 shorter events, 11.4 us)
Async XLA Ops:
  0.6 36.5 %copy-start.1 = (f32[4,1,1,4,512]{4,3,2,1,0:T(4,128)S(1)}, f32[4,1,1,4,512]{4,3,2,1,0:T(4,128)}, u32[]{:S(2)}) copy-start(f32[4,1,1,4,512]{4,3,2,1,0:T(4,128)} %param.15) | copy-start | bytes 98308
  2.1 46.4 %collective-permute-start.3 = (bf16[3,2,8,1]{3,2,1,0:T(8,128)(2,1)}, bf16[3,2,8,1]{3,2,1,0:T(8,128)(2,1)}, u32[]{:S(2)}, u32[]{:S(2)}) collective-permute-start(bf16[3,2,8,1]{3,2,1,0:T(8,128)(2,1)} %slice_select_fusion), channel_id=1, source_target_pairs={{0,1},{1,0},{2,3},{3,2},{4,5},{5,4},{6,7},{7,6},{8,9},{9,8},{10,11... | collective-permute-start | bytes 296 | tf_op jit(solution)/shard_map/ppermute | solution.py:86
  14.4 36.8 %collective-permute-start.2 = (bf16[3,2,1,128]{3,2,1,0:T(2,128)(2,1)}, bf16[3,2,1,128]{3,2,1,0:T(2,128)(2,1)}, u32[]{:S(2)}, u32[]{:S(2)}) collective-permute-start(bf16[3,2,1,128]{3,2,1,0:T(2,128)(2,1)} %broadcast_select_fusion.18), channel_id=1, source_target_pairs={{0,2},{2,0},{1,3},{3,1},{4,6},{6,4},{5,7},{7,5},{8,10},{10,8},{9,1... | collective-permute-start | bytes 4616 | tf_op jit(solution)/shard_map/ppermute | solution.py:86
  17.6 36.5 %collective-permute-start = (bf16[3,1,8,128]{3,2,1,0:T(8,128)(2,1)}, bf16[3,1,8,128]{3,2,1,0:T(8,128)(2,1)}, u32[]{:S(2)}, u32[]{:S(2)}) collective-permute-start(bf16[3,1,8,128]{3,2,1,0:T(8,128)(2,1)} %get-tuple-element.166), channel_id=1, source_target_pairs={{4,0},{8,4},{12,8},{16,12},{20,16},{24,20},{28,24},{32,28},{36,32}... | collective-permute-start | bytes 18440 | tf_op jit(solution)/shard_map/ppermute | solution.py:90
  20.9 37.6 %collective-permute-start.1 = (bf16[3,1,8,128]{3,2,1,0:T(8,128)(2,1)}, bf16[3,1,8,128]{3,2,1,0:T(8,128)(2,1)}, u32[]{:S(2)}, u32[]{:S(2)}) collective-permute-start(bf16[3,1,8,128]{3,2,1,0:T(8,128)(2,1)} %get-tuple-element.167), channel_id=1, source_target_pairs={{0,4},{4,8},{8,12},{12,16},{16,20},{20,24},{24,28},{28,32},{32,36}... | collective-permute-start | bytes 18440 | tf_op jit(solution)/shard_map/ppermute | solution.py:89
  27.7 54.1 %collective-permute-start.6 = (f32[4,4,512]{2,1,0:T(4,128)}, f32[4,4,512]{2,1,0:T(4,128)S(1)}, u32[]{:S(2)}, u32[]{:S(2)}) collective-permute-start(f32[4,4,512]{2,1,0:T(4,128)} %bitcast.181), channel_id=1, source_target_pairs={{0,2},{2,0},{1,3},{3,1},{4,6},{6,4},{5,7},{7,5},{8,10},{10,8},{9,1... | collective-permute-start | bytes 98312 | tf_op jit(solution)/shard_map/ppermute | solution.py:86
  35.8 1.3 copy-start.28
  35.8 7.2 %copy-start.26 = (s32[512]{0:T(512)}, s32[512]{0:T(512)S(1)}, u32[]{:S(2)}) copy-start(s32[512]{0:T(512)S(1)} %get-tuple-element.188) | copy-start | bytes 6148
  35.8 1.3 copy-start.43
  35.8 7.1 %copy-start.41 = (pred[512]{0:T(512)(128)(4,1)}, pred[512]{0:T(512)(128)(4,1)S(1)}, u32[]{:S(2)}) copy-start(pred[512]{0:T(512)(128)(4,1)S(1)} %get-tuple-element.186) | copy-start | bytes 1540
  35.9 4.9 %copy-start.3 = (s32[1,1,2048,1]{2,3,1,0:T(1,128)S(1)}, s32[1,1,2048,1]{2,3,1,0:T(1,128)}, u32[]{:S(2)}) copy-start(s32[1,1,2048,1]{2,3,1,0:T(1,128)} %param.12) | copy-start | bytes 24580
  41.3 1.6 %copy-start.31 = (f32[8,512]{1,0:T(8,128)S(1)}, f32[8,512]{1,0:T(8,128)}, u32[]{:S(2)}) copy-start(f32[8,512]{1,0:T(8,128)} %constant.278.clone) | copy-start | bytes 49156
  42.9 2.4 %copy-start.29 = (s32[512]{0:T(512)S(1)}, s32[512]{0:T(512)}, u32[]{:S(2)}) copy-start(s32[512]{0:T(512)} %copy-done.28) | copy-start | bytes 6148
  42.9 2.4 %copy-start.30 = (f32[8,512]{1,0:T(8,128)S(1)}, f32[8,512]{1,0:T(8,128)}, u32[]{:S(2)}) copy-start(f32[8,512]{1,0:T(8,128)} %constant.279.clone) | copy-start | bytes 49156
  43.0 2.4 %copy-start.44 = (pred[512]{0:T(512)(128)(4,1)S(1)}, pred[512]{0:T(512)(128)(4,1)}, u32[]{:S(2)}) copy-start(pred[512]{0:T(512)(128)(4,1)} %copy-done.43) | copy-start | bytes 1540
  43.4 1.9 %copy-start.27 = (s32[512]{0:T(512)S(1)}, s32[512]{0:T(512)}, u32[]{:S(2)}) copy-start(s32[512]{0:T(512)} %copy-done.26) | copy-start | bytes 6148
  43.5 1.9 %copy-start.42 = (pred[512]{0:T(512)(128)(4,1)S(1)}, pred[512]{0:T(512)(128)(4,1)}, u32[]{:S(2)}) copy-start(pred[512]{0:T(512)(128)(4,1)} %copy-done.41) | copy-start | bytes 1540
  45.4 3.0 %copy-start.32 = (s32[1,1,2048]{2,1,0:T(1,128)S(1)}, s32[1,1,2048]{2,1,0:T(1,128)}, u32[]{:S(2)}) copy-start(s32[1,1,2048]{2,1,0:T(1,128)} %param.14) | copy-start | bytes 24580
  45.4 3.0 %copy-start.33 = (s32[1,1,2048]{2,1,0:T(1,128)S(1)}, s32[1,1,2048]{2,1,0:T(1,128)}, u32[]{:S(2)}) copy-start(s32[1,1,2048]{2,1,0:T(1,128)} %param.13) | copy-start | bytes 24580
  45.4 3.0 %copy-start = (bf16[3,2,8,128]{3,2,1,0:T(8,128)(2,1)S(1)}, bf16[3,2,8,128]{3,2,1,0:T(8,128)(2,1)}, u32[]{:S(2)}) copy-start(bf16[3,2,8,128]{3,2,1,0:T(8,128)(2,1)} %param.10) | copy-start | bytes 36868
  45.9 13.3 %copy-start.34 = (f32[2,8,128]{2,1,0:T(8,128)S(1)}, f32[2,8,128]{2,1,0:T(8,128)}, u32[]{:S(2)}) copy-start(f32[2,8,128]{2,1,0:T(8,128)} %param.11) | copy-start | bytes 24580
  48.5 32.4 %collective-permute-start.7 = (f32[4,1,512]{2,1,0:T(1,128)}, f32[4,1,512]{2,1,0:T(1,128)}, u32[]{:S(2)}, u32[]{:S(2)}) collective-permute-start(f32[4,1,512]{2,1,0:T(1,128)} %broadcast_select_fusion.12), channel_id=1, source_target_pairs={{0,1},{1,0},{2,3},{3,2},{4,5},{5,4},{6,7},{7,6},{8,9},{9,8},{10,11... | collective-permute-start | bytes 24584 | tf_op jit(solution)/shard_map/ppermute | solution.py:86
  51.2 30.8 %collective-permute-start.4 = (f32[4,4,64]{2,1,0:T(4,128)}, f32[4,4,64]{2,1,0:T(4,128)S(1)}, u32[]{:S(2)}, u32[]{:S(2)}) collective-permute-start(f32[4,4,64]{2,1,0:T(4,128)} %get-tuple-element.153), channel_id=1, source_target_pairs={{0,4},{4,8},{8,12},{12,16},{16,20},{20,24},{24,28},{28,32},{32,36}... | collective-permute-start | bytes 12296 | tf_op jit(solution)/shard_map/ppermute | solution.py:89
  54.1 27.9 %collective-permute-start.5 = (f32[4,4,64]{2,1,0:T(4,128)}, f32[4,4,64]{2,1,0:T(4,128)}, u32[]{:S(2)}, u32[]{:S(2)}) collective-permute-start(f32[4,4,64]{2,1,0:T(4,128)} %get-tuple-element.152), channel_id=1, source_target_pairs={{4,0},{8,4},{12,8},{16,12},{20,16},{24,20},{28,24},{32,28},{36,32}... | collective-permute-start | bytes 12296 | tf_op jit(solution)/shard_map/ppermute | solution.py:90
  70.5 19.3 %all-to-all-start = ((f32[128,1,96]{2,1,0:T(1,128)}), f32[128,1,96]{2,1,0:T(1,128)S(1)}, u32[]{:S(2)}, u32[]{:S(2)}) async-start(f32[128,1,96]{2,1,0:T(1,128)} %copy.36), calls=%async_computation | async-start | bytes 131072 | tf_op jit(solution)/shard_map/all_to_all | solution.py:210
  94.2 1.2 copy-start.4
  94.2 1.2 copy-start.5
  94.3 1.2 copy-start.6
  94.3 1.2 copy-start.7
  94.3 1.2 copy-start.8
  94.3 1.2 copy-start.9
  94.3 1.2 copy-start.10
  94.3 1.2 copy-start.11
  94.3 1.2 copy-start.12
  94.3 1.2 copy-start.13
  94.3 1.2 copy-start.14
  94.3 1.2 copy-start.15
  94.4 1.2 copy-start.16
  94.4 1.2 copy-start.17
  94.4 1.2 copy-start.18
  94.4 1.2 copy-start.19
  94.4 1.2 copy-start.20
  94.4 1.2 copy-start.21
  94.4 1.2 copy-start.22
  94.4 1.2 copy-start.23
  94.4 1.2 copy-start.24
  94.4 1.2 copy-start.25
  94.5 1.2 copy-start.35
  94.5 1.2 copy-start.36
  94.5 1.2 copy-start.37
  94.5 1.2 copy-start.38
  95.4 4.9 %copy-start.2 = (f32[3,4,512]{2,1,0:T(4,128)}, f32[3,4,512]{2,1,0:T(4,128)S(1)}, u32[]{:S(2)}) copy-start(f32[3,4,512]{2,1,0:T(4,128)S(1)} %reshape.4564) | copy-start | bytes 73732
  96.5 21.2 %collective-permute-start.10 = (f32[4,4,512]{2,1,0:T(4,128)S(1)}, f32[4,4,512]{2,1,0:T(4,128)S(1)}, u32[]{:S(2)}, u32[]{:S(2)}) collective-permute-start(f32[4,4,512]{2,1,0:T(4,128)S(1)} %fusion.26), channel_id=1, source_target_pairs={{0,2},{2,0},{1,3},{3,1},{4,6},{6,4},{5,7},{7,5},{8,10},{10,8},{9,1... | collective-permute-start | bytes 98312 | tf_op jit(solution)/shard_map/ppermute | solution.py:86
  100.4 17.2 %collective-permute-start.11 = (f32[4,1,512]{2,1,0:T(1,128)S(1)}, f32[4,1,512]{2,1,0:T(1,128)S(1)}, u32[]{:S(2)}, u32[]{:S(2)}) collective-permute-start(f32[4,1,512]{2,1,0:T(1,128)S(1)} %broadcast_select_fusion.10), channel_id=1, source_target_pairs={{0,1},{1,0},{2,3},{3,2},{4,5},{5,4},{6,7},{7,6},{8,9},{9,8},{10,11... | collective-permute-start | bytes 24584 | tf_op jit(solution)/shard_map/ppermute | solution.py:86
  108.8 16.9 %copy-start.39 = (pred[512]{0:T(512)(128)(4,1)S(1)}, pred[512]{0:T(512)(128)(4,1)}, u32[]{:S(2)}) copy-start(pred[512]{0:T(512)(128)(4,1)} %get-tuple-element.206) | copy-start | bytes 1540
  108.8 16.9 %copy-start.40 = (pred[512]{0:T(512)(128)(4,1)S(1)}, pred[512]{0:T(512)(128)(4,1)}, u32[]{:S(2)}) copy-start(pred[512]{0:T(512)(128)(4,1)} %get-tuple-element.207) | copy-start | bytes 1540
  110.0 7.9 %collective-permute-start.8 = (f32[4,4,64]{2,1,0:T(4,128)S(1)}, f32[4,4,64]{2,1,0:T(4,128)S(1)}, u32[]{:S(2)}, u32[]{:S(2)}) collective-permute-start(f32[4,4,64]{2,1,0:T(4,128)S(1)} %get-tuple-element.133), channel_id=1, source_target_pairs={{0,4},{4,8},{8,12},{12,16},{16,20},{20,24},{24,28},{28,32},{32,36}... | collective-permute-start | bytes 12296 | tf_op jit(solution)/shard_map/ppermute | solution.py:89
  115.7 9.8 %collective-permute-start.9 = (f32[4,4,64]{2,1,0:T(4,128)S(1)}, f32[4,4,64]{2,1,0:T(4,128)S(1)}, u32[]{:S(2)}, u32[]{:S(2)}) collective-permute-start(f32[4,4,64]{2,1,0:T(4,128)S(1)} %get-tuple-element.132), channel_id=1, source_target_pairs={{4,0},{8,4},{12,8},{16,12},{20,16},{24,20},{28,24},{32,28},{36,32}... | collective-permute-start | bytes 12296 | tf_op jit(solution)/shard_map/ppermute | solution.py:90
  125.9 13.6 %collective-permute-start.14 = (f32[4,4,512]{2,1,0:T(4,128)S(1)}, f32[4,4,512]{2,1,0:T(4,128)S(1)}, u32[]{:S(2)}, u32[]{:S(2)}) collective-permute-start(f32[4,4,512]{2,1,0:T(4,128)S(1)} %fusion.30), channel_id=1, source_target_pairs={{0,2},{2,0},{1,3},{3,1},{4,6},{6,4},{5,7},{7,5},{8,10},{10,8},{9,1... | collective-permute-start | bytes 98312 | tf_op jit(solution)/shard_map/ppermute | solution.py:86
  129.8 9.6 %collective-permute-start.15 = (f32[4,1,512]{2,1,0:T(1,128)S(1)}, f32[4,1,512]{2,1,0:T(1,128)S(1)}, u32[]{:S(2)}, u32[]{:S(2)}) collective-permute-start(f32[4,1,512]{2,1,0:T(1,128)S(1)} %broadcast_select_fusion.8), channel_id=1, source_target_pairs={{0,1},{1,0},{2,3},{3,2},{4,5},{5,4},{6,7},{7,6},{8,9},{9,8},{10,11... | collective-permute-start | bytes 24584 | tf_op jit(solution)/shard_map/ppermute | solution.py:86
  133.5 6.2 %collective-permute-start.12 = (f32[4,4,64]{2,1,0:T(4,128)S(1)}, f32[4,4,64]{2,1,0:T(4,128)S(1)}, u32[]{:S(2)}, u32[]{:S(2)}) collective-permute-start(f32[4,4,64]{2,1,0:T(4,128)S(1)} %get-tuple-element.113), channel_id=1, source_target_pairs={{0,4},{4,8},{8,12},{12,16},{16,20},{20,24},{24,28},{28,32},{32,36}... | collective-permute-start | bytes 12296 | tf_op jit(solution)/shard_map/ppermute | solution.py:89
  135.4 9.8 %collective-permute-start.13 = (f32[4,4,64]{2,1,0:T(4,128)S(1)}, f32[4,4,64]{2,1,0:T(4,128)S(1)}, u32[]{:S(2)}, u32[]{:S(2)}) collective-permute-start(f32[4,4,64]{2,1,0:T(4,128)S(1)} %get-tuple-element.112), channel_id=1, source_target_pairs={{4,0},{8,4},{12,8},{16,12},{20,16},{24,20},{28,24},{32,28},{36,32}... | collective-permute-start | bytes 12296 | tf_op jit(solution)/shard_map/ppermute | solution.py:90

commit v5 on v4

--- a/solution.py
+++ b/solution.py
@@ -129,14 +129,13 @@
 
 
 def tendency(fields, tables):
-    highest = lax.Precision.HIGHEST
+    precision = lax.Precision.HIGH
     count = fields.shape[1]
-    grads = [jnp.dot(fields[0], table, precision=highest) for table in tables]
-    divergence = (
-        jnp.dot(fields[1], tables[0], precision=highest)
-        + jnp.dot(fields[2], tables[1], precision=highest)
-        + jnp.dot(fields[3], tables[2], precision=highest)
-    )
+    grad_table, div_table = tables
+    grads = jnp.dot(fields[0], grad_table, precision=precision)
+    grads = [grads[:, k * NODES : (k + 1) * NODES] for k in range(3)]
+    velocity_rows = jnp.concatenate([fields[1], fields[2], fields[3]], axis=1)
+    divergence = jnp.dot(velocity_rows, div_table, precision=precision)
     result = jnp.stack([-divergence, -grads[0], -grads[1], -grads[2]])
 
     face = 64
@@ -167,7 +166,8 @@
 
 
 def runge_kutta(fields, forcing):
-    tables = kron_tables()
+    parts = kron_tables()
+    tables = (jnp.concatenate(parts, axis=1), jnp.concatenate(parts, axis=0))
     coupled = jnp.concatenate([jnp.zeros_like(forcing[:1]), COUPLING * forcing])
     step = lambda f: tendency(f, tables) + coupled
     first = tendency(fields, tables)
@@ -191,13 +191,13 @@
     positions = cell_position.reshape(cell_count)
     owner_count = lax.axis_size("gx")
     capacity = 3 * cell_count // (2 * owner_count)
+    subcells = SUB * SUB * SUB
     owner_hot = (owners[:, None] == jnp.arange(owner_count, dtype=jnp.int32)[None, :]).astype(
         jnp.int32
     )
     earlier = jnp.cumsum(owner_hot, axis=0) - owner_hot
     order_within = jnp.sum(earlier * owner_hot, axis=1)
     slot_index = owners * capacity + order_within
-    subcells = SUB * SUB * SUB
     ident = (elements * subcells + positions).astype(jnp.float32)
     payload = jnp.concatenate([flat_source, ident[None]], axis=0)
     send = (

time: 148 us -> 125 us (0.84)
  other arithmetic: 22.7 us -> 9.73 us
  matrix products: 14.5 us -> 6.24 us
  local copies, waits for them, and re-layouts: 20.2 us -> 16.9 us
  waiting for transfers between devices: 16.9 us -> 19.5 us
    dot_general x18 -> x6, matrix products: 13.6 us -> 5.32 us  [the longest x3 2.73 us: tendency(): divergence = jnp.dot(velocity_rows, div_table, precision=precision)]
    all_to_all x1, waiting for transfers between devices: 3.9 us -> 8.28 us  [on_device_body(): got = lax.all_to_all(send, 'gx', split_axis=0, concat_axis=0, tiled=True)]
    convert_element_type x4, other arithmetic: 2.8 us -> 0.03 us  [source_cells(): f32 = lambda t: t.astype(jnp.float32)]
    ppermute x4, waiting for transfers between devices: 13 us -> 10.4 us  [neighbours(): lax.ppermute(lower, axis, [(i + 1, i) for i in range(count - 1)])]
    add x15, other arithmetic: 2.02 us -> 0.16 us  [face_correction(): first = result[0] + 0.5 * normal * difference[component]]
    select_n x5, other arithmetic: 4.3 us -> 2.53 us  [neighbours(): sent = jnp.where(index == 0, upper, lower)]
  transfers between devices with their start and end apart: 17 -> 17, of which waited for: 3 -> 4; matrix products, arithmetic and copies ran while one was open for 33% -> 21% of each run, Pallas kernels for 0% -> 0%
where the time goes in v5:
time: 125 us; the launch traced here: 124 us
  starting transfers between devices  70.1 us (56%)
  waiting for transfers between devices  19.5 us (16%)
  local copies, waits for them, and re-layouts  16.9 us (14%)
  other arithmetic  9.73 us (8%)
  matrix products  6.24 us (5%)
  between operations  1.71 us (1%)
    ppermute x8, starting transfers between devices, neighbours(): got = lax.ppermute(sent, axis, [(0, 1), (1, 0)])  30.4 us
    ppermute x4, starting transfers between devices, neighbours(): lax.ppermute(upper, axis, [(i, i + 1) for i in range(count - 1)])  16.5 us
    ppermute x4, starting transfers between devices, neighbours(): lax.ppermute(lower, axis, [(i + 1, i) for i in range(count - 1)])  12.8 us
    ppermute x4, waiting for transfers between devices, neighbours(): lax.ppermute(lower, axis, [(i + 1, i) for i in range(count - 1)])  10.4 us
    all_to_all x1, starting transfers between devices, on_device_body(): got = lax.all_to_all(send, 'gx', split_axis=0, concat_axis=0, tiled=True)  10.4 us
    all_to_all x1, waiting for transfers between devices, on_device_body(): got = lax.all_to_all(send, 'gx', split_axis=0, concat_axis=0, tiled=True)  8.28 us
    scatter x1, local copies, waits for them, and re-layouts, on_device_body(): send = jnp.zeros((4, owner_count * capacity), jnp.float32).at[:, slot_ind...  6.35 us
    dot_general x3, matrix products, tendency(): divergence = jnp.dot(velocity_rows, div_table, precision=precision)  2.73 us
  transfers between devices with their start and end apart: 17, of which 4 were waited for; matrix products, arithmetic and copies ran while one was open for 21% of the time, Pallas kernels for 0%

profile of v5, /device:TPU:62, one launch (start us, length us, event | category | flops | bytes accessed | tf_op | source)
XLA Modules:
  0.0 124.2 jit_solution(7804694010492515801)
XLA Ops:
  0.6 0.9 slice_select_fusion
  1.5 10.9 %collective-permute-start.3 = (bf16[3,2,8,1]{3,2,1,0:T(8,128)(2,1)S(1)}, bf16[3,2,8,1]{3,2,1,0:T(8,128)(2,1)S(1)}, u32[]{:S(2)}, u32[]{:S(2)}) collective-permute-start(bf16[3,2,8,1]{3,2,1,0:T(8,128)(2,1)S(1)} %slice_select_fusion), channel_id=1, source_target_pairs={{0,1},{1,0},{2,3},{3,2},{4,5},{5,4},{6,7},{7,6},{8,9},{9,8},{10,11... | collective-permute-start | bytes 296 | tf_op jit(solution)/shard_map/ppermute | solution.py:86
  12.4 0.8 broadcast_select_fusion.18
  13.2 1.9 %collective-permute-start.2 = (bf16[3,2,1,128]{3,2,1,0:T(2,128)(2,1)S(1)}, bf16[3,2,1,128]{3,2,1,0:T(2,128)(2,1)S(1)}, u32[]{:S(2)}, u32[]{:S(2)}) collective-permute-start(bf16[3,2,1,128]{3,2,1,0:T(2,128)(2,1)S(1)} %broadcast_select_fusion.18), channel_id=1, source_target_pairs={{0,2},{2,0},{1,3},{3,1},{4,6},{6,4},{5,7},{7,5},{8,10},{10,8},{9,1... | collective-permute-start | bytes 4616 | tf_op jit(solution)/shard_map/ppermute | solution.py:86
  15.2 0.7 fusion.177
  15.9 3.2 %collective-permute-start = (bf16[3,1,8,128]{3,2,1,0:T(8,128)(2,1)S(1)}, bf16[3,1,8,128]{3,2,1,0:T(8,128)(2,1)S(1)}, u32[]{:S(2)}, u32[]{:S(2)}) collective-permute-start(bf16[3,1,8,128]{3,2,1,0:T(8,128)(2,1)S(1)} %get-tuple-element.184), channel_id=1, source_target_pairs={{4,0},{8,4},{12,8},{16,12},{20,16},{24,20},{28,24},{32,28},{36,32}... | collective-permute-start | bytes 18440 | tf_op jit(solution)/shard_map/ppermute | solution.py:90
  19.1 6.8 %collective-permute-start.1 = (bf16[3,1,8,128]{3,2,1,0:T(8,128)(2,1)S(1)}, bf16[3,1,8,128]{3,2,1,0:T(8,128)(2,1)S(1)}, u32[]{:S(2)}, u32[]{:S(2)}) collective-permute-start(bf16[3,1,8,128]{3,2,1,0:T(8,128)(2,1)S(1)} %get-tuple-element.185), channel_id=1, source_target_pairs={{0,4},{4,8},{8,12},{12,16},{16,20},{20,24},{24,28},{28,32},{32,36}... | collective-permute-start | bytes 18440 | tf_op jit(solution)/shard_map/ppermute | solution.py:89
  25.9 1.9 %collective-permute-start.6 = (f32[4,4,512]{2,1,0:T(4,128)}, f32[4,4,512]{2,1,0:T(4,128)S(1)}, u32[]{:S(2)}, u32[]{:S(2)}) collective-permute-start(f32[4,4,512]{2,1,0:T(4,128)} %bitcast.125), channel_id=1, source_target_pairs={{0,2},{2,0},{1,3},{3,1},{4,6},{6,4},{5,7},{7,5},{8,10},{10,8},{9,1... | collective-permute-start | bytes 98312 | tf_op jit(solution)/shard_map/ppermute | solution.py:86
  27.9 0.8 fusion.174
  28.7 0.9 fusion.175
  29.5 0.7 fusion.176
  30.2 0.8 broadcast_select_fusion.12
  31.1 0.8 fusion.172
  31.9 0.8 fusion.173
  32.8 0.7 slice_bitcast_fusion.13
  33.5 0.6 broadcast_compare_fusion
  34.1 0.8 copy.32
  34.9 0.3 fusion.16
  35.4 0.3 copy.33
  35.7 0.6 fusion.15
  36.4 0.8 bitcast_select_fusion.2
  37.3 0.8 convolution_bitcast_fusion
  38.2 1.0 fusion.6
  39.3 1.9 %collective-permute-start.7 = (f32[4,1,512]{2,1,0:T(1,128)S(1)}, f32[4,1,512]{2,1,0:T(1,128)S(1)}, u32[]{:S(2)}, u32[]{:S(2)}) collective-permute-start(f32[4,1,512]{2,1,0:T(1,128)S(1)} %broadcast_select_fusion.12), channel_id=1, source_target_pairs={{0,1},{1,0},{2,3},{3,2},{4,5},{5,4},{6,7},{7,6},{8,9},{9,8},{10,11... | collective-permute-start | bytes 24584 | tf_op jit(solution)/shard_map/ppermute | solution.py:86
  41.2 2.1 %collective-permute-start.4 = (f32[4,4,64]{2,1,0:T(4,128)S(1)}, f32[4,4,64]{2,1,0:T(4,128)S(1)}, u32[]{:S(2)}, u32[]{:S(2)}) collective-permute-start(f32[4,4,64]{2,1,0:T(4,128)S(1)} %get-tuple-element.159), channel_id=1, source_target_pairs={{0,4},{4,8},{8,12},{12,16},{16,20},{20,24},{24,28},{28,32},{32,36}... | collective-permute-start | bytes 12296 | tf_op jit(solution)/shard_map/ppermute | solution.py:89
  43.4 0.1 subtract_multiply_fusion
  43.5 3.7 %collective-permute-start.5 = (f32[4,4,64]{2,1,0:T(4,128)S(1)}, f32[4,4,64]{2,1,0:T(4,128)S(1)}, u32[]{:S(2)}, u32[]{:S(2)}) collective-permute-start(f32[4,4,64]{2,1,0:T(4,128)S(1)} %get-tuple-element.158), channel_id=1, source_target_pairs={{4,0},{8,4},{12,8},{16,12},{20,16},{24,20},{28,24},{32,28},{36,32}... | collective-permute-start | bytes 12296 | tf_op jit(solution)/shard_map/ppermute | solution.py:90
  47.3 0.1 convert_bitcast_fusion
  47.4 1.3 %copy.34 = f32[2048,4]{1,0:T(8,128)} copy(f32[2048,4]{0,1:T(4,128)S(1)} %maximum_bitcast_fusion) | data formatting | bytes 65536 | tf_op jit(solution)/shard_map/concatenate | solution.py:202
  48.8 6.3 %scatter_custom_fusion = f32[4,3072]{0,1:T(8,128)S(1)} fusion(s32[2048]{0:T(1024)S(1)} %bitcast.140, f32[2048,4]{1,0:T(8,128)} %copy.34, f32[]{:T(128)} %constant.222.clone.1), kind=kCustom, calls=%fused_computation.45 | custom fusion | bytes 49664 | tf_op jit(solution)/shard_map/scatter | solution.py:206
  55.1 0.5 copy.35
  55.6 0.7 copy.36
  56.4 10.4 %all-to-all-start = ((f32[128,1,96]{2,1,0:T(1,128)}), f32[128,1,96]{2,1,0:T(1,128)S(1)}, u32[]{:S(2)}, u32[]{:S(2)}) async-start(f32[128,1,96]{2,1,0:T(1,128)} %copy.36), calls=%async_computation | async-start | bytes 131072 | tf_op jit(solution)/shard_map/all_to_all | solution.py:210
  66.8 0.1 slice_maximum_fusion.2
  67.1 0.2 broadcast_multiply_fusion.13
  67.4 8.3 %all-to-all-done = f32[128,1,96]{2,1,0:T(1,128)S(1)} async-done(((f32[128,1,96]{2,1,0:T(1,128)}), f32[128,1,96]{2,1,0:T(1,128)S(1)}, u32[]{:S(2)}, u32[]{:S(2)}) %all-to-all-start) | async-done | bytes 49184 | tf_op jit(solution)/shard_map/all_to_all | solution.py:210
  75.8 0.1 copy.38
  76.2 0.1 copy.39
  76.3 0.2 convert_element_type.114
  76.6 0.9 select_reduce_fusion.2
  77.5 0.6 multiply_convert_fusion
  78.1 0.9 convolution_multiply_fusion
  79.1 0.8 fusion.22
  79.9 1.9 %collective-permute-start.10 = (f32[4,4,512]{2,1,0:T(4,128)S(1)}, f32[4,4,512]{2,1,0:T(4,128)S(1)}, u32[]{:S(2)}, u32[]{:S(2)}) collective-permute-start(f32[4,4,512]{2,1,0:T(4,128)S(1)} %fusion.22), channel_id=1, source_target_pairs={{0,2},{2,0},{1,3},{3,1},{4,6},{6,4},{5,7},{7,5},{8,10},{10,8},{9,1... | collective-permute-start | bytes 98312 | tf_op jit(solution)/shard_map/ppermute | solution.py:86
  81.9 0.9 fusion.1
  82.8 8.0 %collective-permute-start.11 = (f32[4,1,512]{2,1,0:T(1,128)S(1)}, f32[4,1,512]{2,1,0:T(1,128)S(1)}, u32[]{:S(2)}, u32[]{:S(2)}) collective-permute-start(f32[4,1,512]{2,1,0:T(1,128)S(1)} %broadcast_select_fusion.10), channel_id=1, source_target_pairs={{0,1},{1,0},{2,3},{3,2},{4,5},{5,4},{6,7},{7,6},{8,9},{9,8},{10,11... | collective-permute-start | bytes 24584 | tf_op jit(solution)/shard_map/ppermute | solution.py:86
  90.8 5.6 %collective-permute-start.8 = (f32[4,4,64]{2,1,0:T(4,128)S(1)}, f32[4,4,64]{2,1,0:T(4,128)S(1)}, u32[]{:S(2)}, u32[]{:S(2)}) collective-permute-start(f32[4,4,64]{2,1,0:T(4,128)S(1)} %get-tuple-element.136), channel_id=1, source_target_pairs={{0,4},{4,8},{8,12},{12,16},{16,20},{20,24},{24,28},{28,32},{32,36}... | collective-permute-start | bytes 12296 | tf_op jit(solution)/shard_map/ppermute | solution.py:89
  96.4 1.9 %collective-permute-start.9 = (f32[4,4,64]{2,1,0:T(4,128)S(1)}, f32[4,4,64]{2,1,0:T(4,128)S(1)}, u32[]{:S(2)}, u32[]{:S(2)}) collective-permute-start(f32[4,4,64]{2,1,0:T(4,128)S(1)} %get-tuple-element.135), channel_id=1, source_target_pairs={{4,0},{8,4},{12,8},{16,12},{20,16},{24,20},{28,24},{32,28},{36,32}... | collective-permute-start | bytes 12296 | tf_op jit(solution)/shard_map/ppermute | solution.py:90
  98.4 0.9 fusion.8
  99.3 0.1 slice_maximum_fusion.1
  99.6 6.6 %collective-permute-done.9 = f32[4,4,64]{2,1,0:T(4,128)S(1)} collective-permute-done((f32[4,4,64]{2,1,0:T(4,128)S(1)}, f32[4,4,64]{2,1,0:T(4,128)S(1)}, u32[]{:S(2)}, u32[]{:S(2)}) %collective-permute-start.9) | collective-permute-done | bytes 4128 | tf_op jit(solution)/shard_map/ppermute | solution.py:90
  106.2 0.1 broadcast_multiply_fusion.7
  106.5 0.1 fusion.26
  106.7 1.9 %collective-permute-start.14 = (f32[4,4,512]{2,1,0:T(4,128)S(1)}, f32[4,4,512]{2,1,0:T(4,128)S(1)}, u32[]{:S(2)}, u32[]{:S(2)}) collective-permute-start(f32[4,4,512]{2,1,0:T(4,128)S(1)} %fusion.26), channel_id=1, source_target_pairs={{0,2},{2,0},{1,3},{3,1},{4,6},{6,4},{5,7},{7,5},{8,10},{10,8},{9,1... | collective-permute-start | bytes 98312 | tf_op jit(solution)/shard_map/ppermute | solution.py:86
  108.7 0.9 fusion
  109.5 1.9 %collective-permute-start.15 = (f32[4,1,512]{2,1,0:T(1,128)S(1)}, f32[4,1,512]{2,1,0:T(1,128)S(1)}, u32[]{:S(2)}, u32[]{:S(2)}) collective-permute-start(f32[4,1,512]{2,1,0:T(1,128)S(1)} %broadcast_select_fusion.8), channel_id=1, source_target_pairs={{0,1},{1,0},{2,3},{3,2},{4,5},{5,4},{6,7},{7,6},{8,9},{9,8},{10,11... | collective-permute-start | bytes 24584 | tf_op jit(solution)/shard_map/ppermute | solution.py:86
  111.5 1.9 %collective-permute-start.12 = (f32[4,4,64]{2,1,0:T(4,128)S(1)}, f32[4,4,64]{2,1,0:T(4,128)S(1)}, u32[]{:S(2)}, u32[]{:S(2)}) collective-permute-start(f32[4,4,64]{2,1,0:T(4,128)S(1)} %get-tuple-element.113), channel_id=1, source_target_pairs={{0,4},{4,8},{8,12},{12,16},{16,20},{20,24},{24,28},{28,32},{32,36}... | collective-permute-start | bytes 12296 | tf_op jit(solution)/shard_map/ppermute | solution.py:89
  113.4 3.9 %collective-permute-start.13 = (f32[4,4,64]{2,1,0:T(4,128)S(1)}, f32[4,4,64]{2,1,0:T(4,128)S(1)}, u32[]{:S(2)}, u32[]{:S(2)}) collective-permute-start(f32[4,4,64]{2,1,0:T(4,128)S(1)} %get-tuple-element.112), channel_id=1, source_target_pairs={{4,0},{8,4},{12,8},{16,12},{20,16},{24,20},{28,24},{32,28},{36,32}... | collective-permute-start | bytes 12296 | tf_op jit(solution)/shard_map/ppermute | solution.py:90
  117.3 0.9 fusion.10
  118.2 0.8 collective-permute-done.15
  119.0 0.1 slice_maximum_fusion
  119.3 3.8 %collective-permute-done.13 = f32[4,4,64]{2,1,0:T(4,128)S(1)} collective-permute-done((f32[4,4,64]{2,1,0:T(4,128)S(1)}, f32[4,4,64]{2,1,0:T(4,128)S(1)}, u32[]{:S(2)}, u32[]{:S(2)}) %collective-permute-start.13) | collective-permute-done | bytes 4128 | tf_op jit(solution)/shard_map/ppermute | solution.py:90
  123.2 0.2 broadcast_multiply_fusion.1
  123.5 0.7 fusion.31
  (136 shorter events, 1.9 us)
Async XLA Ops:
  0.6 35.1 %copy-start.7 = (s32[1,1,2048,1]{2,3,1,0:T(1,128)S(1)}, s32[1,1,2048,1]{2,3,1,0:T(1,128)}, u32[]{:S(2)}) copy-start(s32[1,1,2048,1]{2,3,1,0:T(1,128)} %param.12) | copy-start | bytes 24580
  1.5 37.7 %collective-permute-start.3 = (bf16[3,2,8,1]{3,2,1,0:T(8,128)(2,1)S(1)}, bf16[3,2,8,1]{3,2,1,0:T(8,128)(2,1)S(1)}, u32[]{:S(2)}, u32[]{:S(2)}) collective-permute-start(bf16[3,2,8,1]{3,2,1,0:T(8,128)(2,1)S(1)} %slice_select_fusion), channel_id=1, source_target_pairs={{0,1},{1,0},{2,3},{3,2},{4,5},{5,4},{6,7},{7,6},{8,9},{9,8},{10,11... | collective-permute-start | bytes 296 | tf_op jit(solution)/shard_map/ppermute | solution.py:86
  13.2 28.0 %collective-permute-start.2 = (bf16[3,2,1,128]{3,2,1,0:T(2,128)(2,1)S(1)}, bf16[3,2,1,128]{3,2,1,0:T(2,128)(2,1)S(1)}, u32[]{:S(2)}, u32[]{:S(2)}) collective-permute-start(bf16[3,2,1,128]{3,2,1,0:T(2,128)(2,1)S(1)} %broadcast_select_fusion.18), channel_id=1, source_target_pairs={{0,2},{2,0},{1,3},{3,1},{4,6},{6,4},{5,7},{7,5},{8,10},{10,8},{9,1... | collective-permute-start | bytes 4616 | tf_op jit(solution)/shard_map/ppermute | solution.py:86
  15.9 27.6 %collective-permute-start = (bf16[3,1,8,128]{3,2,1,0:T(8,128)(2,1)S(1)}, bf16[3,1,8,128]{3,2,1,0:T(8,128)(2,1)S(1)}, u32[]{:S(2)}, u32[]{:S(2)}) collective-permute-start(bf16[3,1,8,128]{3,2,1,0:T(8,128)(2,1)S(1)} %get-tuple-element.184), channel_id=1, source_target_pairs={{4,0},{8,4},{12,8},{16,12},{20,16},{24,20},{28,24},{32,28},{36,32}... | collective-permute-start | bytes 18440 | tf_op jit(solution)/shard_map/ppermute | solution.py:90
  19.1 28.1 %collective-permute-start.1 = (bf16[3,1,8,128]{3,2,1,0:T(8,128)(2,1)S(1)}, bf16[3,1,8,128]{3,2,1,0:T(8,128)(2,1)S(1)}, u32[]{:S(2)}, u32[]{:S(2)}) collective-permute-start(bf16[3,1,8,128]{3,2,1,0:T(8,128)(2,1)S(1)} %get-tuple-element.185), channel_id=1, source_target_pairs={{0,4},{4,8},{8,12},{12,16},{16,20},{20,24},{24,28},{28,32},{32,36}... | collective-permute-start | bytes 18440 | tf_op jit(solution)/shard_map/ppermute | solution.py:89
  25.9 41.0 %collective-permute-start.6 = (f32[4,4,512]{2,1,0:T(4,128)}, f32[4,4,512]{2,1,0:T(4,128)S(1)}, u32[]{:S(2)}, u32[]{:S(2)}) collective-permute-start(f32[4,4,512]{2,1,0:T(4,128)} %bitcast.125), channel_id=1, source_target_pairs={{0,2},{2,0},{1,3},{3,1},{4,6},{6,4},{5,7},{7,5},{8,10},{10,8},{9,1... | collective-permute-start | bytes 98312 | tf_op jit(solution)/shard_map/ppermute | solution.py:86
  34.9 1.5 %copy-start.8 = (f32[8,512]{1,0:T(8,128)S(1)}, f32[8,512]{1,0:T(8,128)}, u32[]{:S(2)}) copy-start(f32[8,512]{1,0:T(8,128)} %constant.254.clone) | copy-start | bytes 49156
  34.9 1.5 %copy-start.9 = (f32[8,512]{1,0:T(8,128)S(1)}, f32[8,512]{1,0:T(8,128)}, u32[]{:S(2)}) copy-start(f32[8,512]{1,0:T(8,128)} %constant.255.clone) | copy-start | bytes 49156
  34.9 1.5 %copy-start.10 = (f32[8,512]{1,0:T(8,128)S(1)}, f32[8,512]{1,0:T(8,128)}, u32[]{:S(2)}) copy-start(f32[8,512]{1,0:T(8,128)} %constant.256.clone) | copy-start | bytes 49156
  35.4 2.0 %copy-start.1 = (f32[4,1,1,4,512]{4,3,2,1,0:T(4,128)S(1)}, f32[4,1,1,4,512]{4,3,2,1,0:T(4,128)}, u32[]{:S(2)}) copy-start(f32[4,1,1,4,512]{4,3,2,1,0:T(4,128)} %param.15) | copy-start | bytes 98308
  36.4 1.8 %copy-start.11 = (s32[1,1,2048]{2,1,0:T(1,128)S(1)}, s32[1,1,2048]{2,1,0:T(1,128)}, u32[]{:S(2)}) copy-start(s32[1,1,2048]{2,1,0:T(1,128)} %param.14) | copy-start | bytes 24580
  36.4 1.8 %copy-start.12 = (s32[1,1,2048]{2,1,0:T(1,128)S(1)}, s32[1,1,2048]{2,1,0:T(1,128)}, u32[]{:S(2)}) copy-start(s32[1,1,2048]{2,1,0:T(1,128)} %param.13) | copy-start | bytes 24580
  37.3 1.9 %copy-start.2 = (f32[512,512]{1,0:T(8,128)}, f32[512,512]{1,0:T(8,128)S(1)}, u32[]{:S(2)}) copy-start(f32[512,512]{1,0:T(8,128)S(1)} %get-tuple-element.193) | copy-start | bytes 3145732
  37.3 1.9 %copy-start.4 = (f32[512,512]{1,0:T(8,128)}, f32[512,512]{1,0:T(8,128)S(1)}, u32[]{:S(2)}) copy-start(f32[512,512]{1,0:T(8,128)S(1)} %get-tuple-element.194) | copy-start | bytes 3145732
  37.3 1.9 %copy-start = (bf16[3,2,8,128]{3,2,1,0:T(8,128)(2,1)S(1)}, bf16[3,2,8,128]{3,2,1,0:T(8,128)(2,1)}, u32[]{:S(2)}) copy-start(bf16[3,2,8,128]{3,2,1,0:T(8,128)(2,1)} %param.10) | copy-start | bytes 36868
  38.2 9.1 %copy-start.13 = (f32[2,8,128]{2,1,0:T(8,128)S(1)}, f32[2,8,128]{2,1,0:T(8,128)}, u32[]{:S(2)}) copy-start(f32[2,8,128]{2,1,0:T(8,128)} %param.11) | copy-start | bytes 24580
  39.3 27.5 %collective-permute-start.7 = (f32[4,1,512]{2,1,0:T(1,128)S(1)}, f32[4,1,512]{2,1,0:T(1,128)S(1)}, u32[]{:S(2)}, u32[]{:S(2)}) collective-permute-start(f32[4,1,512]{2,1,0:T(1,128)S(1)} %broadcast_select_fusion.12), channel_id=1, source_target_pairs={{0,1},{1,0},{2,3},{3,2},{4,5},{5,4},{6,7},{7,6},{8,9},{9,8},{10,11... | collective-permute-start | bytes 24584 | tf_op jit(solution)/shard_map/ppermute | solution.py:86
  41.2 25.9 %collective-permute-start.4 = (f32[4,4,64]{2,1,0:T(4,128)S(1)}, f32[4,4,64]{2,1,0:T(4,128)S(1)}, u32[]{:S(2)}, u32[]{:S(2)}) collective-permute-start(f32[4,4,64]{2,1,0:T(4,128)S(1)} %get-tuple-element.159), channel_id=1, source_target_pairs={{0,4},{4,8},{8,12},{12,16},{16,20},{20,24},{24,28},{28,32},{32,36}... | collective-permute-start | bytes 12296 | tf_op jit(solution)/shard_map/ppermute | solution.py:89
  43.5 23.6 %collective-permute-start.5 = (f32[4,4,64]{2,1,0:T(4,128)S(1)}, f32[4,4,64]{2,1,0:T(4,128)S(1)}, u32[]{:S(2)}, u32[]{:S(2)}) collective-permute-start(f32[4,4,64]{2,1,0:T(4,128)S(1)} %get-tuple-element.158), channel_id=1, source_target_pairs={{4,0},{8,4},{12,8},{16,12},{20,16},{24,20},{28,24},{32,28},{36,32}... | collective-permute-start | bytes 12296 | tf_op jit(solution)/shard_map/ppermute | solution.py:90
  48.8 27.8 %copy-start.16 = (f32[8,16]{1,0:T(8,128)S(1)}, f32[8,16]{1,0:T(8,128)}, u32[]{:S(2)}) copy-start(f32[8,16]{1,0:T(8,128)} %constant.253.clone) | copy-start | bytes 1540
  56.4 19.3 %all-to-all-start = ((f32[128,1,96]{2,1,0:T(1,128)}), f32[128,1,96]{2,1,0:T(1,128)S(1)}, u32[]{:S(2)}, u32[]{:S(2)}) async-start(f32[128,1,96]{2,1,0:T(1,128)} %copy.36), calls=%async_computation | async-start | bytes 131072 | tf_op jit(solution)/shard_map/all_to_all | solution.py:210
  77.5 4.4 %copy-start.3 = (f32[512,512]{1,0:T(8,128)S(1)}, f32[512,512]{1,0:T(8,128)}, u32[]{:S(2)}) copy-start(f32[512,512]{1,0:T(8,128)} %copy-done.2) | copy-start | bytes 3145732
  77.5 4.4 %copy-start.5 = (f32[512,512]{1,0:T(8,128)S(1)}, f32[512,512]{1,0:T(8,128)}, u32[]{:S(2)}) copy-start(f32[512,512]{1,0:T(8,128)} %copy-done.4) | copy-start | bytes 3145732
  79.1 20.2 %copy-start.6 = (f32[3,4,512]{2,1,0:T(4,128)}, f32[3,4,512]{2,1,0:T(4,128)S(1)}, u32[]{:S(2)}) copy-start(f32[3,4,512]{2,1,0:T(4,128)S(1)} %reshape.356) | copy-start | bytes 73732
  79.9 19.5 %collective-permute-start.10 = (f32[4,4,512]{2,1,0:T(4,128)S(1)}, f32[4,4,512]{2,1,0:T(4,128)S(1)}, u32[]{:S(2)}, u32[]{:S(2)}) collective-permute-start(f32[4,4,512]{2,1,0:T(4,128)S(1)} %fusion.22), channel_id=1, source_target_pairs={{0,2},{2,0},{1,3},{3,1},{4,6},{6,4},{5,7},{7,5},{8,10},{10,8},{9,1... | collective-permute-start | bytes 98312 | tf_op jit(solution)/shard_map/ppermute | solution.py:86
  82.8 23.7 %copy-start.14 = (pred[512]{0:T(512)(128)(4,1)S(1)}, pred[512]{0:T(512)(128)(4,1)}, u32[]{:S(2)}) copy-start(pred[512]{0:T(512)(128)(4,1)} %get-tuple-element.219) | copy-start | bytes 1540
  82.8 23.7 %copy-start.15 = (pred[512]{0:T(512)(128)(4,1)S(1)}, pred[512]{0:T(512)(128)(4,1)}, u32[]{:S(2)}) copy-start(pred[512]{0:T(512)(128)(4,1)} %get-tuple-element.220) | copy-start | bytes 1540
  82.8 16.4 %collective-permute-start.11 = (f32[4,1,512]{2,1,0:T(1,128)S(1)}, f32[4,1,512]{2,1,0:T(1,128)S(1)}, u32[]{:S(2)}, u32[]{:S(2)}) collective-permute-start(f32[4,1,512]{2,1,0:T(1,128)S(1)} %broadcast_select_fusion.10), channel_id=1, source_target_pairs={{0,1},{1,0},{2,3},{3,2},{4,5},{5,4},{6,7},{7,6},{8,9},{9,8},{10,11... | collective-permute-start | bytes 24584 | tf_op jit(solution)/shard_map/ppermute | solution.py:86
  90.8 8.8 %collective-permute-start.8 = (f32[4,4,64]{2,1,0:T(4,128)S(1)}, f32[4,4,64]{2,1,0:T(4,128)S(1)}, u32[]{:S(2)}, u32[]{:S(2)}) collective-permute-start(f32[4,4,64]{2,1,0:T(4,128)S(1)} %get-tuple-element.136), channel_id=1, source_target_pairs={{0,4},{4,8},{8,12},{12,16},{16,20},{20,24},{24,28},{28,32},{32,36}... | collective-permute-start | bytes 12296 | tf_op jit(solution)/shard_map/ppermute | solution.py:89
  96.4 9.8 %collective-permute-start.9 = (f32[4,4,64]{2,1,0:T(4,128)S(1)}, f32[4,4,64]{2,1,0:T(4,128)S(1)}, u32[]{:S(2)}, u32[]{:S(2)}) collective-permute-start(f32[4,4,64]{2,1,0:T(4,128)S(1)} %get-tuple-element.135), channel_id=1, source_target_pairs={{4,0},{8,4},{12,8},{16,12},{20,16},{24,20},{28,24},{32,28},{36,32}... | collective-permute-start | bytes 12296 | tf_op jit(solution)/shard_map/ppermute | solution.py:90
  106.7 12.5 %collective-permute-start.14 = (f32[4,4,512]{2,1,0:T(4,128)S(1)}, f32[4,4,512]{2,1,0:T(4,128)S(1)}, u32[]{:S(2)}, u32[]{:S(2)}) collective-permute-start(f32[4,4,512]{2,1,0:T(4,128)S(1)} %fusion.26), channel_id=1, source_target_pairs={{0,2},{2,0},{1,3},{3,1},{4,6},{6,4},{5,7},{7,5},{8,10},{10,8},{9,1... | collective-permute-start | bytes 98312 | tf_op jit(solution)/shard_map/ppermute | solution.py:86
  109.5 9.4 %collective-permute-start.15 = (f32[4,1,512]{2,1,0:T(1,128)S(1)}, f32[4,1,512]{2,1,0:T(1,128)S(1)}, u32[]{:S(2)}, u32[]{:S(2)}) collective-permute-start(f32[4,1,512]{2,1,0:T(1,128)S(1)} %broadcast_select_fusion.8), channel_id=1, source_target_pairs={{0,1},{1,0},{2,3},{3,2},{4,5},{5,4},{6,7},{7,6},{8,9},{9,8},{10,11... | collective-permute-start | bytes 24584 | tf_op jit(solution)/shard_map/ppermute | solution.py:86
  111.5 7.8 %collective-permute-start.12 = (f32[4,4,64]{2,1,0:T(4,128)S(1)}, f32[4,4,64]{2,1,0:T(4,128)S(1)}, u32[]{:S(2)}, u32[]{:S(2)}) collective-permute-start(f32[4,4,64]{2,1,0:T(4,128)S(1)} %get-tuple-element.113), channel_id=1, source_target_pairs={{0,4},{4,8},{8,12},{12,16},{16,20},{20,24},{24,28},{28,32},{32,36}... | collective-permute-start | bytes 12296 | tf_op jit(solution)/shard_map/ppermute | solution.py:89
  113.4 9.8 %collective-permute-start.13 = (f32[4,4,64]{2,1,0:T(4,128)S(1)}, f32[4,4,64]{2,1,0:T(4,128)S(1)}, u32[]{:S(2)}, u32[]{:S(2)}) collective-permute-start(f32[4,4,64]{2,1,0:T(4,128)S(1)} %get-tuple-element.112), channel_id=1, source_target_pairs={{4,0},{8,4},{12,8},{16,12},{20,16},{24,20},{28,24},{32,28},{36,32}... | collective-permute-start | bytes 12296 | tf_op jit(solution)/shard_map/ppermute | solution.py:90

commit v6 on v5

--- a/solution.py
+++ b/solution.py
@@ -176,12 +176,6 @@
     return 1.0 / 3.0 * fields + 2.0 / 3.0 * (section_two + TIME_STEP * step(section_two))
 
 
-def pick_columns(index, table):
-    levels = jnp.arange(table.shape[1], dtype=jnp.int32)
-    chosen = jnp.where(index[None, None, :] == levels[None, :, None], table[:, :, None], 0.0)
-    return jnp.sum(chosen, axis=1)
-
-
 def on_device_body(velocity, eddy_viscosity, cell_owner, cell_element, cell_position, acoustic_state):
     sources = source_cells(velocity, eddy_viscosity)
     cell_count = sources.shape[1] * sources.shape[2] * sources.shape[3]
@@ -217,9 +211,12 @@
     got_position = got_ident % subcells
 
     values = jnp.asarray(basis_table().T)
-    along_a = pick_columns(got_position // (SUB * SUB), values)
-    along_b = pick_columns(got_position // SUB % SUB, values)
-    along_c = pick_columns(got_position % SUB, values)
+    index = jnp.stack([got_position // (SUB * SUB), got_position // SUB % SUB, got_position % SUB])
+    levels = jnp.arange(SUB, dtype=jnp.int32)
+    chosen = jnp.where(
+        index[:, None, None, :] == levels[None, None, :, None], values[None, :, :, None], 0.0
+    )
+    along_a, along_b, along_c = jnp.sum(chosen, axis=2)
     rows = got_position.shape[0]
     node_columns = (
         along_a[:, None, None, :] * along_b[None, :, None, :] * along_c[None, None, :, :]

time: 125 us -> 129 us (1.032)
  the two profiles are of different devices: /device:TPU:62 before, /device:TPU:64 now
where the time goes in v6:
time: 129 us; the launch traced here: 128 us
  starting transfers between devices  70.4 us (55%)
  waiting for transfers between devices  21.8 us (17%)
  local copies, waits for them, and re-layouts  17.1 us (13%)
  other arithmetic  10.7 us (8%)
  matrix products  6.19 us (5%)
  between operations  1.73 us (1%)
    ppermute x8, starting transfers between devices, neighbours(): got = lax.ppermute(sent, axis, [(0, 1), (1, 0)])  29.8 us
    ppermute x4, starting transfers between devices, neighbours(): lax.ppermute(lower, axis, [(i + 1, i) for i in range(count - 1)])  21 us
    ppermute x4, starting transfers between devices, neighbours(): lax.ppermute(upper, axis, [(i, i + 1) for i in range(count - 1)])  11.2 us
    ppermute x4, waiting for transfers between devices, neighbours(): lax.ppermute(upper, axis, [(i, i + 1) for i in range(count - 1)])  10.7 us
    all_to_all x1, waiting for transfers between devices, on_device_body(): got = lax.all_to_all(send, 'gx', split_axis=0, concat_axis=0, tiled=True)  10.5 us
    all_to_all x1, starting transfers between devices, on_device_body(): got = lax.all_to_all(send, 'gx', split_axis=0, concat_axis=0, tiled=True)  8.27 us
    scatter x1, local copies, waits for them, and re-layouts, on_device_body(): send = jnp.zeros((4, owner_count * capacity), jnp.float32).at[:, slot_ind...  6.35 us
    dot_general x3, matrix products, tendency(): divergence = jnp.dot(velocity_rows, div_table, precision=precision)  2.67 us
  transfers between devices with their start and end apart: 17, of which 4 were waited for; matrix products, arithmetic and copies ran while one was open for 20% of the time, Pallas kernels for 0%

profile of v6, /device:TPU:64, one launch (start us, length us, event | category | flops | bytes accessed | tf_op | source)
XLA Modules:
  0.0 128.0 jit_solution(13761968645475436455)
XLA Ops:
  0.6 0.7 fusion.175
  1.4 3.5 %collective-permute-start.1 = (bf16[3,1,8,128]{3,2,1,0:T(8,128)(2,1)S(1)}, bf16[3,1,8,128]{3,2,1,0:T(8,128)(2,1)S(1)}, u32[]{:S(2)}, u32[]{:S(2)}) collective-permute-start(bf16[3,1,8,128]{3,2,1,0:T(8,128)(2,1)S(1)} %get-tuple-element.185), channel_id=1, source_target_pairs={{0,4},{4,8},{8,12},{12,16},{16,20},{20,24},{24,28},{28,32},{32,36}... | collective-permute-start | bytes 18440 | tf_op jit(solution)/shard_map/ppermute | solution.py:89
  4.8 6.6 %collective-permute-start = (bf16[3,1,8,128]{3,2,1,0:T(8,128)(2,1)S(1)}, bf16[3,1,8,128]{3,2,1,0:T(8,128)(2,1)S(1)}, u32[]{:S(2)}, u32[]{:S(2)}) collective-permute-start(bf16[3,1,8,128]{3,2,1,0:T(8,128)(2,1)S(1)} %get-tuple-element.184), channel_id=1, source_target_pairs={{4,0},{8,4},{12,8},{16,12},{20,16},{24,20},{28,24},{32,28},{36,32}... | collective-permute-start | bytes 18440 | tf_op jit(solution)/shard_map/ppermute | solution.py:90
  11.4 0.8 broadcast_select_fusion.18
  12.2 1.9 %collective-permute-start.2 = (bf16[3,2,1,128]{3,2,1,0:T(2,128)(2,1)S(1)}, bf16[3,2,1,128]{3,2,1,0:T(2,128)(2,1)S(1)}, u32[]{:S(2)}, u32[]{:S(2)}) collective-permute-start(bf16[3,2,1,128]{3,2,1,0:T(2,128)(2,1)S(1)} %broadcast_select_fusion.18), channel_id=1, source_target_pairs={{0,2},{2,0},{1,3},{3,1},{4,6},{6,4},{5,7},{7,5},{8,10},{10,8},{9,1... | collective-permute-start | bytes 4616 | tf_op jit(solution)/shard_map/ppermute | solution.py:86
  14.2 0.9 slice_select_fusion
  15.0 10.0 %collective-permute-start.3 = (bf16[3,2,8,1]{3,2,1,0:T(8,128)(2,1)S(1)}, bf16[3,2,8,1]{3,2,1,0:T(8,128)(2,1)S(1)}, u32[]{:S(2)}, u32[]{:S(2)}) collective-permute-start(bf16[3,2,8,1]{3,2,1,0:T(8,128)(2,1)S(1)} %slice_select_fusion), channel_id=1, source_target_pairs={{0,1},{1,0},{2,3},{3,2},{4,5},{5,4},{6,7},{7,6},{8,9},{9,8},{10,11... | collective-permute-start | bytes 296 | tf_op jit(solution)/shard_map/ppermute | solution.py:86
  25.0 2.1 %collective-permute-start.6 = (f32[4,4,512]{2,1,0:T(4,128)}, f32[4,4,512]{2,1,0:T(4,128)S(1)}, u32[]{:S(2)}, u32[]{:S(2)}) collective-permute-start(f32[4,4,512]{2,1,0:T(4,128)} %bitcast.131), channel_id=1, source_target_pairs={{0,2},{2,0},{1,3},{3,1},{4,6},{6,4},{5,7},{7,5},{8,10},{10,8},{9,1... | collective-permute-start | bytes 98312 | tf_op jit(solution)/shard_map/ppermute | solution.py:86
  27.2 0.7 convert_element_type.107
  27.9 0.7 fusion.174
  28.6 0.8 fusion.172
  29.4 0.9 fusion.173
  30.3 0.7 slice_bitcast_fusion.16
  31.0 0.8 broadcast_select_fusion.12
  31.9 0.8 fusion.170
  32.7 0.8 fusion.171
  33.5 0.6 fusion.149
  34.1 0.8 copy.34
  35.0 0.3 fusion.16
  35.4 0.3 copy.35
  35.8 0.6 fusion.15
  36.5 0.8 bitcast_select_fusion.2
  37.4 0.8 convolution_bitcast_fusion
  38.4 0.9 fusion.6
  39.3 2.2 %collective-permute-start.7 = (f32[4,1,512]{2,1,0:T(1,128)S(1)}, f32[4,1,512]{2,1,0:T(1,128)S(1)}, u32[]{:S(2)}, u32[]{:S(2)}) collective-permute-start(f32[4,1,512]{2,1,0:T(1,128)S(1)} %broadcast_select_fusion.12), channel_id=1, source_target_pairs={{0,1},{1,0},{2,3},{3,2},{4,5},{5,4},{6,7},{7,6},{8,9},{9,8},{10,11... | collective-permute-start | bytes 24584 | tf_op jit(solution)/shard_map/ppermute | solution.py:86
  41.6 1.9 %collective-permute-start.4 = (f32[4,4,64]{2,1,0:T(4,128)S(1)}, f32[4,4,64]{2,1,0:T(4,128)S(1)}, u32[]{:S(2)}, u32[]{:S(2)}) collective-permute-start(f32[4,4,64]{2,1,0:T(4,128)S(1)} %get-tuple-element.163), channel_id=1, source_target_pairs={{0,4},{4,8},{8,12},{12,16},{16,20},{20,24},{24,28},{28,32},{32,36}... | collective-permute-start | bytes 12296 | tf_op jit(solution)/shard_map/ppermute | solution.py:89
  43.6 8.1 %collective-permute-start.5 = (f32[4,4,64]{2,1,0:T(4,128)S(1)}, f32[4,4,64]{2,1,0:T(4,128)S(1)}, u32[]{:S(2)}, u32[]{:S(2)}) collective-permute-start(f32[4,4,64]{2,1,0:T(4,128)S(1)} %get-tuple-element.162), channel_id=1, source_target_pairs={{4,0},{8,4},{12,8},{16,12},{20,16},{24,20},{28,24},{32,28},{36,32}... | collective-permute-start | bytes 12296 | tf_op jit(solution)/shard_map/ppermute | solution.py:90
  52.0 1.4 %copy.36 = f32[2048,4]{1,0:T(8,128)} copy(f32[2048,4]{0,1:T(4,128)S(1)} %maximum_bitcast_fusion) | data formatting | bytes 65536 | tf_op jit(solution)/shard_map/concatenate | solution.py:196
  53.4 6.3 %scatter_custom_fusion = f32[4,3072]{0,1:T(8,128)S(1)} fusion(s32[2048]{0:T(1024)S(1)} %bitcast.146, f32[2048,4]{1,0:T(8,128)} %copy.36, f32[]{:T(128)} %constant.222.clone.1), kind=kCustom, calls=%fused_computation.43 | custom fusion | bytes 49664 | tf_op jit(solution)/shard_map/scatter | solution.py:200
  59.7 0.5 copy.37
  60.2 0.8 copy.38
  61.0 8.3 %all-to-all-start = ((f32[128,1,96]{2,1,0:T(1,128)}), f32[128,1,96]{2,1,0:T(1,128)S(1)}, u32[]{:S(2)}, u32[]{:S(2)}) async-start(f32[128,1,96]{2,1,0:T(1,128)} %copy.38), calls=%async_computation | async-start | bytes 131072 | tf_op jit(solution)/shard_map/all_to_all | solution.py:204
  69.3 0.1 slice_maximum_fusion.2
  69.6 0.2 broadcast_multiply_fusion.13
  69.9 10.5 %all-to-all-done = f32[128,1,96]{2,1,0:T(1,128)S(1)} async-done(((f32[128,1,96]{2,1,0:T(1,128)}), f32[128,1,96]{2,1,0:T(1,128)S(1)}, u32[]{:S(2)}, u32[]{:S(2)}) %all-to-all-start) | async-done | bytes 49184 | tf_op jit(solution)/shard_map/all_to_all | solution.py:204
  80.7 0.1 convert_element_type.122
  80.9 0.1 copy.41
  81.0 0.2 convert_element_type.121
  81.4 0.1 and_select_fusion.1
  81.7 0.9 select_reduce_fusion
  82.6 0.6 multiply_convert_fusion
  83.2 0.9 convolution_multiply_fusion
  84.2 0.8 fusion.22
  85.0 0.9 fusion.1
  86.0 1.9 %collective-permute-start.10 = (f32[4,4,512]{2,1,0:T(4,128)S(1)}, f32[4,4,512]{2,1,0:T(4,128)S(1)}, u32[]{:S(2)}, u32[]{:S(2)}) collective-permute-start(f32[4,4,512]{2,1,0:T(4,128)S(1)} %fusion.22), channel_id=1, source_target_pairs={{0,2},{2,0},{1,3},{3,1},{4,6},{6,4},{5,7},{7,5},{8,10},{10,8},{9,1... | collective-permute-start | bytes 98312 | tf_op jit(solution)/shard_map/ppermute | solution.py:86
  88.0 7.5 %collective-permute-start.11 = (f32[4,1,512]{2,1,0:T(1,128)S(1)}, f32[4,1,512]{2,1,0:T(1,128)S(1)}, u32[]{:S(2)}, u32[]{:S(2)}) collective-permute-start(f32[4,1,512]{2,1,0:T(1,128)S(1)} %broadcast_select_fusion.10), channel_id=1, source_target_pairs={{0,1},{1,0},{2,3},{3,2},{4,5},{5,4},{6,7},{7,6},{8,9},{9,8},{10,11... | collective-permute-start | bytes 24584 | tf_op jit(solution)/shard_map/ppermute | solution.py:86
  95.5 4.4 %collective-permute-start.9 = (f32[4,4,64]{2,1,0:T(4,128)S(1)}, f32[4,4,64]{2,1,0:T(4,128)S(1)}, u32[]{:S(2)}, u32[]{:S(2)}) collective-permute-start(f32[4,4,64]{2,1,0:T(4,128)S(1)} %get-tuple-element.139), channel_id=1, source_target_pairs={{4,0},{8,4},{12,8},{16,12},{20,16},{24,20},{28,24},{32,28},{36,32}... | collective-permute-start | bytes 12296 | tf_op jit(solution)/shard_map/ppermute | solution.py:90
  99.9 1.9 %collective-permute-start.8 = (f32[4,4,64]{2,1,0:T(4,128)S(1)}, f32[4,4,64]{2,1,0:T(4,128)S(1)}, u32[]{:S(2)}, u32[]{:S(2)}) collective-permute-start(f32[4,4,64]{2,1,0:T(4,128)S(1)} %get-tuple-element.140), channel_id=1, source_target_pairs={{0,4},{4,8},{8,12},{12,16},{16,20},{20,24},{24,28},{28,32},{32,36}... | collective-permute-start | bytes 12296 | tf_op jit(solution)/shard_map/ppermute | solution.py:89
  101.9 0.9 fusion.8
  102.8 0.1 slice_maximum_fusion.1
  103.1 6.6 %collective-permute-done.8 = f32[4,4,64]{2,1,0:T(4,128)S(1)} collective-permute-done((f32[4,4,64]{2,1,0:T(4,128)S(1)}, f32[4,4,64]{2,1,0:T(4,128)S(1)}, u32[]{:S(2)}, u32[]{:S(2)}) %collective-permute-start.8) | collective-permute-done | bytes 4128 | tf_op jit(solution)/shard_map/ppermute | solution.py:89
  109.7 0.2 broadcast_multiply_fusion.7
  110.0 0.1 fusion.26
  110.1 0.9 fusion
  111.0 1.9 %collective-permute-start.14 = (f32[4,4,512]{2,1,0:T(4,128)S(1)}, f32[4,4,512]{2,1,0:T(4,128)S(1)}, u32[]{:S(2)}, u32[]{:S(2)}) collective-permute-start(f32[4,4,512]{2,1,0:T(4,128)S(1)} %fusion.26), channel_id=1, source_target_pairs={{0,2},{2,0},{1,3},{3,1},{4,6},{6,4},{5,7},{7,5},{8,10},{10,8},{9,1... | collective-permute-start | bytes 98312 | tf_op jit(solution)/shard_map/ppermute | solution.py:86
  113.1 2.2 %collective-permute-start.15 = (f32[4,1,512]{2,1,0:T(1,128)S(1)}, f32[4,1,512]{2,1,0:T(1,128)S(1)}, u32[]{:S(2)}, u32[]{:S(2)}) collective-permute-start(f32[4,1,512]{2,1,0:T(1,128)S(1)} %broadcast_select_fusion.8), channel_id=1, source_target_pairs={{0,1},{1,0},{2,3},{3,2},{4,5},{5,4},{6,7},{7,6},{8,9},{9,8},{10,11... | collective-permute-start | bytes 24584 | tf_op jit(solution)/shard_map/ppermute | solution.py:86
  115.3 1.9 %collective-permute-start.13 = (f32[4,4,64]{2,1,0:T(4,128)S(1)}, f32[4,4,64]{2,1,0:T(4,128)S(1)}, u32[]{:S(2)}, u32[]{:S(2)}) collective-permute-start(f32[4,4,64]{2,1,0:T(4,128)S(1)} %get-tuple-element.116), channel_id=1, source_target_pairs={{4,0},{8,4},{12,8},{16,12},{20,16},{24,20},{28,24},{32,28},{36,32}... | collective-permute-start | bytes 12296 | tf_op jit(solution)/shard_map/ppermute | solution.py:90
  117.2 3.9 %collective-permute-start.12 = (f32[4,4,64]{2,1,0:T(4,128)S(1)}, f32[4,4,64]{2,1,0:T(4,128)S(1)}, u32[]{:S(2)}, u32[]{:S(2)}) collective-permute-start(f32[4,4,64]{2,1,0:T(4,128)S(1)} %get-tuple-element.117), channel_id=1, source_target_pairs={{0,4},{4,8},{8,12},{12,16},{16,20},{20,24},{24,28},{28,32},{32,36}... | collective-permute-start | bytes 12296 | tf_op jit(solution)/shard_map/ppermute | solution.py:89
  121.1 0.9 fusion.10
  122.0 0.6 collective-permute-done.15
  122.6 0.1 slice_maximum_fusion
  122.9 4.0 %collective-permute-done.12 = f32[4,4,64]{2,1,0:T(4,128)S(1)} collective-permute-done((f32[4,4,64]{2,1,0:T(4,128)S(1)}, f32[4,4,64]{2,1,0:T(4,128)S(1)}, u32[]{:S(2)}, u32[]{:S(2)}) %collective-permute-start.12) | collective-permute-done | bytes 4128 | tf_op jit(solution)/shard_map/ppermute | solution.py:89
  126.9 0.1 broadcast_multiply_fusion.1
  127.2 0.7 fusion.31
  (140 shorter events, 2.4 us)
Async XLA Ops:
  0.6 35.2 %copy-start.7 = (s32[1,1,2048,1]{2,3,1,0:T(1,128)S(1)}, s32[1,1,2048,1]{2,3,1,0:T(1,128)}, u32[]{:S(2)}) copy-start(s32[1,1,2048,1]{2,3,1,0:T(1,128)} %param.12) | copy-start | bytes 24580
  1.4 42.3 %collective-permute-start.1 = (bf16[3,1,8,128]{3,2,1,0:T(8,128)(2,1)S(1)}, bf16[3,1,8,128]{3,2,1,0:T(8,128)(2,1)S(1)}, u32[]{:S(2)}, u32[]{:S(2)}) collective-permute-start(bf16[3,1,8,128]{3,2,1,0:T(8,128)(2,1)S(1)} %get-tuple-element.185), channel_id=1, source_target_pairs={{0,4},{4,8},{8,12},{12,16},{16,20},{20,24},{24,28},{28,32},{32,36}... | collective-permute-start | bytes 18440 | tf_op jit(solution)/shard_map/ppermute | solution.py:89
  4.8 46.9 %collective-permute-start = (bf16[3,1,8,128]{3,2,1,0:T(8,128)(2,1)S(1)}, bf16[3,1,8,128]{3,2,1,0:T(8,128)(2,1)S(1)}, u32[]{:S(2)}, u32[]{:S(2)}) collective-permute-start(bf16[3,1,8,128]{3,2,1,0:T(8,128)(2,1)S(1)} %get-tuple-element.184), channel_id=1, source_target_pairs={{4,0},{8,4},{12,8},{16,12},{20,16},{24,20},{28,24},{32,28},{36,32}... | collective-permute-start | bytes 18440 | tf_op jit(solution)/shard_map/ppermute | solution.py:90
  12.2 29.3 %collective-permute-start.2 = (bf16[3,2,1,128]{3,2,1,0:T(2,128)(2,1)S(1)}, bf16[3,2,1,128]{3,2,1,0:T(2,128)(2,1)S(1)}, u32[]{:S(2)}, u32[]{:S(2)}) collective-permute-start(bf16[3,2,1,128]{3,2,1,0:T(2,128)(2,1)S(1)} %broadcast_select_fusion.18), channel_id=1, source_target_pairs={{0,2},{2,0},{1,3},{3,1},{4,6},{6,4},{5,7},{7,5},{8,10},{10,8},{9,1... | collective-permute-start | bytes 4616 | tf_op jit(solution)/shard_map/ppermute | solution.py:86
  15.0 24.3 %collective-permute-start.3 = (bf16[3,2,8,1]{3,2,1,0:T(8,128)(2,1)S(1)}, bf16[3,2,8,1]{3,2,1,0:T(8,128)(2,1)S(1)}, u32[]{:S(2)}, u32[]{:S(2)}) collective-permute-start(bf16[3,2,8,1]{3,2,1,0:T(8,128)(2,1)S(1)} %slice_select_fusion), channel_id=1, source_target_pairs={{0,1},{1,0},{2,3},{3,2},{4,5},{5,4},{6,7},{7,6},{8,9},{9,8},{10,11... | collective-permute-start | bytes 296 | tf_op jit(solution)/shard_map/ppermute | solution.py:86
  25.0 44.4 %collective-permute-start.6 = (f32[4,4,512]{2,1,0:T(4,128)}, f32[4,4,512]{2,1,0:T(4,128)S(1)}, u32[]{:S(2)}, u32[]{:S(2)}) collective-permute-start(f32[4,4,512]{2,1,0:T(4,128)} %bitcast.131), channel_id=1, source_target_pairs={{0,2},{2,0},{1,3},{3,1},{4,6},{6,4},{5,7},{7,5},{8,10},{10,8},{9,1... | collective-permute-start | bytes 98312 | tf_op jit(solution)/shard_map/ppermute | solution.py:86
  34.9 1.5 %copy-start.8 = (f32[8,512]{1,0:T(8,128)S(1)}, f32[8,512]{1,0:T(8,128)}, u32[]{:S(2)}) copy-start(f32[8,512]{1,0:T(8,128)} %constant.254.clone) | copy-start | bytes 49156
  34.9 1.5 %copy-start.9 = (f32[8,512]{1,0:T(8,128)S(1)}, f32[8,512]{1,0:T(8,128)}, u32[]{:S(2)}) copy-start(f32[8,512]{1,0:T(8,128)} %constant.255.clone) | copy-start | bytes 49156
  35.0 1.5 %copy-start.10 = (f32[8,512]{1,0:T(8,128)S(1)}, f32[8,512]{1,0:T(8,128)}, u32[]{:S(2)}) copy-start(f32[8,512]{1,0:T(8,128)} %constant.256.clone) | copy-start | bytes 49156
  35.4 2.0 %copy-start.1 = (f32[4,1,1,4,512]{4,3,2,1,0:T(4,128)S(1)}, f32[4,1,1,4,512]{4,3,2,1,0:T(4,128)}, u32[]{:S(2)}) copy-start(f32[4,1,1,4,512]{4,3,2,1,0:T(4,128)} %param.15) | copy-start | bytes 98308
  36.5 1.8 %copy-start.11 = (s32[1,1,2048]{2,1,0:T(1,128)S(1)}, s32[1,1,2048]{2,1,0:T(1,128)}, u32[]{:S(2)}) copy-start(s32[1,1,2048]{2,1,0:T(1,128)} %param.14) | copy-start | bytes 24580
  36.5 1.8 %copy-start.12 = (s32[1,1,2048]{2,1,0:T(1,128)S(1)}, s32[1,1,2048]{2,1,0:T(1,128)}, u32[]{:S(2)}) copy-start(s32[1,1,2048]{2,1,0:T(1,128)} %param.13) | copy-start | bytes 24580
  37.4 1.0 copy-start.4
  37.4 1.9 %copy-start.2 = (f32[512,512]{1,0:T(8,128)}, f32[512,512]{1,0:T(8,128)S(1)}, u32[]{:S(2)}) copy-start(f32[512,512]{1,0:T(8,128)S(1)} %get-tuple-element.193) | copy-start | bytes 3145732
  38.3 13.6 %copy-start = (bf16[3,2,8,128]{3,2,1,0:T(8,128)(2,1)S(1)}, bf16[3,2,8,128]{3,2,1,0:T(8,128)(2,1)}, u32[]{:S(2)}) copy-start(bf16[3,2,8,128]{3,2,1,0:T(8,128)(2,1)} %param.10) | copy-start | bytes 36868
  38.3 13.6 %copy-start.13 = (f32[2,8,128]{2,1,0:T(8,128)S(1)}, f32[2,8,128]{2,1,0:T(8,128)}, u32[]{:S(2)}) copy-start(f32[2,8,128]{2,1,0:T(8,128)} %param.11) | copy-start | bytes 24580
  39.3 29.9 %collective-permute-start.7 = (f32[4,1,512]{2,1,0:T(1,128)S(1)}, f32[4,1,512]{2,1,0:T(1,128)S(1)}, u32[]{:S(2)}, u32[]{:S(2)}) collective-permute-start(f32[4,1,512]{2,1,0:T(1,128)S(1)} %broadcast_select_fusion.12), channel_id=1, source_target_pairs={{0,1},{1,0},{2,3},{3,2},{4,5},{5,4},{6,7},{7,6},{8,9},{9,8},{10,11... | collective-permute-start | bytes 24584 | tf_op jit(solution)/shard_map/ppermute | solution.py:86
  41.6 28.0 %collective-permute-start.4 = (f32[4,4,64]{2,1,0:T(4,128)S(1)}, f32[4,4,64]{2,1,0:T(4,128)S(1)}, u32[]{:S(2)}, u32[]{:S(2)}) collective-permute-start(f32[4,4,64]{2,1,0:T(4,128)S(1)} %get-tuple-element.163), channel_id=1, source_target_pairs={{0,4},{4,8},{8,12},{12,16},{16,20},{20,24},{24,28},{28,32},{32,36}... | collective-permute-start | bytes 12296 | tf_op jit(solution)/shard_map/ppermute | solution.py:89
  43.6 26.0 %collective-permute-start.5 = (f32[4,4,64]{2,1,0:T(4,128)S(1)}, f32[4,4,64]{2,1,0:T(4,128)S(1)}, u32[]{:S(2)}, u32[]{:S(2)}) collective-permute-start(f32[4,4,64]{2,1,0:T(4,128)S(1)} %get-tuple-element.162), channel_id=1, source_target_pairs={{4,0},{8,4},{12,8},{16,12},{20,16},{24,20},{28,24},{32,28},{36,32}... | collective-permute-start | bytes 12296 | tf_op jit(solution)/shard_map/ppermute | solution.py:90
  53.4 28.3 %copy-start.16 = (f32[8,16]{1,0:T(8,128)S(1)}, f32[8,16]{1,0:T(8,128)}, u32[]{:S(2)}) copy-start(f32[8,16]{1,0:T(8,128)} %constant.253.clone) | copy-start | bytes 1540
  61.0 19.4 %all-to-all-start = ((f32[128,1,96]{2,1,0:T(1,128)}), f32[128,1,96]{2,1,0:T(1,128)S(1)}, u32[]{:S(2)}, u32[]{:S(2)}) async-start(f32[128,1,96]{2,1,0:T(1,128)} %copy.38), calls=%async_computation | async-start | bytes 131072 | tf_op jit(solution)/shard_map/all_to_all | solution.py:204
  82.6 2.4 %copy-start.3 = (f32[512,512]{1,0:T(8,128)S(1)}, f32[512,512]{1,0:T(8,128)}, u32[]{:S(2)}) copy-start(f32[512,512]{1,0:T(8,128)} %copy-done.2) | copy-start | bytes 3145732
  82.6 2.4 %copy-start.5 = (f32[512,512]{1,0:T(8,128)S(1)}, f32[512,512]{1,0:T(8,128)}, u32[]{:S(2)}) copy-start(f32[512,512]{1,0:T(8,128)} %copy-done.4) | copy-start | bytes 3145732
  84.2 18.6 %copy-start.6 = (f32[3,4,512]{2,1,0:T(4,128)}, f32[3,4,512]{2,1,0:T(4,128)S(1)}, u32[]{:S(2)}) copy-start(f32[3,4,512]{2,1,0:T(4,128)S(1)} %reshape.401) | copy-start | bytes 73732
  85.9 24.1 %copy-start.14 = (pred[512]{0:T(512)(128)(4,1)S(1)}, pred[512]{0:T(512)(128)(4,1)}, u32[]{:S(2)}) copy-start(pred[512]{0:T(512)(128)(4,1)} %get-tuple-element.215) | copy-start | bytes 1540
  85.9 24.1 %copy-start.15 = (pred[512]{0:T(512)(128)(4,1)S(1)}, pred[512]{0:T(512)(128)(4,1)}, u32[]{:S(2)}) copy-start(pred[512]{0:T(512)(128)(4,1)} %get-tuple-element.216) | copy-start | bytes 1540
  86.0 16.9 %collective-permute-start.10 = (f32[4,4,512]{2,1,0:T(4,128)S(1)}, f32[4,4,512]{2,1,0:T(4,128)S(1)}, u32[]{:S(2)}, u32[]{:S(2)}) collective-permute-start(f32[4,4,512]{2,1,0:T(4,128)S(1)} %fusion.22), channel_id=1, source_target_pairs={{0,2},{2,0},{1,3},{3,1},{4,6},{6,4},{5,7},{7,5},{8,10},{10,8},{9,1... | collective-permute-start | bytes 98312 | tf_op jit(solution)/shard_map/ppermute | solution.py:86
  88.0 14.8 %collective-permute-start.11 = (f32[4,1,512]{2,1,0:T(1,128)S(1)}, f32[4,1,512]{2,1,0:T(1,128)S(1)}, u32[]{:S(2)}, u32[]{:S(2)}) collective-permute-start(f32[4,1,512]{2,1,0:T(1,128)S(1)} %broadcast_select_fusion.10), channel_id=1, source_target_pairs={{0,1},{1,0},{2,3},{3,2},{4,5},{5,4},{6,7},{7,6},{8,9},{9,8},{10,11... | collective-permute-start | bytes 24584 | tf_op jit(solution)/shard_map/ppermute | solution.py:86
  95.5 7.6 %collective-permute-start.9 = (f32[4,4,64]{2,1,0:T(4,128)S(1)}, f32[4,4,64]{2,1,0:T(4,128)S(1)}, u32[]{:S(2)}, u32[]{:S(2)}) collective-permute-start(f32[4,4,64]{2,1,0:T(4,128)S(1)} %get-tuple-element.139), channel_id=1, source_target_pairs={{4,0},{8,4},{12,8},{16,12},{20,16},{24,20},{28,24},{32,28},{36,32}... | collective-permute-start | bytes 12296 | tf_op jit(solution)/shard_map/ppermute | solution.py:90
  99.9 9.8 %collective-permute-start.8 = (f32[4,4,64]{2,1,0:T(4,128)S(1)}, f32[4,4,64]{2,1,0:T(4,128)S(1)}, u32[]{:S(2)}, u32[]{:S(2)}) collective-permute-start(f32[4,4,64]{2,1,0:T(4,128)S(1)} %get-tuple-element.140), channel_id=1, source_target_pairs={{0,4},{4,8},{8,12},{12,16},{16,20},{20,24},{24,28},{28,32},{32,36}... | collective-permute-start | bytes 12296 | tf_op jit(solution)/shard_map/ppermute | solution.py:89
  111.0 11.7 %collective-permute-start.14 = (f32[4,4,512]{2,1,0:T(4,128)S(1)}, f32[4,4,512]{2,1,0:T(4,128)S(1)}, u32[]{:S(2)}, u32[]{:S(2)}) collective-permute-start(f32[4,4,512]{2,1,0:T(4,128)S(1)} %fusion.26), channel_id=1, source_target_pairs={{0,2},{2,0},{1,3},{3,1},{4,6},{6,4},{5,7},{7,5},{8,10},{10,8},{9,1... | collective-permute-start | bytes 98312 | tf_op jit(solution)/shard_map/ppermute | solution.py:86
  113.1 9.5 %collective-permute-start.15 = (f32[4,1,512]{2,1,0:T(1,128)S(1)}, f32[4,1,512]{2,1,0:T(1,128)S(1)}, u32[]{:S(2)}, u32[]{:S(2)}) collective-permute-start(f32[4,1,512]{2,1,0:T(1,128)S(1)} %broadcast_select_fusion.8), channel_id=1, source_target_pairs={{0,1},{1,0},{2,3},{3,2},{4,5},{5,4},{6,7},{7,6},{8,9},{9,8},{10,11... | collective-permute-start | bytes 24584 | tf_op jit(solution)/shard_map/ppermute | solution.py:86
  115.3 7.7 %collective-permute-start.13 = (f32[4,4,64]{2,1,0:T(4,128)S(1)}, f32[4,4,64]{2,1,0:T(4,128)S(1)}, u32[]{:S(2)}, u32[]{:S(2)}) collective-permute-start(f32[4,4,64]{2,1,0:T(4,128)S(1)} %get-tuple-element.116), channel_id=1, source_target_pairs={{4,0},{8,4},{12,8},{16,12},{20,16},{24,20},{28,24},{32,28},{36,32}... | collective-permute-start | bytes 12296 | tf_op jit(solution)/shard_map/ppermute | solution.py:90
  117.2 9.8 %collective-permute-start.12 = (f32[4,4,64]{2,1,0:T(4,128)S(1)}, f32[4,4,64]{2,1,0:T(4,128)S(1)}, u32[]{:S(2)}, u32[]{:S(2)}) collective-permute-start(f32[4,4,64]{2,1,0:T(4,128)S(1)} %get-tuple-element.117), channel_id=1, source_target_pairs={{0,4},{4,8},{8,12},{12,16},{16,20},{20,24},{24,28},{28,32},{32,36}... | collective-permute-start | bytes 12296 | tf_op jit(solution)/shard_map/ppermute | solution.py:89

commit v7 on v5

--- a/solution.py
+++ b/solution.py
@@ -191,30 +191,31 @@
     positions = cell_position.reshape(cell_count)
     owner_count = lax.axis_size("gx")
     capacity = 3 * cell_count // (2 * owner_count)
-    subcells = SUB * SUB * SUB
     owner_hot = (owners[:, None] == jnp.arange(owner_count, dtype=jnp.int32)[None, :]).astype(
         jnp.int32
     )
     earlier = jnp.cumsum(owner_hot, axis=0) - owner_hot
     order_within = jnp.sum(earlier * owner_hot, axis=1)
     slot_index = owners * capacity + order_within
-    ident = (elements * subcells + positions).astype(jnp.float32)
-    payload = jnp.concatenate([flat_source, ident[None]], axis=0)
+    ident_high = (elements * SUB + positions // (SUB * SUB)).astype(jnp.float32)
+    ident_low = (positions % (SUB * SUB)).astype(jnp.float32)
+    payload = jnp.concatenate([flat_source, ident_high[None], ident_low[None]], axis=0)
+    payload = payload.astype(jnp.bfloat16)
     send = (
-        jnp.zeros((4, owner_count * capacity), jnp.float32)
+        jnp.zeros((5, owner_count * capacity), jnp.bfloat16)
         .at[:, slot_index]
         .set(payload)
-        .reshape(4, owner_count, capacity)
-    )
-    send = jnp.transpose(send, (1, 0, 2)).reshape(owner_count, 4 * capacity)
+        .reshape(5, owner_count, capacity)
+    )
+    send = jnp.transpose(send, (1, 0, 2)).reshape(owner_count, 5 * capacity)
     got = lax.all_to_all(send, "gx", split_axis=0, concat_axis=0, tiled=True)
-    got = jnp.transpose(got.reshape(owner_count, 4, capacity), (1, 0, 2)).reshape(
-        4, owner_count * capacity
-    )
-    got_source = got[:3].astype(jnp.bfloat16)
-    got_ident = got[3].astype(jnp.int32)
-    got_element = got_ident // subcells
-    got_position = got_ident % subcells
+    got = jnp.transpose(got.reshape(owner_count, 5, capacity), (1, 0, 2)).reshape(
+        5, owner_count * capacity
+    )
+    got_source = got[:3]
+    got_high = got[3].astype(jnp.int32)
+    got_element = got_high // SUB
+    got_position = got_high % SUB * (SUB * SUB) + got[4].astype(jnp.int32)
 
     values = jnp.asarray(basis_table().T)
     along_a = pick_columns(got_position // (SUB * SUB), values)

time: 125 us -> 129 us (1.032)
  other arithmetic: 9.73 us -> 14.2 us
  waiting for transfers between devices: 19.5 us -> 18.1 us
    all_to_all x1, waiting for transfers between devices: 8.28 us -> 6.86 us  [on_device_body(): got = lax.all_to_all(send, 'gx', split_axis=0, concat_axis=0, tiled=True)]
  transfers between devices with their start and end apart: 17 -> 17, of which waited for: 4 -> 4; matrix products, arithmetic and copies ran while one was open for 21% -> 24% of each run, Pallas kernels for 0% -> 0%
where the time goes in v7:
time: 129 us; the launch traced here: 127 us
  starting transfers between devices  70.1 us (54%)
  waiting for transfers between devices  18.1 us (14%)
  local copies, waits for them, and re-layouts  16.5 us (13%)
  other arithmetic  14.2 us (11%)
  matrix products  6.78 us (5%)
  between operations  1.7 us (1%)
    ppermute x8, starting transfers between devices, neighbours(): got = lax.ppermute(sent, axis, [(0, 1), (1, 0)])  30.4 us
    ppermute x4, starting transfers between devices, neighbours(): lax.ppermute(upper, axis, [(i, i + 1) for i in range(count - 1)])  16.5 us
    ppermute x4, starting transfers between devices, neighbours(): lax.ppermute(lower, axis, [(i + 1, i) for i in range(count - 1)])  12.8 us
    ppermute x4, waiting for transfers between devices, neighbours(): lax.ppermute(lower, axis, [(i + 1, i) for i in range(count - 1)])  10.4 us
    all_to_all x1, starting transfers between devices, on_device_body(): got = lax.all_to_all(send, 'gx', split_axis=0, concat_axis=0, tiled=True)  10.4 us
    all_to_all x1, waiting for transfers between devices, on_device_body(): got = lax.all_to_all(send, 'gx', split_axis=0, concat_axis=0, tiled=True)  6.86 us
    scatter x1, local copies, waits for them, and re-layouts, on_device_body(): send = jnp.zeros((5, owner_count * capacity), jnp.bfloat16).at[:, slot_in...  6.1 us
    dot_general x3, matrix products, tendency(): divergence = jnp.dot(velocity_rows, div_table, precision=precision)  3.27 us
  transfers between devices with their start and end apart: 17, of which 4 were waited for; matrix products, arithmetic and copies ran while one was open for 24% of the time, Pallas kernels for 0%

profile of v7, /device:TPU:62, one launch (start us, length us, event | category | flops | bytes accessed | tf_op | source)
XLA Modules:
  0.0 127.4 jit_solution(2945378195369518120)
XLA Ops:
  0.6 0.9 slice_select_fusion
  1.5 10.9 %collective-permute-start.3 = (bf16[3,2,8,1]{3,2,1,0:T(8,128)(2,1)S(1)}, bf16[3,2,8,1]{3,2,1,0:T(8,128)(2,1)S(1)}, u32[]{:S(2)}, u32[]{:S(2)}) collective-permute-start(bf16[3,2,8,1]{3,2,1,0:T(8,128)(2,1)S(1)} %slice_select_fusion), channel_id=1, source_target_pairs={{0,1},{1,0},{2,3},{3,2},{4,5},{5,4},{6,7},{7,6},{8,9},{9,8},{10,11... | collective-permute-start | bytes 296 | tf_op jit(solution)/shard_map/ppermute | solution.py:86
  12.4 0.8 broadcast_select_fusion.18
  13.2 1.9 %collective-permute-start.2 = (bf16[3,2,1,128]{3,2,1,0:T(2,128)(2,1)S(1)}, bf16[3,2,1,128]{3,2,1,0:T(2,128)(2,1)S(1)}, u32[]{:S(2)}, u32[]{:S(2)}) collective-permute-start(bf16[3,2,1,128]{3,2,1,0:T(2,128)(2,1)S(1)} %broadcast_select_fusion.18), channel_id=1, source_target_pairs={{0,2},{2,0},{1,3},{3,1},{4,6},{6,4},{5,7},{7,5},{8,10},{10,8},{9,1... | collective-permute-start | bytes 4616 | tf_op jit(solution)/shard_map/ppermute | solution.py:86
  15.2 0.7 fusion.185
  15.9 3.2 %collective-permute-start = (bf16[3,1,8,128]{3,2,1,0:T(8,128)(2,1)S(1)}, bf16[3,1,8,128]{3,2,1,0:T(8,128)(2,1)S(1)}, u32[]{:S(2)}, u32[]{:S(2)}) collective-permute-start(bf16[3,1,8,128]{3,2,1,0:T(8,128)(2,1)S(1)} %get-tuple-element.187), channel_id=1, source_target_pairs={{4,0},{8,4},{12,8},{16,12},{20,16},{24,20},{28,24},{32,28},{36,32}... | collective-permute-start | bytes 18440 | tf_op jit(solution)/shard_map/ppermute | solution.py:90
  19.1 6.8 %collective-permute-start.1 = (bf16[3,1,8,128]{3,2,1,0:T(8,128)(2,1)S(1)}, bf16[3,1,8,128]{3,2,1,0:T(8,128)(2,1)S(1)}, u32[]{:S(2)}, u32[]{:S(2)}) collective-permute-start(bf16[3,1,8,128]{3,2,1,0:T(8,128)(2,1)S(1)} %get-tuple-element.188), channel_id=1, source_target_pairs={{0,4},{4,8},{8,12},{12,16},{16,20},{20,24},{24,28},{28,32},{32,36}... | collective-permute-start | bytes 18440 | tf_op jit(solution)/shard_map/ppermute | solution.py:89
  25.9 1.9 %collective-permute-start.6 = (f32[4,4,512]{2,1,0:T(4,128)}, f32[4,4,512]{2,1,0:T(4,128)S(1)}, u32[]{:S(2)}, u32[]{:S(2)}) collective-permute-start(f32[4,4,512]{2,1,0:T(4,128)} %bitcast.146), channel_id=1, source_target_pairs={{0,2},{2,0},{1,3},{3,1},{4,6},{6,4},{5,7},{7,5},{8,10},{10,8},{9,1... | collective-permute-start | bytes 98312 | tf_op jit(solution)/shard_map/ppermute | solution.py:86
  27.9 0.8 fusion.182
  28.7 0.9 fusion.183
  29.5 0.7 fusion.184
  30.2 1.4 %broadcast_select_fusion.12 = f32[4,1,512]{2,1,0:T(1,128)} fusion(pred[]{:T(512)S(6)} %eq.225, f32[4,4,512]{2,1,0:T(4,128)} %bitcast.147), kind=kLoop, calls=%fused_computation.229 | loop fusion | flops 2048 | bytes 24577 | tf_op jit(solution)/shard_map/jit(_where)/select_n | solution.py:85
  31.7 0.8 fusion.180
  32.5 1.4 %fusion.181 = (f32[4,4,64]{2,1,0:T(4,128)}, f32[4,4,64]{2,1,0:T(4,128)}) fusion(f32[4,4,512]{2,1,0:T(4,128)} %bitcast.149), kind=kLoop, calls=%fused_computation.410 | loop fusion | bytes 16384 | tf_op jit(solution)/shard_map/slice | solution.py:142
  33.9 0.7 slice_bitcast_fusion.13
  34.7 0.6 fusion.158
  35.2 0.5 fusion.160
  35.8 0.6 broadcast_compare_fusion
  36.4 0.8 copy.35
  37.2 0.3 fusion.16
  37.7 0.3 copy.36
  38.0 0.6 fusion.15
  38.7 0.6 compare_select_fusion
  39.3 0.8 bitcast_select_fusion.2
  40.2 0.8 convolution_bitcast_fusion
  41.0 0.6 fusion.137
  41.7 1.5 %fusion.6 = f32[1,4,512]{2,1,0:T(4,128)} fusion(f32[512,512]{1,0:T(8,128)S(1)} %get-tuple-element.198, f32[512,512]{1,0:T(8,128)S(1)} %get-tuple-element.199, f32[512,512]{1,0:T(8,128)S(1)} %get-tuple-element.197, f32[4,512]{1,0:T(4,128)S(1)} %get-tuple-element.164, f32[4,512]{1,0:T(4,128)S(1)} %get-tuple-element.163, f32[4,512]{1,0:T(4,128)S(1)} %get-tuple-element.162), kind=kOutput, calls=%fused_computation.25 | convolution fusion | flops 20461568 | bytes 3178496 | tf_op jit(solution)/shard_map/dot_general | solution.py:138
  43.3 1.9 %collective-permute-start.7 = (f32[4,1,512]{2,1,0:T(1,128)}, f32[4,1,512]{2,1,0:T(1,128)}, u32[]{:S(2)}, u32[]{:S(2)}) collective-permute-start(f32[4,1,512]{2,1,0:T(1,128)} %broadcast_select_fusion.12), channel_id=1, source_target_pairs={{0,1},{1,0},{2,3},{3,2},{4,5},{5,4},{6,7},{7,6},{8,9},{9,8},{10,11... | collective-permute-start | bytes 24584 | tf_op jit(solution)/shard_map/ppermute | solution.py:86
  45.2 2.1 %collective-permute-start.4 = (f32[4,4,64]{2,1,0:T(4,128)}, f32[4,4,64]{2,1,0:T(4,128)}, u32[]{:S(2)}, u32[]{:S(2)}) collective-permute-start(f32[4,4,64]{2,1,0:T(4,128)} %get-tuple-element.161), channel_id=1, source_target_pairs={{0,4},{4,8},{8,12},{12,16},{16,20},{20,24},{24,28},{28,32},{32,36}... | collective-permute-start | bytes 12296 | tf_op jit(solution)/shard_map/ppermute | solution.py:89
  47.5 3.7 %collective-permute-start.5 = (f32[4,4,64]{2,1,0:T(4,128)}, f32[4,4,64]{2,1,0:T(4,128)}, u32[]{:S(2)}, u32[]{:S(2)}) collective-permute-start(f32[4,4,64]{2,1,0:T(4,128)} %get-tuple-element.160), channel_id=1, source_target_pairs={{4,0},{8,4},{12,8},{16,12},{20,16},{24,20},{28,24},{32,28},{36,32}... | collective-permute-start | bytes 12296 | tf_op jit(solution)/shard_map/ppermute | solution.py:90
  51.5 0.3 copy.37
  51.8 6.1 %scatter_custom_fusion = bf16[5,3072]{0,1:T(8,128)(2,1)S(1)} fusion(s32[2048]{0:T(1024)} %bitcast.161, bf16[2048,5]{1,0:T(8,128)(2,1)S(1)} %copy.37, bf16[]{:T(256)} %constant.238.clone.1), kind=kCustom, calls=%fused_computation.48 | custom fusion | bytes 31232 | tf_op jit(solution)/shard_map/scatter | solution.py:207
  57.9 0.5 copy.38
  58.4 0.8 copy.39
  59.2 10.4 %all-to-all-start = ((bf16[128,1,120]{2,1,0:T(2,128)(2,1)}), bf16[128,1,120]{2,1,0:T(2,128)(2,1)S(1)}, u32[]{:S(2)}, u32[]{:S(2)}) async-start(bf16[128,1,120]{2,1,0:T(2,128)(2,1)} %copy.39), calls=%async_computation | async-start | bytes 131072 | tf_op jit(solution)/shard_map/all_to_all | solution.py:211
  69.6 0.7 broadcast_select_fusion.11
  70.6 0.9 broadcast_multiply_fusion.13
  71.6 6.9 %all-to-all-done = bf16[128,1,120]{2,1,0:T(2,128)(2,1)S(1)} async-done(((bf16[128,1,120]{2,1,0:T(2,128)(2,1)}), bf16[128,1,120]{2,1,0:T(2,128)(2,1)S(1)}, u32[]{:S(2)}, u32[]{:S(2)}) %all-to-all-start) | async-done | bytes 30752 | tf_op jit(solution)/shard_map/all_to_all | solution.py:211
  78.5 0.1 copy.40
  79.2 0.1 copy.42
  79.3 0.2 broadcast_in_dim.187
  79.6 0.9 select_reduce_fusion.2
  80.6 0.6 multiply_convert_fusion
  81.2 0.9 convolution_multiply_fusion
  82.2 0.8 fusion.22
  83.1 1.9 %collective-permute-start.10 = (f32[4,4,512]{2,1,0:T(4,128)S(1)}, f32[4,4,512]{2,1,0:T(4,128)S(1)}, u32[]{:S(2)}, u32[]{:S(2)}) collective-permute-start(f32[4,4,512]{2,1,0:T(4,128)S(1)} %fusion.22), channel_id=1, source_target_pairs={{0,2},{2,0},{1,3},{3,1},{4,6},{6,4},{5,7},{7,5},{8,10},{10,8},{9,1... | collective-permute-start | bytes 98312 | tf_op jit(solution)/shard_map/ppermute | solution.py:86
  85.1 0.9 fusion.1
  85.9 8.0 %collective-permute-start.11 = (f32[4,1,512]{2,1,0:T(1,128)S(1)}, f32[4,1,512]{2,1,0:T(1,128)S(1)}, u32[]{:S(2)}, u32[]{:S(2)}) collective-permute-start(f32[4,1,512]{2,1,0:T(1,128)S(1)} %broadcast_select_fusion.10), channel_id=1, source_target_pairs={{0,1},{1,0},{2,3},{3,2},{4,5},{5,4},{6,7},{7,6},{8,9},{9,8},{10,11... | collective-permute-start | bytes 24584 | tf_op jit(solution)/shard_map/ppermute | solution.py:86
  93.9 5.7 %collective-permute-start.8 = (f32[4,4,64]{2,1,0:T(4,128)S(1)}, f32[4,4,64]{2,1,0:T(4,128)S(1)}, u32[]{:S(2)}, u32[]{:S(2)}) collective-permute-start(f32[4,4,64]{2,1,0:T(4,128)S(1)} %get-tuple-element.138), channel_id=1, source_target_pairs={{0,4},{4,8},{8,12},{12,16},{16,20},{20,24},{24,28},{28,32},{32,36}... | collective-permute-start | bytes 12296 | tf_op jit(solution)/shard_map/ppermute | solution.py:89
  99.6 1.9 %collective-permute-start.9 = (f32[4,4,64]{2,1,0:T(4,128)S(1)}, f32[4,4,64]{2,1,0:T(4,128)S(1)}, u32[]{:S(2)}, u32[]{:S(2)}) collective-permute-start(f32[4,4,64]{2,1,0:T(4,128)S(1)} %get-tuple-element.137), channel_id=1, source_target_pairs={{4,0},{8,4},{12,8},{16,12},{20,16},{24,20},{28,24},{32,28},{36,32}... | collective-permute-start | bytes 12296 | tf_op jit(solution)/shard_map/ppermute | solution.py:90
  101.5 0.9 fusion.8
  102.7 6.6 %collective-permute-done.9 = f32[4,4,64]{2,1,0:T(4,128)S(1)} collective-permute-done((f32[4,4,64]{2,1,0:T(4,128)S(1)}, f32[4,4,64]{2,1,0:T(4,128)S(1)}, u32[]{:S(2)}, u32[]{:S(2)}) %collective-permute-start.9) | collective-permute-done | bytes 4128 | tf_op jit(solution)/shard_map/ppermute | solution.py:90
  109.3 0.2 broadcast_multiply_fusion.7
  109.7 0.1 fusion.26
  109.8 1.9 %collective-permute-start.14 = (f32[4,4,512]{2,1,0:T(4,128)S(1)}, f32[4,4,512]{2,1,0:T(4,128)S(1)}, u32[]{:S(2)}, u32[]{:S(2)}) collective-permute-start(f32[4,4,512]{2,1,0:T(4,128)S(1)} %fusion.26), channel_id=1, source_target_pairs={{0,2},{2,0},{1,3},{3,1},{4,6},{6,4},{5,7},{7,5},{8,10},{10,8},{9,1... | collective-permute-start | bytes 98312 | tf_op jit(solution)/shard_map/ppermute | solution.py:86
  111.8 0.9 fusion
  112.7 1.9 %collective-permute-start.15 = (f32[4,1,512]{2,1,0:T(1,128)S(1)}, f32[4,1,512]{2,1,0:T(1,128)S(1)}, u32[]{:S(2)}, u32[]{:S(2)}) collective-permute-start(f32[4,1,512]{2,1,0:T(1,128)S(1)} %broadcast_select_fusion.8), channel_id=1, source_target_pairs={{0,1},{1,0},{2,3},{3,2},{4,5},{5,4},{6,7},{7,6},{8,9},{9,8},{10,11... | collective-permute-start | bytes 24584 | tf_op jit(solution)/shard_map/ppermute | solution.py:86
  114.6 1.9 %collective-permute-start.12 = (f32[4,4,64]{2,1,0:T(4,128)S(1)}, f32[4,4,64]{2,1,0:T(4,128)S(1)}, u32[]{:S(2)}, u32[]{:S(2)}) collective-permute-start(f32[4,4,64]{2,1,0:T(4,128)S(1)} %get-tuple-element.115), channel_id=1, source_target_pairs={{0,4},{4,8},{8,12},{12,16},{16,20},{20,24},{24,28},{28,32},{32,36}... | collective-permute-start | bytes 12296 | tf_op jit(solution)/shard_map/ppermute | solution.py:89
  116.5 3.9 %collective-permute-start.13 = (f32[4,4,64]{2,1,0:T(4,128)S(1)}, f32[4,4,64]{2,1,0:T(4,128)S(1)}, u32[]{:S(2)}, u32[]{:S(2)}) collective-permute-start(f32[4,4,64]{2,1,0:T(4,128)S(1)} %get-tuple-element.114), channel_id=1, source_target_pairs={{4,0},{8,4},{12,8},{16,12},{20,16},{24,20},{28,24},{32,28},{36,32}... | collective-permute-start | bytes 12296 | tf_op jit(solution)/shard_map/ppermute | solution.py:90
  120.5 0.9 fusion.10
  121.4 0.8 collective-permute-done.15
  122.5 3.8 %collective-permute-done.13 = f32[4,4,64]{2,1,0:T(4,128)S(1)} collective-permute-done((f32[4,4,64]{2,1,0:T(4,128)S(1)}, f32[4,4,64]{2,1,0:T(4,128)S(1)}, u32[]{:S(2)}, u32[]{:S(2)}) %collective-permute-start.13) | collective-permute-done | bytes 4128 | tf_op jit(solution)/shard_map/ppermute | solution.py:90
  126.3 0.2 broadcast_multiply_fusion.1
  126.6 0.7 fusion.31
  (147 shorter events, 2.6 us)
Async XLA Ops:
  0.6 37.4 %copy-start.5 = (s32[1,1,2048,1]{2,3,1,0:T(1,128)S(1)}, s32[1,1,2048,1]{2,3,1,0:T(1,128)}, u32[]{:S(2)}) copy-start(s32[1,1,2048,1]{2,3,1,0:T(1,128)} %param.12) | copy-start | bytes 24580
  1.5 41.8 %collective-permute-start.3 = (bf16[3,2,8,1]{3,2,1,0:T(8,128)(2,1)S(1)}, bf16[3,2,8,1]{3,2,1,0:T(8,128)(2,1)S(1)}, u32[]{:S(2)}, u32[]{:S(2)}) collective-permute-start(bf16[3,2,8,1]{3,2,1,0:T(8,128)(2,1)S(1)} %slice_select_fusion), channel_id=1, source_target_pairs={{0,1},{1,0},{2,3},{3,2},{4,5},{5,4},{6,7},{7,6},{8,9},{9,8},{10,11... | collective-permute-start | bytes 296 | tf_op jit(solution)/shard_map/ppermute | solution.py:86
  13.2 32.0 %collective-permute-start.2 = (bf16[3,2,1,128]{3,2,1,0:T(2,128)(2,1)S(1)}, bf16[3,2,1,128]{3,2,1,0:T(2,128)(2,1)S(1)}, u32[]{:S(2)}, u32[]{:S(2)}) collective-permute-start(bf16[3,2,1,128]{3,2,1,0:T(2,128)(2,1)S(1)} %broadcast_select_fusion.18), channel_id=1, source_target_pairs={{0,2},{2,0},{1,3},{3,1},{4,6},{6,4},{5,7},{7,5},{8,10},{10,8},{9,1... | collective-permute-start | bytes 4616 | tf_op jit(solution)/shard_map/ppermute | solution.py:86
  15.9 31.6 %collective-permute-start = (bf16[3,1,8,128]{3,2,1,0:T(8,128)(2,1)S(1)}, bf16[3,1,8,128]{3,2,1,0:T(8,128)(2,1)S(1)}, u32[]{:S(2)}, u32[]{:S(2)}) collective-permute-start(bf16[3,1,8,128]{3,2,1,0:T(8,128)(2,1)S(1)} %get-tuple-element.187), channel_id=1, source_target_pairs={{4,0},{8,4},{12,8},{16,12},{20,16},{24,20},{28,24},{32,28},{36,32}... | collective-permute-start | bytes 18440 | tf_op jit(solution)/shard_map/ppermute | solution.py:90
  19.1 32.1 %collective-permute-start.1 = (bf16[3,1,8,128]{3,2,1,0:T(8,128)(2,1)S(1)}, bf16[3,1,8,128]{3,2,1,0:T(8,128)(2,1)S(1)}, u32[]{:S(2)}, u32[]{:S(2)}) collective-permute-start(bf16[3,1,8,128]{3,2,1,0:T(8,128)(2,1)S(1)} %get-tuple-element.188), channel_id=1, source_target_pairs={{0,4},{4,8},{8,12},{12,16},{16,20},{20,24},{24,28},{28,32},{32,36}... | collective-permute-start | bytes 18440 | tf_op jit(solution)/shard_map/ppermute | solution.py:89
  25.9 44.5 %collective-permute-start.6 = (f32[4,4,512]{2,1,0:T(4,128)}, f32[4,4,512]{2,1,0:T(4,128)S(1)}, u32[]{:S(2)}, u32[]{:S(2)}) collective-permute-start(f32[4,4,512]{2,1,0:T(4,128)} %bitcast.146), channel_id=1, source_target_pairs={{0,2},{2,0},{1,3},{3,1},{4,6},{6,4},{5,7},{7,5},{8,10},{10,8},{9,1... | collective-permute-start | bytes 98312 | tf_op jit(solution)/shard_map/ppermute | solution.py:86
  37.2 2.1 %copy-start.7 = (f32[8,512]{1,0:T(8,128)S(1)}, f32[8,512]{1,0:T(8,128)}, u32[]{:S(2)}) copy-start(f32[8,512]{1,0:T(8,128)} %constant.268.clone) | copy-start | bytes 49156
  37.2 2.1 %copy-start.8 = (f32[8,512]{1,0:T(8,128)S(1)}, f32[8,512]{1,0:T(8,128)}, u32[]{:S(2)}) copy-start(f32[8,512]{1,0:T(8,128)} %constant.269.clone) | copy-start | bytes 49156
  37.2 2.1 %copy-start.9 = (f32[8,512]{1,0:T(8,128)S(1)}, f32[8,512]{1,0:T(8,128)}, u32[]{:S(2)}) copy-start(f32[8,512]{1,0:T(8,128)} %constant.270.clone) | copy-start | bytes 49156
  37.7 2.5 %copy-start.1 = (f32[4,1,1,4,512]{4,3,2,1,0:T(4,128)S(1)}, f32[4,1,1,4,512]{4,3,2,1,0:T(4,128)}, u32[]{:S(2)}) copy-start(f32[4,1,1,4,512]{4,3,2,1,0:T(4,128)} %param.15) | copy-start | bytes 98308
  39.3 2.4 %copy-start.12 = (s32[1,1,2048]{2,1,0:T(1,128)S(1)}, s32[1,1,2048]{2,1,0:T(1,128)}, u32[]{:S(2)}) copy-start(s32[1,1,2048]{2,1,0:T(1,128)} %param.13) | copy-start | bytes 24580
  39.3 2.4 %copy-start.13 = (s32[1,1,2048]{2,1,0:T(1,128)S(1)}, s32[1,1,2048]{2,1,0:T(1,128)}, u32[]{:S(2)}) copy-start(s32[1,1,2048]{2,1,0:T(1,128)} %param.14) | copy-start | bytes 24580
  40.2 3.1 %copy-start.2 = (f32[512,512]{1,0:T(8,128)}, f32[512,512]{1,0:T(8,128)S(1)}, u32[]{:S(2)}) copy-start(f32[512,512]{1,0:T(8,128)S(1)} %get-tuple-element.199) | copy-start | bytes 3145732
  40.2 3.1 %copy-start = (bf16[3,2,8,128]{3,2,1,0:T(8,128)(2,1)S(1)}, bf16[3,2,8,128]{3,2,1,0:T(8,128)(2,1)}, u32[]{:S(2)}) copy-start(bf16[3,2,8,128]{3,2,1,0:T(8,128)(2,1)} %param.10) | copy-start | bytes 36868
  41.0 10.3 %copy-start.10 = (f32[2,8,128]{2,1,0:T(8,128)S(1)}, f32[2,8,128]{2,1,0:T(8,128)}, u32[]{:S(2)}) copy-start(f32[2,8,128]{2,1,0:T(8,128)} %param.11) | copy-start | bytes 24580
  43.3 26.3 %collective-permute-start.7 = (f32[4,1,512]{2,1,0:T(1,128)}, f32[4,1,512]{2,1,0:T(1,128)}, u32[]{:S(2)}, u32[]{:S(2)}) collective-permute-start(f32[4,1,512]{2,1,0:T(1,128)} %broadcast_select_fusion.12), channel_id=1, source_target_pairs={{0,1},{1,0},{2,3},{3,2},{4,5},{5,4},{6,7},{7,6},{8,9},{9,8},{10,11... | collective-permute-start | bytes 24584 | tf_op jit(solution)/shard_map/ppermute | solution.py:86
  45.2 25.4 %collective-permute-start.4 = (f32[4,4,64]{2,1,0:T(4,128)}, f32[4,4,64]{2,1,0:T(4,128)}, u32[]{:S(2)}, u32[]{:S(2)}) collective-permute-start(f32[4,4,64]{2,1,0:T(4,128)} %get-tuple-element.161), channel_id=1, source_target_pairs={{0,4},{4,8},{8,12},{12,16},{16,20},{20,24},{24,28},{28,32},{32,36}... | collective-permute-start | bytes 12296 | tf_op jit(solution)/shard_map/ppermute | solution.py:89
  47.5 23.1 %collective-permute-start.5 = (f32[4,4,64]{2,1,0:T(4,128)}, f32[4,4,64]{2,1,0:T(4,128)}, u32[]{:S(2)}, u32[]{:S(2)}) collective-permute-start(f32[4,4,64]{2,1,0:T(4,128)} %get-tuple-element.160), channel_id=1, source_target_pairs={{4,0},{8,4},{12,8},{16,12},{20,16},{24,20},{28,24},{32,28},{36,32}... | collective-permute-start | bytes 12296 | tf_op jit(solution)/shard_map/ppermute | solution.py:90
  57.9 21.7 %copy-start.20 = (f32[8,16]{1,0:T(8,128)S(1)}, f32[8,16]{1,0:T(8,128)}, u32[]{:S(2)}) copy-start(f32[8,16]{1,0:T(8,128)} %constant.267.clone) | copy-start | bytes 1540
  59.2 19.3 %all-to-all-start = ((bf16[128,1,120]{2,1,0:T(2,128)(2,1)}), bf16[128,1,120]{2,1,0:T(2,128)(2,1)S(1)}, u32[]{:S(2)}, u32[]{:S(2)}) async-start(bf16[128,1,120]{2,1,0:T(2,128)(2,1)} %copy.39), calls=%async_computation | async-start | bytes 131072 | tf_op jit(solution)/shard_map/all_to_all | solution.py:211
  80.5 1.6 %copy-start.6 = (f32[1,4,512]{2,1,0:T(4,128)S(1)}, f32[1,4,512]{2,1,0:T(4,128)}, u32[]{:S(2)}) copy-start(f32[1,4,512]{2,1,0:T(4,128)} %get-tuple-element.175) | copy-start | bytes 24580
  80.6 1.6 %copy-start.11 = (f32[1,4,512]{2,1,0:T(4,128)S(1)}, f32[1,4,512]{2,1,0:T(4,128)}, u32[]{:S(2)}) copy-start(f32[1,4,512]{2,1,0:T(4,128)} %fusion.6) | copy-start | bytes 24580
  80.6 1.6 %copy-start.14 = (pred[512]{0:T(512)(128)(4,1)S(1)}, pred[512]{0:T(512)(128)(4,1)}, u32[]{:S(2)}) copy-start(pred[512]{0:T(512)(128)(4,1)} %get-tuple-element.220) | copy-start | bytes 1540
  80.6 1.6 %copy-start.15 = (pred[512]{0:T(512)(128)(4,1)S(1)}, pred[512]{0:T(512)(128)(4,1)}, u32[]{:S(2)}) copy-start(pred[512]{0:T(512)(128)(4,1)} %get-tuple-element.221) | copy-start | bytes 1540
  80.6 1.6 %copy-start.16 = (pred[512]{0:T(512)(128)(4,1)S(1)}, pred[512]{0:T(512)(128)(4,1)}, u32[]{:S(2)}) copy-start(pred[512]{0:T(512)(128)(4,1)} %get-tuple-element.222) | copy-start | bytes 1540
  80.6 1.6 %copy-start.17 = (pred[512]{0:T(512)(128)(4,1)S(1)}, pred[512]{0:T(512)(128)(4,1)}, u32[]{:S(2)}) copy-start(pred[512]{0:T(512)(128)(4,1)} %get-tuple-element.223) | copy-start | bytes 1540
  80.6 4.5 %copy-start.3 = (f32[512,512]{1,0:T(8,128)S(1)}, f32[512,512]{1,0:T(8,128)}, u32[]{:S(2)}) copy-start(f32[512,512]{1,0:T(8,128)} %copy-done.2) | copy-start | bytes 3145732
  82.1 20.3 %copy-start.4 = (f32[3,4,512]{2,1,0:T(4,128)}, f32[3,4,512]{2,1,0:T(4,128)S(1)}, u32[]{:S(2)}) copy-start(f32[3,4,512]{2,1,0:T(4,128)S(1)} %reshape.469) | copy-start | bytes 73732
  83.1 19.5 %collective-permute-start.10 = (f32[4,4,512]{2,1,0:T(4,128)S(1)}, f32[4,4,512]{2,1,0:T(4,128)S(1)}, u32[]{:S(2)}, u32[]{:S(2)}) collective-permute-start(f32[4,4,512]{2,1,0:T(4,128)S(1)} %fusion.22), channel_id=1, source_target_pairs={{0,2},{2,0},{1,3},{3,1},{4,6},{6,4},{5,7},{7,5},{8,10},{10,8},{9,1... | collective-permute-start | bytes 98312 | tf_op jit(solution)/shard_map/ppermute | solution.py:86
  85.9 23.7 %copy-start.18 = (pred[512]{0:T(512)(128)(4,1)S(1)}, pred[512]{0:T(512)(128)(4,1)}, u32[]{:S(2)}) copy-start(pred[512]{0:T(512)(128)(4,1)} %get-tuple-element.224) | copy-start | bytes 1540
  85.9 23.7 %copy-start.19 = (pred[512]{0:T(512)(128)(4,1)S(1)}, pred[512]{0:T(512)(128)(4,1)}, u32[]{:S(2)}) copy-start(pred[512]{0:T(512)(128)(4,1)} %get-tuple-element.225) | copy-start | bytes 1540
  85.9 16.5 %collective-permute-start.11 = (f32[4,1,512]{2,1,0:T(1,128)S(1)}, f32[4,1,512]{2,1,0:T(1,128)S(1)}, u32[]{:S(2)}, u32[]{:S(2)}) collective-permute-start(f32[4,1,512]{2,1,0:T(1,128)S(1)} %broadcast_select_fusion.10), channel_id=1, source_target_pairs={{0,1},{1,0},{2,3},{3,2},{4,5},{5,4},{6,7},{7,6},{8,9},{9,8},{10,11... | collective-permute-start | bytes 24584 | tf_op jit(solution)/shard_map/ppermute | solution.py:86
  93.9 8.8 %collective-permute-start.8 = (f32[4,4,64]{2,1,0:T(4,128)S(1)}, f32[4,4,64]{2,1,0:T(4,128)S(1)}, u32[]{:S(2)}, u32[]{:S(2)}) collective-permute-start(f32[4,4,64]{2,1,0:T(4,128)S(1)} %get-tuple-element.138), channel_id=1, source_target_pairs={{0,4},{4,8},{8,12},{12,16},{16,20},{20,24},{24,28},{28,32},{32,36}... | collective-permute-start | bytes 12296 | tf_op jit(solution)/shard_map/ppermute | solution.py:89
  99.6 9.8 %collective-permute-start.9 = (f32[4,4,64]{2,1,0:T(4,128)S(1)}, f32[4,4,64]{2,1,0:T(4,128)S(1)}, u32[]{:S(2)}, u32[]{:S(2)}) collective-permute-start(f32[4,4,64]{2,1,0:T(4,128)S(1)} %get-tuple-element.137), channel_id=1, source_target_pairs={{4,0},{8,4},{12,8},{16,12},{20,16},{24,20},{28,24},{32,28},{36,32}... | collective-permute-start | bytes 12296 | tf_op jit(solution)/shard_map/ppermute | solution.py:90
  109.8 12.5 %collective-permute-start.14 = (f32[4,4,512]{2,1,0:T(4,128)S(1)}, f32[4,4,512]{2,1,0:T(4,128)S(1)}, u32[]{:S(2)}, u32[]{:S(2)}) collective-permute-start(f32[4,4,512]{2,1,0:T(4,128)S(1)} %fusion.26), channel_id=1, source_target_pairs={{0,2},{2,0},{1,3},{3,1},{4,6},{6,4},{5,7},{7,5},{8,10},{10,8},{9,1... | collective-permute-start | bytes 98312 | tf_op jit(solution)/shard_map/ppermute | solution.py:86
  112.7 9.4 %collective-permute-start.15 = (f32[4,1,512]{2,1,0:T(1,128)S(1)}, f32[4,1,512]{2,1,0:T(1,128)S(1)}, u32[]{:S(2)}, u32[]{:S(2)}) collective-permute-start(f32[4,1,512]{2,1,0:T(1,128)S(1)} %broadcast_select_fusion.8), channel_id=1, source_target_pairs={{0,1},{1,0},{2,3},{3,2},{4,5},{5,4},{6,7},{7,6},{8,9},{9,8},{10,11... | collective-permute-start | bytes 24584 | tf_op jit(solution)/shard_map/ppermute | solution.py:86
  114.6 7.8 %collective-permute-start.12 = (f32[4,4,64]{2,1,0:T(4,128)S(1)}, f32[4,4,64]{2,1,0:T(4,128)S(1)}, u32[]{:S(2)}, u32[]{:S(2)}) collective-permute-start(f32[4,4,64]{2,1,0:T(4,128)S(1)} %get-tuple-element.115), channel_id=1, source_target_pairs={{0,4},{4,8},{8,12},{12,16},{16,20},{20,24},{24,28},{28,32},{32,36}... | collective-permute-start | bytes 12296 | tf_op jit(solution)/shard_map/ppermute | solution.py:89
  116.5 9.8 %collective-permute-start.13 = (f32[4,4,64]{2,1,0:T(4,128)S(1)}, f32[4,4,64]{2,1,0:T(4,128)S(1)}, u32[]{:S(2)}, u32[]{:S(2)}) collective-permute-start(f32[4,4,64]{2,1,0:T(4,128)S(1)} %get-tuple-element.114), channel_id=1, source_target_pairs={{4,0},{8,4},{12,8},{16,12},{20,16},{24,20},{28,24},{32,28},{36,32}... | collective-permute-start | bytes 12296 | tf_op jit(solution)/shard_map/ppermute | solution.py:90
